TPU v7x, 32 devices: a whole 2x2x4 slice. The times are simulated.
32 devices in a mesh: group: 8 (over y, x, core), tensor: 4 (over z).
Axes of the slice: x: 2, y: 2, z: 4, core: 2. Of those that a mesh axis runs over, the one named last changes fastest.
Arguments:
- hidden: bfloat16 [768, 4096], P('group'), may hold values from -6 to 6
- query_weight: bfloat16 [4096, 4096], P(None, 'tensor'), may hold values from -0.09375 to 0.09375
- out_weight: bfloat16 [4096, 4096], P('tensor'), may hold values from -0.75 to 0.75
- prefix_keys: bfloat16 [9216, 16, 1024], P('group', None, 'tensor')
- prefix_values: bfloat16 [9216, 16, 1024], P('group', None, 'tensor'), may hold values from -6 to 6
- block_table: int32 [144, 64], P('group'), may hold values from 0 to 1151, as said below
- prompt_len: int32 [144], replicated, may hold values from 1 to 1024
- prompt_group: int32 [768], P('group'), may hold values from 0 to 143, as said below
- suffix_keys: bfloat16 [768, 128, 1024], P('group', None, 'tensor')
- suffix_values: bfloat16 [768, 128, 1024], P('group', None, 'tensor'), may hold values from -6 to 6
- suffix_len: int32 [768], P('group'), may hold values from 1 to 128
Outputs:
- attn_out: bfloat16 [768, 4096], P('group', 'tensor')
Inputs may be any that keep to these rules, and one draw needn't show every extreme that they name: `prompt_group`: each of the 144 prompt groups holds 4 to 8 requests, both sizes occurring; no two requests among one index of group's 96 requests share a prompt group. `block_table`: the 18 consecutive rows of one index of group list each of that index's 18 * 64 pool blocks exactly once.
All inputs are finite; a program needn't handle non-finite values.
Results may differ from a plain program's by a relative error of at most 0.0045.
The roundings to bfloat16 on the way count: a program that leaves them out, or rounds other values in their place, can miss the bound.
Values may be sent and summed in bfloat16 or wider, within the bound.
No kernel may reach another device: no remote copies, remote signals or barrier semaphores. Data moves between devices by JAX's collectives and lax.ppermute only.
A program may use at most 192 MiB of HBM per device.

v0:
```python
import math

import jax
import jax.numpy as jnp
from jax import lax
from jax.experimental import pallas as pl
from jax.experimental.pallas import tpu as pltpu
from jax.sharding import PartitionSpec as P

HD = 128


rope_base = 10000.0
masked_score = -1e30


def rotate(projected, position):
    half = projected.shape[-1] // 2
    freqs = rope_base ** (-(2.0 * jnp.arange(half, dtype=jnp.float32)) / projected.shape[-1])
    angles = position.astype(jnp.float32)[:, None, None] * freqs
    cosine = jnp.cos(angles)
    sine = jnp.sin(angles)
    former = projected[..., :half]
    latter = projected[..., half:]
    return jnp.concatenate(
        [former * cosine - latter * sine, latter * cosine + former * sine], axis=-1
    )


def softmax_parts(scores, valid_mask):
    masked = jnp.where(valid_mask, scores, masked_score)
    maximum = jnp.max(masked, axis=-1)
    weights = jnp.where(valid_mask, jnp.exp(masked - maximum[..., None]), 0.0)
    return (maximum, jnp.sum(weights, axis=-1), weights.astype(jnp.bfloat16))


def combine(far_peak, far_total, far_acc, near_peak, near_total, near_acc):
    highest = jnp.maximum(far_peak, near_peak)
    far_factor = jnp.exp(far_peak - highest)
    near_factor = jnp.exp(near_peak - highest)
    numer = far_acc * far_factor[..., None] + near_acc * near_factor[..., None]
    denom = far_total * far_factor + near_total * near_factor
    return numer / denom[..., None]


def spread_lanes(queries, kv_heads):
    lead = queries.shape[:-3]
    share = queries.shape[-2]
    eye = (jnp.arange(kv_heads)[:, None] == jnp.arange(kv_heads)[None, :]).astype(queries.dtype)
    eye = eye.reshape((1,) * len(lead) + (kv_heads, 1, kv_heads, 1))
    wide = queries[..., None, :] * eye
    return wide.reshape(lead + (kv_heads * share, kv_heads * HD))


def pick_lanes(wide, kv_heads):
    lead = wide.shape[:-2]
    share = wide.shape[-2] // kv_heads
    w = wide.reshape(lead + (kv_heads, share, kv_heads, HD))
    return jnp.stack([w[..., k, :, k, :] for k in range(kv_heads)], axis=-3)


def far_kernel(
    table_ref, len_ref, q_ref, k_hbm, v_hbm, acc_ref, stat_ref, kbuf, vbuf, sems, *, share, scale
):
    j = pl.program_id(0)
    steps = pl.num_programs(0)
    pblk = kbuf.shape[1]
    width = kbuf.shape[3]
    kv_heads = width // HD

    block = kbuf.shape[2]

    @pl.when(j == 0)
    def _():
        vbuf[...] = jnp.zeros_like(vbuf)

    def used_blocks(group):
        return (len_ref[group] + block - 1) // block

    def fetch(group, slot):
        def one(b, carry):
            idx = table_ref[group * pblk + b]
            pltpu.make_async_copy(k_hbm.at[idx], kbuf.at[slot, b], sems.at[0, slot, b]).start()
            pltpu.make_async_copy(v_hbm.at[idx], vbuf.at[slot, b], sems.at[1, slot, b]).start()
            return carry

        lax.fori_loop(0, used_blocks(group), one, 0)

    @pl.when(j == 0)
    def _():
        fetch(0, 0)

    slot = j % 2

    @pl.when(j + 1 < steps)
    def _():
        fetch(j + 1, 1 - slot)

    def settle(b, carry):
        pltpu.make_async_copy(k_hbm.at[0], kbuf.at[slot, b], sems.at[0, slot, b]).wait()
        pltpu.make_async_copy(v_hbm.at[0], vbuf.at[slot, b], sems.at[1, slot, b]).wait()
        return carry

    lax.fori_loop(0, used_blocks(j), settle, 0)
    keys = kbuf[slot].reshape(-1, width)
    values = vbuf[slot].reshape(-1, width)
    queries = q_ref[0]
    scores = (
        lax.dot_general(
            queries, keys, (((1,), (1,)), ((), ())), preferred_element_type=jnp.float32
        )
        * scale
    )
    valid = lax.broadcasted_iota(jnp.int32, scores.shape, 1) < len_ref[j]
    masked = jnp.where(valid, scores, masked_score)
    peak = jnp.max(masked, axis=1, keepdims=True)
    weights = jnp.where(valid, jnp.exp(masked - peak), 0.0)
    total = jnp.sum(weights, axis=1, keepdims=True)
    wide = jnp.dot(weights.astype(jnp.bfloat16), values, preferred_element_type=jnp.float32)
    rows = wide.shape[0]
    row_head = (lax.broadcasted_iota(jnp.int32, (rows, HD), 0) // share) % kv_heads
    acc = jnp.zeros((rows, HD), jnp.float32)
    for k in range(kv_heads):
        acc = jnp.where(row_head == k, wide[:, k * HD : (k + 1) * HD], acc)
    acc_ref[0] = acc
    lane = lax.broadcasted_iota(jnp.int32, (rows, HD), 1)
    stat_ref[0] = jnp.where(lane < HD // 2, peak, total)


def far_attention(table, lengths, queries, prefix_keys, prefix_values, share, scale):
    local_groups, pblk = table.shape
    _, rows, width = queries.shape
    block = prefix_keys.shape[1]
    tokens = pblk * block
    kernel = lambda *refs: far_kernel(*refs, share=share, scale=scale)
    grid_spec = pltpu.PrefetchScalarGridSpec(
        num_scalar_prefetch=2,
        grid=(local_groups,),
        in_specs=[
            pl.BlockSpec((1, rows, width), lambda j, *_: (j, 0, 0)),
            pl.BlockSpec(memory_space=pl.ANY),
            pl.BlockSpec(memory_space=pl.ANY),
        ],
        out_specs=[
            pl.BlockSpec((1, rows, HD), lambda j, *_: (j, 0, 0)),
            pl.BlockSpec((1, rows, HD), lambda j, *_: (j, 0, 0)),
        ],
        scratch_shapes=[
            pltpu.VMEM((2, pblk, block, width), prefix_keys.dtype),
            pltpu.VMEM((2, pblk, block, width), prefix_values.dtype),
            pltpu.SemaphoreType.DMA((2, 2, pblk)),
        ],
    )
    cost = pl.CostEstimate(
        flops=4 * local_groups * rows * tokens * width,
        transcendentals=local_groups * rows * tokens,
        bytes_accessed=2 * local_groups * tokens * width * 2 + 3 * local_groups * rows * width * 2,
    )
    return pl.pallas_call(
        kernel,
        grid_spec=grid_spec,
        out_shape=[
            jax.ShapeDtypeStruct((local_groups, rows, HD), jnp.float32),
            jax.ShapeDtypeStruct((local_groups, rows, HD), jnp.float32),
        ],
        compiler_params=pltpu.CompilerParams(dimension_semantics=("arbitrary",)),
        cost_estimate=cost,
    )(table.reshape(-1), lengths, queries, prefix_keys, prefix_values)


def body(
    hidden,
    query_weight,
    out_weight,
    prefix_keys,
    prefix_values,
    block_table,
    prompt_len,
    prompt_group,
    suffix_keys,
    suffix_values,
    suffix_len,
):
    groups = lax.axis_size("group")
    local_groups = block_table.shape[0]
    first_group = lax.axis_index("group") * local_groups
    requests = hidden.shape[0]
    width = prefix_keys.shape[2]
    kv_heads = width // HD
    q_heads = query_weight.shape[1] // HD
    share = q_heads // kv_heads
    score_scale = 1.0 / math.sqrt(HD)

    projected = jnp.dot(hidden, query_weight, preferred_element_type=jnp.float32).reshape(
        requests, q_heads, HD
    )
    position = prompt_len[prompt_group] + suffix_len - 1
    rotated = rotate(projected, position).astype(jnp.bfloat16)

    slots = jnp.arange(groups * local_groups, dtype=jnp.int32)
    picks = (slots[:, None] == prompt_group[None, :]).astype(jnp.bfloat16)
    outgoing = jnp.dot(
        picks, rotated.reshape(requests, q_heads * HD), preferred_element_type=jnp.float32
    ).astype(jnp.bfloat16)
    arrived = lax.all_to_all(
        outgoing.reshape(groups, local_groups, q_heads * HD),
        "group",
        split_axis=0,
        concat_axis=0,
        tiled=True,
    )
    far_queries = jnp.transpose(
        arrived.reshape(groups, local_groups, kv_heads, share, HD), (1, 0, 2, 3, 4)
    )
    far_queries = spread_lanes(far_queries, kv_heads).reshape(
        local_groups, groups * q_heads, width
    )
    my_lengths = lax.dynamic_slice_in_dim(prompt_len, first_group, local_groups)
    held_acc, held_stat = far_attention(
        block_table, my_lengths, far_queries, prefix_keys, prefix_values, share, score_scale
    )
    held_acc = jnp.transpose(held_acc.reshape(local_groups, groups, q_heads, HD), (1, 0, 2, 3))
    held_peak = held_stat[:, :, 0]
    held_total = held_stat[:, :, HD // 2]
    stats = jnp.concatenate(
        [
            held_peak.reshape(local_groups, groups, q_heads),
            held_total.reshape(local_groups, groups, q_heads),
            jnp.zeros((local_groups, groups, HD - 2 * q_heads), jnp.float32),
        ],
        axis=-1,
    )
    stats = jnp.transpose(stats, (1, 0, 2))[:, :, None, :]
    packed = jnp.concatenate([held_acc, stats], axis=2)
    back = lax.all_to_all(packed, "group", split_axis=0, concat_axis=0, tiled=True)
    holder = prompt_group // local_groups
    slot_index = prompt_group % local_groups
    mine = back[holder, slot_index]
    far_acc = mine[:, :q_heads, :]
    far_peak = mine[:, q_heads, :q_heads]
    far_total = mine[:, q_heads, q_heads : 2 * q_heads]

    near_queries = spread_lanes(rotated.reshape(requests, kv_heads, share, HD), kv_heads)
    own_count = suffix_keys.shape[1]
    near_valid = jnp.arange(own_count, dtype=jnp.int32)[None, None, :] < suffix_len[:, None, None]
    near_scores = (
        jnp.einsum("rqc,rtc->rqt", near_queries, suffix_keys, preferred_element_type=jnp.float32)
        * score_scale
    )
    near_peak, near_total, near_weights = softmax_parts(near_scores, near_valid)
    near_wide = jnp.einsum(
        "rqt,rtc->rqc", near_weights, suffix_values, preferred_element_type=jnp.float32
    )
    near_acc = pick_lanes(near_wide, kv_heads).reshape(requests, q_heads, HD)
    attn = combine(far_peak, far_total, far_acc, near_peak, near_total, near_acc)
    attn = attn.reshape(requests, q_heads * HD).astype(jnp.bfloat16)
    partial_out = jnp.dot(attn, out_weight, preferred_element_type=jnp.float32)
    return lax.psum_scatter(partial_out, "tensor", scatter_dimension=1, tiled=True).astype(
        jnp.bfloat16
    )


def solution(mesh):
    in_specs = (
        P("group", None),
        P(None, "tensor"),
        P("tensor", None),
        P("group", None, "tensor"),
        P("group", None, "tensor"),
        P("group", None),
        P(),
        P("group"),
        P("group", None, "tensor"),
        P("group", None, "tensor"),
        P("group"),
    )
    out_specs = P("group", "tensor")
    return jax.shard_map(body, mesh=mesh, in_specs=in_specs, out_specs=out_specs, check_vma=False)
```

profile of v0, /device:TPU:0, one launch (start us, length us, event | category | flops | bytes accessed | tf_op | source)
XLA Modules:
  0.0 133.3 jit_solution(194355837003670880)
XLA Ops:
  6.5 0.7 fusion.23
  7.7 4.9 %convolution_bitcast_fusion = f32[12,8,8,128]{3,1,2,0:T(8,128)S(1)} fusion(bf16[96,4096]{1,0:T(8,128)(2,1)S(1)} %copy-done, bf16[4096,1024]{1,0:T(8,128)(2,1)} %param.12), kind=kOutput, calls=%fused_computation.5 | convolution fusion | flops 805306368 | bytes 9568256 | tf_op jit(solution)/shard_map/dot_general | solution.py:194
  12.7 1.3 gather_fusion
  14.8 0.8 reshape.200
  15.7 5.2 %all-to-all-start = ((bf16[8,18,1024]{2,1,0:T(8,128)(2,1)}), bf16[8,18,1024]{2,1,0:T(8,128)(2,1)S(1)}, u32[]{:S(2)}, u32[]{:S(2)}) async-start(bf16[8,18,1024]{2,1,0:T(8,128)(2,1)} %reshape.200), calls=%async_computation | async-start | bytes 786432 | tf_op jit(solution)/shard_map/all_to_all | solution.py:205
  21.0 0.6 dynamic_slice.3.refs_1_
  21.7 0.7 reshape.198.refs_0_
  23.3 4.6 %fusion.32 = (f32[96,8]{1,0:T(8,128)S(1)}, f32[96,8,128]{2,1,0:T(8,128)S(1)}) fusion(bf16[96,128,256]{2,1,0:T(8,128)(2,1)} %param.19, bf16[96,8,256]{2,1,0:T(8,128)(2,1)S(1)} %mul.157, bf16[8,256]{1,0:T(8,128)(2,1)S(1)} %bitcast.67, pred[96,128]{1,0:T(8,128)(4,1)S(1)} %iota_compare_fusion.2), kind=kOutput, calls=%fused_computation.63 | convolution fusion | flops 50822400 | bytes 7097344 | tf_op jit(solution)/shard_map/rqc,rtc->rqt/dot_general | solution.py:247
  27.9 1.3 all-to-all-done
  29.5 0.5 mul.150
  30.3 0.9 broadcast_multiply_fusion.refs_2_
  31.2 27.7 %shard_map.109 = (f32[18,64,128]{2,1,0:T(8,128)}, f32[18,64,128]{2,1,0:T(8,128)}) custom-call(s32[1152]{0:T(1024)} %reshape.198.refs_0_, s32[18]{0:T(128)} %dynamic_slice.3.refs_1_, bf16[18,64,256]{2,1,0:T(8,128)(2,1)} %broadcast_multiply_fusion.refs_2_, bf16[1152,16,256]{2,1,0:T(8,128)(2,1)} %refs_3_.1, bf16[1152,16,256]{2,1,0:T(8,128)(2,1)} %refs_4_.1), custom_call_target="tpu_custom_call" | custom-call | flops 1207959552 | bytes 20643840 | tf_op jit(solution)/shard_map/pallas_call | solution.py:159
  58.9 1.5 %fusion.31 = (f32[18,64,1]{2,1,0:T(8,128)S(1)}, f32[18,64,1]{2,1,0:T(8,128)S(1)}) fusion(f32[18,64,128]{2,1,0:T(8,128)} %get-tuple-element.8), kind=kLoop, calls=%fused_computation.62 | loop fusion | bytes 18432 | tf_op jit(solution)/shard_map/slice | solution.py:223
  60.4 0.5 copy.40
  61.1 0.5 copy.41
  61.7 1.4 %copy.66 = f32[18,8,8,128]{3,0,2,1:T(8,128)S(1)} copy(f32[18,8,8,128]{3,2,1,0:T(8,128)} %bitcast.60) | data formatting | bytes 1179648 | tf_op jit(solution)/shard_map/reshape | solution.py:222
  63.3 1.0 pad_maximum_fusion
  64.2 4.0 %all-to-all-start.1 = ((f32[8,18,9,128]{3,1,2,0:T(8,128)}), f32[8,18,9,128]{3,1,2,0:T(8,128)S(1)}, u32[]{:S(2)}, u32[]{:S(2)}) async-start(f32[8,18,9,128]{3,1,2,0:T(8,128)} %pad_maximum_fusion), calls=%async_computation.1 | async-start | bytes 1769472 | tf_op jit(solution)/shard_map/all_to_all | solution.py:235
  68.5 3.8 %fusion.7 = f32[96,8,256]{2,1,0:T(8,128)S(1)} fusion(bf16[96,128,256]{2,1,0:T(8,128)(2,1)} %param.20, f32[96,8,128]{2,1,0:T(8,128)S(1)} %get-tuple-element.25, f32[96,8]{1,0:T(8,128)S(1)} %get-tuple-element.24, pred[96,128]{1,0:T(8,128)(4,1)S(1)} %iota_compare_fusion.2), kind=kOutput, calls=%fused_computation.20 | convolution fusion | flops 50626560 | bytes 7486464 | tf_op jit(solution)/shard_map/rqt,rtc->rqc/dot_general | solution.py:251
  73.5 8.4 %all-to-all-done.1 = f32[8,18,9,128]{3,1,2,0:T(8,128)S(1)} async-done(((f32[8,18,9,128]{3,1,2,0:T(8,128)}), f32[8,18,9,128]{3,1,2,0:T(8,128)S(1)}, u32[]{:S(2)}, u32[]{:S(2)}) %all-to-all-start.1) | async-done | bytes 663584 | tf_op jit(solution)/shard_map/all_to_all | solution.py:235
  82.1 1.2 gather_fusion.1
  83.8 6.1 %fusion.9 = f32[96,4096]{1,0:T(8,128)} fusion(bf16[1024,4096]{1,0:T(8,128)(2,1)} %param.13, bf16[12,8,8,128]{3,2,1,0:T(8,128)(2,1)S(1)} %bitcast.55), kind=kOutput, calls=%fused_computation.21 | convolution fusion | flops 805306368 | bytes 10158080 | tf_op jit(solution)/shard_map/dot_general | solution.py:257
  89.9 34.9 %reduce-scatter.2.cloned.1.call-done = f32[96,1024]{1,0:T(8,128)} async-done(((f32[96,4096]{1,0:T(8,128)}), f32[96,1024]{1,0:T(8,128)}) %reduce-scatter.2.cloned.1.call-update) | async-done | bytes 393232 | tf_op jit(solution)/shard_map/reduce_scatter | solution.py:258
  124.8 1.7 %convert_element_type.49 = bf16[96,1024]{1,0:T(8,128)(2,1)} convert(f32[96,1024]{1,0:T(8,128)} %reduce-scatter.2.cloned.1.call-done) | non-fusion elementwise | flops 98304 | bytes 589824 | tf_op jit(solution)/shard_map/convert_element_type | solution.py:258
  (48 shorter events, 5.6 us)
Async XLA Ops:
  6.5 1.1 copy-start
  7.7 5.0 %copy-start.2 = (s32[144]{0:T(256)S(1)}, s32[144]{0:T(256)}, u32[]{:S(2)}) copy-start(s32[144]{0:T(256)} %param.17) | copy-start | bytes 1732
  7.7 6.3 %copy-start.5 = (s32[96]{0:T(128)S(1)}, s32[96]{0:T(128)}, u32[]{:S(2)}) copy-start(s32[96]{0:T(128)} %param.21) | copy-start | bytes 1156
  7.7 6.9 %copy-start.4 = (s32[96]{0:T(128)S(1)}, s32[96]{0:T(128)}, u32[]{:S(2)}) copy-start(s32[96]{0:T(128)} %param.18) | copy-start | bytes 1156
  7.7 14.0 %copy-start.3 = (s32[18,64]{1,0:T(8,128)S(1)}, s32[18,64]{1,0:T(8,128)}, u32[]{:S(2)}) copy-start(s32[18,64]{1,0:T(8,128)} %param.16) | copy-start | bytes 13828
  15.7 13.5 %all-to-all-start = ((bf16[8,18,1024]{2,1,0:T(8,128)(2,1)}), bf16[8,18,1024]{2,1,0:T(8,128)(2,1)S(1)}, u32[]{:S(2)}, u32[]{:S(2)}) async-start(bf16[8,18,1024]{2,1,0:T(8,128)(2,1)} %reshape.200), calls=%async_computation | async-start | bytes 786432 | tf_op jit(solution)/shard_map/all_to_all | solution.py:205
  64.2 17.7 %all-to-all-start.1 = ((f32[8,18,9,128]{3,1,2,0:T(8,128)}), f32[8,18,9,128]{3,1,2,0:T(8,128)S(1)}, u32[]{:S(2)}, u32[]{:S(2)}) async-start(f32[8,18,9,128]{3,1,2,0:T(8,128)} %pad_maximum_fusion), calls=%async_computation.1 | async-start | bytes 1769472 | tf_op jit(solution)/shard_map/all_to_all | solution.py:235
  68.2 56.6 %reduce-scatter.2.cloned.1.call-start = ((), (), s32[]{:S(2)}) async-start(), calls=%async_computation.3 | async-start | bytes 1966080 | tf_op jit(solution)/shard_map/reduce_scatter | solution.py:258
  83.8 42.7 %copy-start.1 = (bf16[96,4096]{1,0:T(8,128)(2,1)S(1)}, bf16[96,4096]{1,0:T(8,128)(2,1)}, u32[]{:S(2)}) copy-start(bf16[96,4096]{1,0:T(8,128)(2,1)} %param.11) | copy-start | bytes 2359300
Sparse Core Ops, SparseCore 0:
  90.1 34.6 reduce-scatter.1
where the time goes:
time: 135 us; the launch traced here: 133 us
  waiting for transfers between devices  44.6 us (33%)
  Pallas kernels  27.7 us (21%)
  matrix products  19.5 us (14%)
  between operations  13.7 us (10%)
  local copies, waits for them, and re-layouts  12.3 us (9%)
  starting transfers between devices  9.39 us (7%)
  other arithmetic  6.13 us (5%)
    reduce_scatter x1, waiting for transfers between devices, body(): lax.psum_scatter(partial_out, 'tensor', scatter_dimension=1, tiled=True)  34.9 us
    pallas_call x1, Pallas kernels, far_attention(): pl.pallas_call(kernel, grid_spec=grid_spec, out_shape=[jax.ShapeDtypeStru...  27.7 us
    all_to_all x1, waiting for transfers between devices, body(): lax.all_to_all(packed, 'group', split_axis=0, concat_axis=0, tiled=True)  8.42 us
    dot_general x1, matrix products, body(): partial_out = jnp.dot(attn, out_weight, preferred_element_type=jnp.float32)  6.07 us
    all_to_all x1, starting transfers between devices, body(): lax.all_to_all(outgoing.reshape(groups, local_groups, q_heads * HD), 'gro...  5.17 us
    dot_general x1, matrix products, body(): jnp.dot(hidden, query_weight, preferred_element_type=jnp.float32)  4.88 us
    dot_general x1, matrix products, body(): jnp.einsum('rqc,rtc->rqt', near_queries, suffix_keys, preferred_element_t...  4.59 us
    all_to_all x1, starting transfers between devices, body(): lax.all_to_all(packed, 'group', split_axis=0, concat_axis=0, tiled=True)  4 us
  transfers between devices with their start and end apart: 3, of which 3 were waited for; matrix products, arithmetic and copies ran while one was open for 9% of the time, Pallas kernels for 0%

commit v1 on v0

--- a/solution.py
+++ b/solution.py
@@ -74,17 +74,21 @@
     def _():
         vbuf[...] = jnp.zeros_like(vbuf)
 
-    def used_blocks(group):
-        return (len_ref[group] + block - 1) // block
+    chunk = 8
+
+    def used_chunks(group):
+        return (len_ref[group] + block * chunk - 1) // (block * chunk)
 
     def fetch(group, slot):
-        def one(b, carry):
-            idx = table_ref[group * pblk + b]
-            pltpu.make_async_copy(k_hbm.at[idx], kbuf.at[slot, b], sems.at[0, slot, b]).start()
-            pltpu.make_async_copy(v_hbm.at[idx], vbuf.at[slot, b], sems.at[1, slot, b]).start()
+        def one(c, carry):
+            for i in range(chunk):
+                b = c * chunk + i
+                idx = table_ref[group * pblk + b]
+                pltpu.make_async_copy(k_hbm.at[idx], kbuf.at[slot, b], sems.at[0, slot, c]).start()
+                pltpu.make_async_copy(v_hbm.at[idx], vbuf.at[slot, b], sems.at[1, slot, c]).start()
             return carry
 
-        lax.fori_loop(0, used_blocks(group), one, 0)
+        lax.fori_loop(0, used_chunks(group), one, 0)
 
     @pl.when(j == 0)
     def _():
@@ -96,12 +100,17 @@
     def _():
         fetch(j + 1, 1 - slot)
 
-    def settle(b, carry):
-        pltpu.make_async_copy(k_hbm.at[0], kbuf.at[slot, b], sems.at[0, slot, b]).wait()
-        pltpu.make_async_copy(v_hbm.at[0], vbuf.at[slot, b], sems.at[1, slot, b]).wait()
+    def settle(c, carry):
+        part = pl.ds(pl.multiple_of(c * chunk, chunk), chunk)
+        pltpu.make_async_copy(
+            k_hbm.at[pl.ds(0, chunk)], kbuf.at[slot, part], sems.at[0, slot, c]
+        ).wait()
+        pltpu.make_async_copy(
+            v_hbm.at[pl.ds(0, chunk)], vbuf.at[slot, part], sems.at[1, slot, c]
+        ).wait()
         return carry
 
-    lax.fori_loop(0, used_blocks(j), settle, 0)
+    lax.fori_loop(0, used_chunks(j), settle, 0)
     keys = kbuf[slot].reshape(-1, width)
     values = vbuf[slot].reshape(-1, width)
     queries = q_ref[0]
@@ -129,6 +138,7 @@
 
 def far_attention(table, lengths, queries, prefix_keys, prefix_values, share, scale):
     local_groups, pblk = table.shape
+    assert pblk % 8 == 0
     _, rows, width = queries.shape
     block = prefix_keys.shape[1]
     tokens = pblk * block
@@ -148,7 +158,7 @@
         scratch_shapes=[
             pltpu.VMEM((2, pblk, block, width), prefix_keys.dtype),
             pltpu.VMEM((2, pblk, block, width), prefix_values.dtype),
-            pltpu.SemaphoreType.DMA((2, 2, pblk)),
+            pltpu.SemaphoreType.DMA((2, 2, pblk // 8)),
         ],
     )
     cost = pl.CostEstimate(

time: 135 us -> 127 us (0.941)
  Pallas kernels: 27.7 us -> 20 us
    pallas_call x1, Pallas kernels: 27.7 us -> 20 us  [far_attention(): pl.pallas_call(kernel, grid_spec=grid_spec, out_shape=[jax.ShapeDtypeStru...]
  transfers between devices with their start and end apart: 3 -> 3, of which waited for: 3 -> 3; matrix products, arithmetic and copies ran while one was open for 9% -> 10% of each run, Pallas kernels for 0% -> 0%
where the time goes in v1:
time: 127 us; the launch traced here: 125 us
  waiting for transfers between devices  44.5 us (35%)
  Pallas kernels  20 us (16%)
  matrix products  19.5 us (15%)
  between operations  13.7 us (11%)
  local copies, waits for them, and re-layouts  12.3 us (10%)
  starting transfers between devices  8.94 us (7%)
  other arithmetic  6.13 us (5%)
    reduce_scatter x1, waiting for transfers between devices, body(): lax.psum_scatter(partial_out, 'tensor', scatter_dimension=1, tiled=True)  34.8 us
    pallas_call x1, Pallas kernels, far_attention(): pl.pallas_call(kernel, grid_spec=grid_spec, out_shape=[jax.ShapeDtypeStru...  20 us
    all_to_all x1, waiting for transfers between devices, body(): lax.all_to_all(packed, 'group', split_axis=0, concat_axis=0, tiled=True)  8.34 us
    dot_general x1, matrix products, body(): partial_out = jnp.dot(attn, out_weight, preferred_element_type=jnp.float32)  6.07 us
    all_to_all x1, starting transfers between devices, body(): lax.all_to_all(outgoing.reshape(groups, local_groups, q_heads * HD), 'gro...  5.17 us
    dot_general x1, matrix products, body(): jnp.dot(hidden, query_weight, preferred_element_type=jnp.float32)  4.88 us
    dot_general x1, matrix products, body(): jnp.einsum('rqc,rtc->rqt', near_queries, suffix_keys, preferred_element_t...  4.59 us
    dot_general x1, matrix products, body(): jnp.einsum('rqt,rtc->rqc', near_weights, suffix_values, preferred_element...  3.77 us
  transfers between devices with their start and end apart: 3, of which 3 were waited for; matrix products, arithmetic and copies ran while one was open for 10% of the time, Pallas kernels for 0%

profile of v1, /device:TPU:0, one launch (start us, length us, event | category | flops | bytes accessed | tf_op | source)
XLA Modules:
  0.0 125.1 jit_solution(13723983693185296141)
XLA Ops:
  6.5 0.7 fusion.23
  7.7 4.9 %convolution_bitcast_fusion = f32[12,8,8,128]{3,1,2,0:T(8,128)S(1)} fusion(bf16[96,4096]{1,0:T(8,128)(2,1)S(1)} %copy-done, bf16[4096,1024]{1,0:T(8,128)(2,1)} %param.12), kind=kOutput, calls=%fused_computation.5 | convolution fusion | flops 805306368 | bytes 9568256 | tf_op jit(solution)/shard_map/dot_general | solution.py:204
  12.7 1.3 %gather_fusion = s32[96]{0:T(128)S(1)} fusion(s32[144]{0:T(256)S(1)} %copy-done.2, s32[1024]{0:T(1024)S(1)} %pad_clamp_fusion), kind=kCustom, calls=%fused_computation | custom fusion | bytes 1152 | tf_op jit(solution)/shard_map/gather | solution.py:207
  14.8 0.8 reshape.200
  15.7 5.2 %all-to-all-start = ((bf16[8,18,1024]{2,1,0:T(8,128)(2,1)}), bf16[8,18,1024]{2,1,0:T(8,128)(2,1)S(1)}, u32[]{:S(2)}, u32[]{:S(2)}) async-start(bf16[8,18,1024]{2,1,0:T(8,128)(2,1)} %reshape.200), calls=%async_computation | async-start | bytes 786432 | tf_op jit(solution)/shard_map/all_to_all | solution.py:215
  21.0 0.6 dynamic_slice.3.refs_1_
  21.7 0.7 reshape.198.refs_0_
  23.3 4.6 %fusion.32 = (f32[96,8]{1,0:T(8,128)S(1)}, f32[96,8,128]{2,1,0:T(8,128)S(1)}) fusion(bf16[96,128,256]{2,1,0:T(8,128)(2,1)} %param.19, bf16[96,8,256]{2,1,0:T(8,128)(2,1)S(1)} %mul.157, bf16[8,256]{1,0:T(8,128)(2,1)S(1)} %bitcast.67, pred[96,128]{1,0:T(8,128)(4,1)S(1)} %iota_compare_fusion.2), kind=kOutput, calls=%fused_computation.63 | convolution fusion | flops 50822400 | bytes 7097344 | tf_op jit(solution)/shard_map/rqc,rtc->rqt/dot_general | solution.py:257
  27.9 1.3 %all-to-all-done = bf16[8,18,1024]{2,1,0:T(8,128)(2,1)S(1)} async-done(((bf16[8,18,1024]{2,1,0:T(8,128)(2,1)}), bf16[8,18,1024]{2,1,0:T(8,128)(2,1)S(1)}, u32[]{:S(2)}, u32[]{:S(2)}) %all-to-all-start) | async-done | bytes 294944 | tf_op jit(solution)/shard_map/all_to_all | solution.py:215
  29.5 0.5 mul.150
  30.3 0.9 broadcast_multiply_fusion.refs_2_
  31.2 20.0 %shard_map.109 = (f32[18,64,128]{2,1,0:T(8,128)}, f32[18,64,128]{2,1,0:T(8,128)}) custom-call(s32[1152]{0:T(1024)} %reshape.198.refs_0_, s32[18]{0:T(128)} %dynamic_slice.3.refs_1_, bf16[18,64,256]{2,1,0:T(8,128)(2,1)} %broadcast_multiply_fusion.refs_2_, bf16[1152,16,256]{2,1,0:T(8,128)(2,1)} %refs_3_.1, bf16[1152,16,256]{2,1,0:T(8,128)(2,1)} %refs_4_.1), custom_call_target="tpu_custom_call" | custom-call | flops 1207959552 | bytes 20643840 | tf_op jit(solution)/shard_map/pallas_call | solution.py:169
  51.2 1.5 %fusion.31 = (f32[18,64,1]{2,1,0:T(8,128)S(1)}, f32[18,64,1]{2,1,0:T(8,128)S(1)}) fusion(f32[18,64,128]{2,1,0:T(8,128)} %get-tuple-element.8), kind=kLoop, calls=%fused_computation.62 | loop fusion | bytes 18432 | tf_op jit(solution)/shard_map/slice | solution.py:233
  52.7 0.5 copy.40
  53.4 0.5 copy.41
  54.0 1.4 %copy.66 = f32[18,8,8,128]{3,0,2,1:T(8,128)S(1)} copy(f32[18,8,8,128]{3,2,1,0:T(8,128)} %bitcast.60) | data formatting | bytes 1179648 | tf_op jit(solution)/shard_map/reshape | solution.py:232
  55.5 1.0 pad_maximum_fusion
  56.5 3.5 %all-to-all-start.1 = ((f32[8,18,9,128]{3,1,2,0:T(8,128)}), f32[8,18,9,128]{3,1,2,0:T(8,128)S(1)}, u32[]{:S(2)}, u32[]{:S(2)}) async-start(f32[8,18,9,128]{3,1,2,0:T(8,128)} %pad_maximum_fusion), calls=%async_computation.1 | async-start | bytes 1769472 | tf_op jit(solution)/shard_map/all_to_all | solution.py:245
  60.3 3.8 %fusion.7 = f32[96,8,256]{2,1,0:T(8,128)S(1)} fusion(bf16[96,128,256]{2,1,0:T(8,128)(2,1)} %param.20, f32[96,8,128]{2,1,0:T(8,128)S(1)} %get-tuple-element.25, f32[96,8]{1,0:T(8,128)S(1)} %get-tuple-element.24, pred[96,128]{1,0:T(8,128)(4,1)S(1)} %iota_compare_fusion.2), kind=kOutput, calls=%fused_computation.20 | convolution fusion | flops 50626560 | bytes 7486464 | tf_op jit(solution)/shard_map/rqt,rtc->rqc/dot_general | solution.py:261
  65.3 8.3 %all-to-all-done.1 = f32[8,18,9,128]{3,1,2,0:T(8,128)S(1)} async-done(((f32[8,18,9,128]{3,1,2,0:T(8,128)}), f32[8,18,9,128]{3,1,2,0:T(8,128)S(1)}, u32[]{:S(2)}, u32[]{:S(2)}) %all-to-all-start.1) | async-done | bytes 663584 | tf_op jit(solution)/shard_map/all_to_all | solution.py:245
  73.8 1.2 gather_fusion.1
  75.6 6.1 %fusion.9 = f32[96,4096]{1,0:T(8,128)} fusion(bf16[1024,4096]{1,0:T(8,128)(2,1)} %param.13, bf16[12,8,8,128]{3,2,1,0:T(8,128)(2,1)S(1)} %bitcast.55), kind=kOutput, calls=%fused_computation.21 | convolution fusion | flops 805306368 | bytes 10158080 | tf_op jit(solution)/shard_map/dot_general | solution.py:267
  81.7 34.8 %reduce-scatter.2.cloned.1.call-done = f32[96,1024]{1,0:T(8,128)} async-done(((f32[96,4096]{1,0:T(8,128)}), f32[96,1024]{1,0:T(8,128)}) %reduce-scatter.2.cloned.1.call-update) | async-done | bytes 393232 | tf_op jit(solution)/shard_map/reduce_scatter | solution.py:268
  116.5 1.7 %convert_element_type.49 = bf16[96,1024]{1,0:T(8,128)(2,1)} convert(f32[96,1024]{1,0:T(8,128)} %reduce-scatter.2.cloned.1.call-done) | non-fusion elementwise | flops 98304 | bytes 589824 | tf_op jit(solution)/shard_map/convert_element_type | solution.py:268
  (48 shorter events, 5.6 us)
Async XLA Ops:
  6.5 1.1 copy-start
  7.7 5.0 %copy-start.2 = (s32[144]{0:T(256)S(1)}, s32[144]{0:T(256)}, u32[]{:S(2)}) copy-start(s32[144]{0:T(256)} %param.17) | copy-start | bytes 1732
  7.7 6.3 %copy-start.5 = (s32[96]{0:T(128)S(1)}, s32[96]{0:T(128)}, u32[]{:S(2)}) copy-start(s32[96]{0:T(128)} %param.21) | copy-start | bytes 1156
  7.7 6.9 %copy-start.4 = (s32[96]{0:T(128)S(1)}, s32[96]{0:T(128)}, u32[]{:S(2)}) copy-start(s32[96]{0:T(128)} %param.18) | copy-start | bytes 1156
  7.7 14.0 %copy-start.3 = (s32[18,64]{1,0:T(8,128)S(1)}, s32[18,64]{1,0:T(8,128)}, u32[]{:S(2)}) copy-start(s32[18,64]{1,0:T(8,128)} %param.16) | copy-start | bytes 13828
  15.7 13.5 %all-to-all-start = ((bf16[8,18,1024]{2,1,0:T(8,128)(2,1)}), bf16[8,18,1024]{2,1,0:T(8,128)(2,1)S(1)}, u32[]{:S(2)}, u32[]{:S(2)}) async-start(bf16[8,18,1024]{2,1,0:T(8,128)(2,1)} %reshape.200), calls=%async_computation | async-start | bytes 786432 | tf_op jit(solution)/shard_map/all_to_all | solution.py:215
  56.5 17.1 %all-to-all-start.1 = ((f32[8,18,9,128]{3,1,2,0:T(8,128)}), f32[8,18,9,128]{3,1,2,0:T(8,128)S(1)}, u32[]{:S(2)}, u32[]{:S(2)}) async-start(f32[8,18,9,128]{3,1,2,0:T(8,128)} %pad_maximum_fusion), calls=%async_computation.1 | async-start | bytes 1769472 | tf_op jit(solution)/shard_map/all_to_all | solution.py:245
  60.1 56.5 %reduce-scatter.2.cloned.1.call-start = ((), (), s32[]{:S(2)}) async-start(), calls=%async_computation.3 | async-start | bytes 1966080 | tf_op jit(solution)/shard_map/reduce_scatter | solution.py:268
  75.6 42.6 %copy-start.1 = (bf16[96,4096]{1,0:T(8,128)(2,1)S(1)}, bf16[96,4096]{1,0:T(8,128)(2,1)}, u32[]{:S(2)}) copy-start(bf16[96,4096]{1,0:T(8,128)(2,1)} %param.11) | copy-start | bytes 2359300
Sparse Core Ops, SparseCore 0:
  81.8 34.6 reduce-scatter.1

commit v2 on v1

--- a/solution.py
+++ b/solution.py
@@ -60,21 +60,23 @@
 
 
 def far_kernel(
-    table_ref, len_ref, q_ref, k_hbm, v_hbm, acc_ref, stat_ref, kbuf, vbuf, sems, *, share, scale
+    table_ref, len_ref, q_ref, k_hbm, v_hbm, out_ref, kbuf, vbuf, sbuf, wbuf, sems, *, share, scale
 ):
     j = pl.program_id(0)
     steps = pl.num_programs(0)
     pblk = kbuf.shape[1]
+    block = kbuf.shape[2]
     width = kbuf.shape[3]
     kv_heads = width // HD
-
-    block = kbuf.shape[2]
+    sources = out_ref.shape[0]
+    q_heads = out_ref.shape[2] - 1
+    chunk = 8
+    tile_blocks = 16
+    tile = tile_blocks * block
 
     @pl.when(j == 0)
     def _():
         vbuf[...] = jnp.zeros_like(vbuf)
-
-    chunk = 8
 
     def used_chunks(group):
         return (len_ref[group] + block * chunk - 1) // (block * chunk)
@@ -111,35 +113,57 @@
         return carry
 
     lax.fori_loop(0, used_chunks(j), settle, 0)
-    keys = kbuf[slot].reshape(-1, width)
-    values = vbuf[slot].reshape(-1, width)
+
+    length = len_ref[j]
+    used_tiles = (length + tile - 1) // tile
     queries = q_ref[0]
-    scores = (
-        lax.dot_general(
-            queries, keys, (((1,), (1,)), ((), ())), preferred_element_type=jnp.float32
+
+    def score_tile(c, carry):
+        keys = kbuf[slot, pl.ds(pl.multiple_of(c * tile_blocks, tile_blocks), tile_blocks)]
+        part = lax.dot_general(
+            queries, keys.reshape(tile, width), (((1,), (1,)), ((), ())),
+            preferred_element_type=jnp.float32,
         )
-        * scale
-    )
-    valid = lax.broadcasted_iota(jnp.int32, scores.shape, 1) < len_ref[j]
+        sbuf[:, pl.ds(pl.multiple_of(c * tile, tile), tile)] = part * scale
+        return carry
+
+    lax.fori_loop(0, used_tiles, score_tile, 0)
+    scores = sbuf[...]
+    valid = lax.broadcasted_iota(jnp.int32, scores.shape, 1) < length
     masked = jnp.where(valid, scores, masked_score)
     peak = jnp.max(masked, axis=1, keepdims=True)
     weights = jnp.where(valid, jnp.exp(masked - peak), 0.0)
     total = jnp.sum(weights, axis=1, keepdims=True)
-    wide = jnp.dot(weights.astype(jnp.bfloat16), values, preferred_element_type=jnp.float32)
-    rows = wide.shape[0]
+    wbuf[...] = weights.astype(jnp.bfloat16)
+    rows = scores.shape[0]
+
+    def value_tile(c, acc):
+        values = vbuf[slot, pl.ds(pl.multiple_of(c * tile_blocks, tile_blocks), tile_blocks)]
+        w = wbuf[:, pl.ds(pl.multiple_of(c * tile, tile), tile)]
+        return acc + jnp.dot(
+            w, values.reshape(tile, width), preferred_element_type=jnp.float32
+        )
+
+    wide = lax.fori_loop(0, used_tiles, value_tile, jnp.zeros((rows, width), jnp.float32))
     row_head = (lax.broadcasted_iota(jnp.int32, (rows, HD), 0) // share) % kv_heads
     acc = jnp.zeros((rows, HD), jnp.float32)
     for k in range(kv_heads):
         acc = jnp.where(row_head == k, wide[:, k * HD : (k + 1) * HD], acc)
-    acc_ref[0] = acc
-    lane = lax.broadcasted_iota(jnp.int32, (rows, HD), 1)
-    stat_ref[0] = jnp.where(lane < HD // 2, peak, total)
-
-
-def far_attention(table, lengths, queries, prefix_keys, prefix_values, share, scale):
+    out_ref[:, 0, :q_heads, :] = acc.reshape(sources, q_heads, HD)
+    lane = lax.broadcasted_iota(jnp.int32, (sources, q_heads, HD), 2)
+    head = lax.broadcasted_iota(jnp.int32, (sources, q_heads, HD), 1)
+    peak3 = jnp.broadcast_to(peak, (rows, HD)).reshape(sources, q_heads, HD)
+    total3 = jnp.broadcast_to(total, (rows, HD)).reshape(sources, q_heads, HD)
+    stat = jnp.where(lane == head, peak3, 0.0) + jnp.where(lane == head + q_heads, total3, 0.0)
+    out_ref[:, 0, q_heads, :] = jnp.sum(stat, axis=1)
+
+
+def far_attention(table, lengths, queries, prefix_keys, prefix_values, share, scale, sources):
     local_groups, pblk = table.shape
-    assert pblk % 8 == 0
+    assert pblk % 16 == 0
     _, rows, width = queries.shape
+    q_heads = rows // sources
+    assert 2 * q_heads <= HD
     block = prefix_keys.shape[1]
     tokens = pblk * block
     kernel = lambda *refs: far_kernel(*refs, share=share, scale=scale)
@@ -151,13 +175,12 @@
             pl.BlockSpec(memory_space=pl.ANY),
             pl.BlockSpec(memory_space=pl.ANY),
         ],
-        out_specs=[
-            pl.BlockSpec((1, rows, HD), lambda j, *_: (j, 0, 0)),
-            pl.BlockSpec((1, rows, HD), lambda j, *_: (j, 0, 0)),
-        ],
+        out_specs=pl.BlockSpec((sources, 1, q_heads + 1, HD), lambda j, *_: (0, j, 0, 0)),
         scratch_shapes=[
             pltpu.VMEM((2, pblk, block, width), prefix_keys.dtype),
             pltpu.VMEM((2, pblk, block, width), prefix_values.dtype),
+            pltpu.VMEM((rows, tokens), jnp.float32),
+            pltpu.VMEM((rows, tokens), jnp.bfloat16),
             pltpu.SemaphoreType.DMA((2, 2, pblk // 8)),
         ],
     )
@@ -169,10 +192,7 @@
     return pl.pallas_call(
         kernel,
         grid_spec=grid_spec,
-        out_shape=[
-            jax.ShapeDtypeStruct((local_groups, rows, HD), jnp.float32),
-            jax.ShapeDtypeStruct((local_groups, rows, HD), jnp.float32),
-        ],
+        out_shape=jax.ShapeDtypeStruct((sources, local_groups, q_heads + 1, HD), jnp.float32),
         compiler_params=pltpu.CompilerParams(dimension_semantics=("arbitrary",)),
         cost_estimate=cost,
     )(table.reshape(-1), lengths, queries, prefix_keys, prefix_values)
@@ -226,22 +246,10 @@
         local_groups, groups * q_heads, width
     )
     my_lengths = lax.dynamic_slice_in_dim(prompt_len, first_group, local_groups)
-    held_acc, held_stat = far_attention(
-        block_table, my_lengths, far_queries, prefix_keys, prefix_values, share, score_scale
-    )
-    held_acc = jnp.transpose(held_acc.reshape(local_groups, groups, q_heads, HD), (1, 0, 2, 3))
-    held_peak = held_stat[:, :, 0]
-    held_total = held_stat[:, :, HD // 2]
-    stats = jnp.concatenate(
-        [
-            held_peak.reshape(local_groups, groups, q_heads),
-            held_total.reshape(local_groups, groups, q_heads),
-            jnp.zeros((local_groups, groups, HD - 2 * q_heads), jnp.float32),
-        ],
-        axis=-1,
-    )
-    stats = jnp.transpose(stats, (1, 0, 2))[:, :, None, :]
-    packed = jnp.concatenate([held_acc, stats], axis=2)
+    packed = far_attention(
+        block_table, my_lengths, far_queries, prefix_keys, prefix_values, share, score_scale,
+        groups,
+    )
     back = lax.all_to_all(packed, "group", split_axis=0, concat_axis=0, tiled=True)
     holder = prompt_group // local_groups
     slot_index = prompt_group % local_groups

time: 127 us -> 135 us (1.063)
  Pallas kernels: 20 us -> 29.2 us
  waiting for transfers between devices: 44.5 us -> 42.4 us
    pallas_call x1, Pallas kernels: 20 us -> 29.2 us  [far_attention(): pl.pallas_call(kernel, grid_spec=grid_spec, out_shape=jax.ShapeDtypeStruc...]
    slice x3 -> x0, local copies, waits for them, and re-layouts: 2.54 us -> none  [the longest x2 2.01 us: body(): held_peak = held_stat[:, :, 0]]
    pallas_call x0 -> x1, local copies, waits for them, and re-layouts: none -> 2.45 us  [far_attention(): pl.pallas_call(kernel, grid_spec=grid_spec, out_shape=jax.ShapeDtypeStruc...]
    all_to_all x1, waiting for transfers between devices: 8.34 us -> 5.89 us  [body(): lax.all_to_all(packed, 'group', split_axis=0, concat_axis=0, tiled=True)]
    reshape x1 -> x0, local copies, waits for them, and re-layouts: 1.43 us -> none  [body(): held_acc.reshape(local_groups, groups, q_heads, HD)]
  transfers between devices with their start and end apart: 3 -> 3, of which waited for: 3 -> 3; matrix products, arithmetic and copies ran while one was open for 10% -> 11% of each run, Pallas kernels for 0% -> 0%
where the time goes in v2:
time: 135 us; the launch traced here: 133 us
  waiting for transfers between devices  42.4 us (31%)
  Pallas kernels  29.2 us (22%)
  matrix products  19.5 us (14%)
  between operations  13.6 us (10%)
  local copies, waits for them, and re-layouts  13.3 us (10%)
  starting transfers between devices  9.01 us (7%)
  other arithmetic  6.1 us (5%)
    reduce_scatter x1, waiting for transfers between devices, body(): lax.psum_scatter(partial_out, 'tensor', scatter_dimension=1, tiled=True)  35.2 us
    pallas_call x1, Pallas kernels, far_attention(): pl.pallas_call(kernel, grid_spec=grid_spec, out_shape=jax.ShapeDtypeStruc...  29.2 us
    dot_general x1, matrix products, body(): partial_out = jnp.dot(attn, out_weight, preferred_element_type=jnp.float32)  5.99 us
    all_to_all x1, waiting for transfers between devices, body(): lax.all_to_all(packed, 'group', split_axis=0, concat_axis=0, tiled=True)  5.89 us
    all_to_all x1, starting transfers between devices, body(): lax.all_to_all(outgoing.reshape(groups, local_groups, q_heads * HD), 'gro...  5.17 us
    dot_general x1, matrix products, body(): jnp.dot(hidden, query_weight, preferred_element_type=jnp.float32)  4.88 us
    dot_general x1, matrix products, body(): jnp.einsum('rqc,rtc->rqt', near_queries, suffix_keys, preferred_element_t...  4.59 us
    all_to_all x1, starting transfers between devices, body(): lax.all_to_all(packed, 'group', split_axis=0, concat_axis=0, tiled=True)  3.8 us
  transfers between devices with their start and end apart: 3, of which 3 were waited for; matrix products, arithmetic and copies ran while one was open for 11% of the time, Pallas kernels for 0%

profile of v2, /device:TPU:0, one launch (start us, length us, event | category | flops | bytes accessed | tf_op | source)
XLA Modules:
  0.0 133.0 jit_solution(5723473209739979571)
XLA Ops:
  6.5 0.7 fusion.23
  7.7 4.9 %convolution_bitcast_fusion = f32[12,8,8,128]{3,1,2,0:T(8,128)S(1)} fusion(bf16[96,4096]{1,0:T(8,128)(2,1)S(1)} %copy-done, bf16[4096,1024]{1,0:T(8,128)(2,1)} %param.12), kind=kOutput, calls=%fused_computation.5 | convolution fusion | flops 805306368 | bytes 9568256 | tf_op jit(solution)/shard_map/dot_general | solution.py:224
  12.7 1.3 gather_fusion
  14.8 0.8 reshape.197
  15.7 5.2 %all-to-all-start = ((bf16[8,18,1024]{2,1,0:T(8,128)(2,1)}), bf16[8,18,1024]{2,1,0:T(8,128)(2,1)S(1)}, u32[]{:S(2)}, u32[]{:S(2)}) async-start(bf16[8,18,1024]{2,1,0:T(8,128)(2,1)} %reshape.197), calls=%async_computation | async-start | bytes 786432 | tf_op jit(solution)/shard_map/all_to_all | solution.py:235
  20.9 0.7 dynamic_slice.3.refs_1_
  21.7 0.7 reshape.195.refs_0_
  23.3 4.6 %fusion.31 = (f32[96,8]{1,0:T(8,128)S(1)}, f32[96,8,128]{2,1,0:T(8,128)S(1)}) fusion(bf16[96,128,256]{2,1,0:T(8,128)(2,1)} %param.19, bf16[96,8,256]{2,1,0:T(8,128)(2,1)S(1)} %mul.157, bf16[8,256]{1,0:T(8,128)(2,1)S(1)} %bitcast.53, pred[96,128]{1,0:T(8,128)(4,1)S(1)} %iota_compare_fusion.2), kind=kOutput, calls=%fused_computation.59 | convolution fusion | flops 50822400 | bytes 7097344 | tf_op jit(solution)/shard_map/rqc,rtc->rqt/dot_general | solution.py:265
  27.9 1.3 all-to-all-done
  29.5 0.5 mul.150
  30.4 0.9 broadcast_multiply_fusion.refs_2_
  31.2 29.2 %shard_map.109 = f32[8,18,9,128]{3,2,1,0:T(8,128)} custom-call(s32[1152]{0:T(1024)} %reshape.195.refs_0_, s32[18]{0:T(128)} %dynamic_slice.3.refs_1_, bf16[18,64,256]{2,1,0:T(8,128)(2,1)} %broadcast_multiply_fusion.refs_2_, bf16[1152,16,256]{2,1,0:T(8,128)(2,1)} %refs_3_.1, bf16[1152,16,256]{2,1,0:T(8,128)(2,1)} %refs_4_.1), custom_call_target="tpu_custom_call" | custom-call | flops 1207959552 | bytes 20643840 | tf_op jit(solution)/shard_map/pallas_call | solution.py:192
  60.4 2.4 %copy.31 = f32[8,18,9,128]{3,1,2,0:T(8,128)} copy(f32[8,18,9,128]{3,2,1,0:T(8,128)} %shard_map.109) | data formatting | bytes 1327104 | tf_op jit(solution)/shard_map/pallas_call | solution.py:192
  62.9 3.8 %all-to-all-start.1 = ((f32[8,18,9,128]{3,1,2,0:T(8,128)}), f32[8,18,9,128]{3,1,2,0:T(8,128)S(1)}, u32[]{:S(2)}, u32[]{:S(2)}) async-start(f32[8,18,9,128]{3,1,2,0:T(8,128)} %copy.31), calls=%async_computation.1 | async-start | bytes 1769472 | tf_op jit(solution)/shard_map/all_to_all | solution.py:253
  66.7 3.8 %fusion.7 = f32[96,8,256]{2,1,0:T(8,128)S(1)} fusion(bf16[96,128,256]{2,1,0:T(8,128)(2,1)} %param.20, f32[96,8,128]{2,1,0:T(8,128)S(1)} %get-tuple-element.19, f32[96,8]{1,0:T(8,128)S(1)} %get-tuple-element.18, pred[96,128]{1,0:T(8,128)(4,1)S(1)} %iota_compare_fusion.2), kind=kOutput, calls=%fused_computation.18 | convolution fusion | flops 50626560 | bytes 7486464 | tf_op jit(solution)/shard_map/rqt,rtc->rqc/dot_general | solution.py:269
  70.5 1.3 reshape.199
  71.8 1.5 %fusion.30 = (f32[96,1,4,1,128]{4,3,2,1,0:T(1,128)S(1)}, f32[96,1,4,1,128]{4,3,2,1,0:T(1,128)S(1)}) fusion(f32[96,2,4,2,128]{4,3,2,1,0:T(2,128)} %reshape.199), kind=kLoop, calls=%fused_computation.58 | loop fusion | bytes 786432 | tf_op jit(solution)/shard_map/slice | solution.py:59
  73.3 0.8 copy.34
  74.4 5.9 %all-to-all-done.1 = f32[8,18,9,128]{3,1,2,0:T(8,128)S(1)} async-done(((f32[8,18,9,128]{3,1,2,0:T(8,128)}), f32[8,18,9,128]{3,1,2,0:T(8,128)S(1)}, u32[]{:S(2)}, u32[]{:S(2)}) %all-to-all-start.1) | async-done | bytes 663584 | tf_op jit(solution)/shard_map/all_to_all | solution.py:253
  80.5 1.2 gather_fusion.1
  81.9 1.4 %fusion.4 = bf16[96,8,128]{2,1,0:T(8,128)(2,1)S(1)} fusion(f32[96,8,128]{2,1,0:T(8,128)} %bitcast.43, f32[96,9,128]{2,1,0:T(8,128)S(1)} %gather_fusion.1, f32[96,8]{1,0:T(8,128)S(1)} %get-tuple-element.5, f32[96,8]{1,0:T(8,128)S(1)} %get-tuple-element.7, f32[96,8]{1,0:T(8,128)S(1)} %get-tuple-element.6), kind=kLoop, calls=%fused_computation.14 | loop fusion | flops 491520 | bytes 992256 | tf_op jit(solution)/shard_map/convert_element_type | solution.py:274
  83.3 6.0 %fusion.9 = f32[96,4096]{1,0:T(8,128)} fusion(bf16[1024,4096]{1,0:T(8,128)(2,1)} %param.13, bf16[12,8,8,128]{3,2,1,0:T(8,128)(2,1)S(1)} %bitcast.44), kind=kOutput, calls=%fused_computation.19 | convolution fusion | flops 805306368 | bytes 10158080 | tf_op jit(solution)/shard_map/dot_general | solution.py:275
  89.3 35.2 %reduce-scatter.2.cloned.1.call-done = f32[96,1024]{1,0:T(8,128)} async-done(((f32[96,4096]{1,0:T(8,128)}), f32[96,1024]{1,0:T(8,128)}) %reduce-scatter.2.cloned.1.call-update) | async-done | bytes 393232 | tf_op jit(solution)/shard_map/reduce_scatter | solution.py:276
  124.5 1.7 %convert_element_type.49 = bf16[96,1024]{1,0:T(8,128)(2,1)} convert(f32[96,1024]{1,0:T(8,128)} %reduce-scatter.2.cloned.1.call-done) | non-fusion elementwise | flops 98304 | bytes 589824 | tf_op jit(solution)/shard_map/convert_element_type | solution.py:276
  (37 shorter events, 3.9 us)
Async XLA Ops:
  6.5 1.1 copy-start
  7.7 5.0 %copy-start.1 = (s32[144]{0:T(256)S(1)}, s32[144]{0:T(256)}, u32[]{:S(2)}) copy-start(s32[144]{0:T(256)} %param.17) | copy-start | bytes 1732
  7.7 6.3 %copy-start.4 = (s32[96]{0:T(128)S(1)}, s32[96]{0:T(128)}, u32[]{:S(2)}) copy-start(s32[96]{0:T(128)} %param.21) | copy-start | bytes 1156
  7.7 6.9 %copy-start.3 = (s32[96]{0:T(128)S(1)}, s32[96]{0:T(128)}, u32[]{:S(2)}) copy-start(s32[96]{0:T(128)} %param.18) | copy-start | bytes 1156
  7.7 14.0 %copy-start.2 = (s32[18,64]{1,0:T(8,128)S(1)}, s32[18,64]{1,0:T(8,128)}, u32[]{:S(2)}) copy-start(s32[18,64]{1,0:T(8,128)} %param.16) | copy-start | bytes 13828
  15.7 13.5 %all-to-all-start = ((bf16[8,18,1024]{2,1,0:T(8,128)(2,1)}), bf16[8,18,1024]{2,1,0:T(8,128)(2,1)S(1)}, u32[]{:S(2)}, u32[]{:S(2)}) async-start(bf16[8,18,1024]{2,1,0:T(8,128)(2,1)} %reshape.197), calls=%async_computation | async-start | bytes 786432 | tf_op jit(solution)/shard_map/all_to_all | solution.py:235
  62.9 17.5 %all-to-all-start.1 = ((f32[8,18,9,128]{3,1,2,0:T(8,128)}), f32[8,18,9,128]{3,1,2,0:T(8,128)S(1)}, u32[]{:S(2)}, u32[]{:S(2)}) async-start(f32[8,18,9,128]{3,1,2,0:T(8,128)} %copy.31), calls=%async_computation.1 | async-start | bytes 1769472 | tf_op jit(solution)/shard_map/all_to_all | solution.py:253
  66.7 57.8 %reduce-scatter.2.cloned.1.call-start = ((), (), s32[]{:S(2)}) async-start(), calls=%async_computation.3 | async-start | bytes 1966080 | tf_op jit(solution)/shard_map/reduce_scatter | solution.py:276
Sparse Core Ops, SparseCore 0:
  89.4 35.0 reduce-scatter.1

commit v3 on v2

--- a/solution.py
+++ b/solution.py
@@ -60,7 +60,8 @@
 
 
 def far_kernel(
-    table_ref, len_ref, q_ref, k_hbm, v_hbm, out_ref, kbuf, vbuf, sbuf, wbuf, sems, *, share, scale
+    table_ref, len_ref, q_ref, k_hbm, v_hbm, out_ref, kbuf, vbuf, sbuf, wbuf, abuf, sems, *,
+    share, scale,
 ):
     j = pl.program_id(0)
     steps = pl.num_programs(0)
@@ -118,16 +119,17 @@
     used_tiles = (length + tile - 1) // tile
     queries = q_ref[0]
 
-    def score_tile(c, carry):
-        keys = kbuf[slot, pl.ds(pl.multiple_of(c * tile_blocks, tile_blocks), tile_blocks)]
-        part = lax.dot_general(
-            queries, keys.reshape(tile, width), (((1,), (1,)), ((), ())),
-            preferred_element_type=jnp.float32,
-        )
-        sbuf[:, pl.ds(pl.multiple_of(c * tile, tile), tile)] = part * scale
-        return carry
-
-    lax.fori_loop(0, used_tiles, score_tile, 0)
+    n_tiles = pblk // tile_blocks
+    for c in range(n_tiles):
+
+        @pl.when(c < used_tiles)
+        def _():
+            keys = kbuf[slot, c * tile_blocks : (c + 1) * tile_blocks].reshape(tile, width)
+            part = lax.dot_general(
+                queries, keys, (((1,), (1,)), ((), ())), preferred_element_type=jnp.float32
+            )
+            sbuf[:, c * tile : (c + 1) * tile] = part * scale
+
     scores = sbuf[...]
     valid = lax.broadcasted_iota(jnp.int32, scores.shape, 1) < length
     masked = jnp.where(valid, scores, masked_score)
@@ -136,15 +138,17 @@
     total = jnp.sum(weights, axis=1, keepdims=True)
     wbuf[...] = weights.astype(jnp.bfloat16)
     rows = scores.shape[0]
-
-    def value_tile(c, acc):
-        values = vbuf[slot, pl.ds(pl.multiple_of(c * tile_blocks, tile_blocks), tile_blocks)]
-        w = wbuf[:, pl.ds(pl.multiple_of(c * tile, tile), tile)]
-        return acc + jnp.dot(
-            w, values.reshape(tile, width), preferred_element_type=jnp.float32
-        )
-
-    wide = lax.fori_loop(0, used_tiles, value_tile, jnp.zeros((rows, width), jnp.float32))
+    abuf[...] = jnp.zeros_like(abuf)
+    for c in range(n_tiles):
+
+        @pl.when(c < used_tiles)
+        def _():
+            values = vbuf[slot, c * tile_blocks : (c + 1) * tile_blocks].reshape(tile, width)
+            abuf[...] += jnp.dot(
+                wbuf[:, c * tile : (c + 1) * tile], values, preferred_element_type=jnp.float32
+            )
+
+    wide = abuf[...]
     row_head = (lax.broadcasted_iota(jnp.int32, (rows, HD), 0) // share) % kv_heads
     acc = jnp.zeros((rows, HD), jnp.float32)
     for k in range(kv_heads):
@@ -181,6 +185,7 @@
             pltpu.VMEM((2, pblk, block, width), prefix_values.dtype),
             pltpu.VMEM((rows, tokens), jnp.float32),
             pltpu.VMEM((rows, tokens), jnp.bfloat16),
+            pltpu.VMEM((rows, width), jnp.float32),
             pltpu.SemaphoreType.DMA((2, 2, pblk // 8)),
         ],
     )

time: 135 us -> 136 us (level)
  the two profiles are of different devices: /device:TPU:0 before, /device:TPU:2 now
where the time goes in v3:
time: 136 us; the launch traced here: 134 us
  waiting for transfers between devices  40.3 us (30%)
  Pallas kernels  29.6 us (22%)
  matrix products  19.4 us (14%)
  between operations  13.6 us (10%)
  local copies, waits for them, and re-layouts  13.3 us (10%)
  starting transfers between devices  11.3 us (8%)
  other arithmetic  6.1 us (4%)
    reduce_scatter x1, waiting for transfers between devices, body(): lax.psum_scatter(partial_out, 'tensor', scatter_dimension=1, tiled=True)  35.8 us
    pallas_call x1, Pallas kernels, far_attention(): pl.pallas_call(kernel, grid_spec=grid_spec, out_shape=jax.ShapeDtypeStruc...  29.6 us
    all_to_all x1, starting transfers between devices, body(): lax.all_to_all(packed, 'group', split_axis=0, concat_axis=0, tiled=True)  7.08 us
    dot_general x1, matrix products, body(): partial_out = jnp.dot(attn, out_weight, preferred_element_type=jnp.float32)  5.99 us
    dot_general x1, matrix products, body(): jnp.dot(hidden, query_weight, preferred_element_type=jnp.float32)  4.88 us
    dot_general x1, matrix products, body(): jnp.einsum('rqc,rtc->rqt', near_queries, suffix_keys, preferred_element_t...  4.59 us
    all_to_all x1, waiting for transfers between devices, body(): lax.all_to_all(packed, 'group', split_axis=0, concat_axis=0, tiled=True)  4.45 us
    all_to_all x1, starting transfers between devices, body(): lax.all_to_all(outgoing.reshape(groups, local_groups, q_heads * HD), 'gro...  4.26 us
  transfers between devices with their start and end apart: 3, of which 2 were waited for; matrix products, arithmetic and copies ran while one was open for 11% of the time, Pallas kernels for 0%

profile of v3, /device:TPU:2, one launch (start us, length us, event | category | flops | bytes accessed | tf_op | source)
XLA Modules:
  0.0 133.7 jit_solution(13620743039110586792)
XLA Ops:
  6.5 0.7 fusion.23
  7.7 4.9 %convolution_bitcast_fusion = f32[12,8,8,128]{3,1,2,0:T(8,128)S(1)} fusion(bf16[96,4096]{1,0:T(8,128)(2,1)S(1)} %copy-done, bf16[4096,1024]{1,0:T(8,128)(2,1)} %param.12), kind=kOutput, calls=%fused_computation.5 | convolution fusion | flops 805306368 | bytes 9568256 | tf_op jit(solution)/shard_map/dot_general | solution.py:229
  12.7 1.3 gather_fusion
  14.8 0.8 reshape.197
  15.7 4.3 %all-to-all-start = ((bf16[8,18,1024]{2,1,0:T(8,128)(2,1)}), bf16[8,18,1024]{2,1,0:T(8,128)(2,1)S(1)}, u32[]{:S(2)}, u32[]{:S(2)}) async-start(bf16[8,18,1024]{2,1,0:T(8,128)(2,1)} %reshape.197), calls=%async_computation | async-start | bytes 786432 | tf_op jit(solution)/shard_map/all_to_all | solution.py:240
  20.0 0.7 dynamic_slice.3.refs_1_
  20.8 0.7 reshape.195.refs_0_
  22.4 4.6 %fusion.31 = (f32[96,8]{1,0:T(8,128)S(1)}, f32[96,8,128]{2,1,0:T(8,128)S(1)}) fusion(bf16[96,128,256]{2,1,0:T(8,128)(2,1)} %param.19, bf16[96,8,256]{2,1,0:T(8,128)(2,1)S(1)} %mul.157, bf16[8,256]{1,0:T(8,128)(2,1)S(1)} %bitcast.53, pred[96,128]{1,0:T(8,128)(4,1)S(1)} %iota_compare_fusion.2), kind=kOutput, calls=%fused_computation.59 | convolution fusion | flops 50822400 | bytes 7097344 | tf_op jit(solution)/shard_map/rqc,rtc->rqt/dot_general | solution.py:270
  27.3 0.5 mul.150
  27.8 0.4 mul.151
  28.2 0.9 broadcast_multiply_fusion.refs_2_
  29.0 29.6 %shard_map.109 = f32[8,18,9,128]{3,2,1,0:T(8,128)} custom-call(s32[1152]{0:T(1024)} %reshape.195.refs_0_, s32[18]{0:T(128)} %dynamic_slice.3.refs_1_, bf16[18,64,256]{2,1,0:T(8,128)(2,1)} %broadcast_multiply_fusion.refs_2_, bf16[1152,16,256]{2,1,0:T(8,128)(2,1)} %refs_3_.1, bf16[1152,16,256]{2,1,0:T(8,128)(2,1)} %refs_4_.1), custom_call_target="tpu_custom_call" | custom-call | flops 1207959552 | bytes 20643840 | tf_op jit(solution)/shard_map/pallas_call | solution.py:197
  58.7 2.4 %copy.31 = f32[8,18,9,128]{3,1,2,0:T(8,128)} copy(f32[8,18,9,128]{3,2,1,0:T(8,128)} %shard_map.109) | data formatting | bytes 1327104 | tf_op jit(solution)/shard_map/pallas_call | solution.py:197
  61.1 7.1 %all-to-all-start.1 = ((f32[8,18,9,128]{3,1,2,0:T(8,128)}), f32[8,18,9,128]{3,1,2,0:T(8,128)S(1)}, u32[]{:S(2)}, u32[]{:S(2)}) async-start(f32[8,18,9,128]{3,1,2,0:T(8,128)} %copy.31), calls=%async_computation.1 | async-start | bytes 1769472 | tf_op jit(solution)/shard_map/all_to_all | solution.py:258
  68.2 3.8 %fusion.7 = f32[96,8,256]{2,1,0:T(8,128)S(1)} fusion(bf16[96,128,256]{2,1,0:T(8,128)(2,1)} %param.20, f32[96,8,128]{2,1,0:T(8,128)S(1)} %get-tuple-element.19, f32[96,8]{1,0:T(8,128)S(1)} %get-tuple-element.18, pred[96,128]{1,0:T(8,128)(4,1)S(1)} %iota_compare_fusion.2), kind=kOutput, calls=%fused_computation.18 | convolution fusion | flops 50626560 | bytes 7486464 | tf_op jit(solution)/shard_map/rqt,rtc->rqc/dot_general | solution.py:274
  72.0 1.3 reshape.199
  73.2 1.5 %fusion.30 = (f32[96,1,4,1,128]{4,3,2,1,0:T(1,128)S(1)}, f32[96,1,4,1,128]{4,3,2,1,0:T(1,128)S(1)}) fusion(f32[96,2,4,2,128]{4,3,2,1,0:T(2,128)} %reshape.199), kind=kLoop, calls=%fused_computation.58 | loop fusion | bytes 786432 | tf_op jit(solution)/shard_map/slice | solution.py:59
  74.8 0.8 copy.34
  75.9 4.4 %all-to-all-done.1 = f32[8,18,9,128]{3,1,2,0:T(8,128)S(1)} async-done(((f32[8,18,9,128]{3,1,2,0:T(8,128)}), f32[8,18,9,128]{3,1,2,0:T(8,128)S(1)}, u32[]{:S(2)}, u32[]{:S(2)}) %all-to-all-start.1) | async-done | bytes 663584 | tf_op jit(solution)/shard_map/all_to_all | solution.py:258
  80.5 1.2 gather_fusion.1
  81.9 1.4 %fusion.4 = bf16[96,8,128]{2,1,0:T(8,128)(2,1)S(1)} fusion(f32[96,8,128]{2,1,0:T(8,128)} %bitcast.43, f32[96,9,128]{2,1,0:T(8,128)S(1)} %gather_fusion.1, f32[96,8]{1,0:T(8,128)S(1)} %get-tuple-element.5, f32[96,8]{1,0:T(8,128)S(1)} %get-tuple-element.7, f32[96,8]{1,0:T(8,128)S(1)} %get-tuple-element.6), kind=kLoop, calls=%fused_computation.14 | loop fusion | flops 491520 | bytes 992256 | tf_op jit(solution)/shard_map/convert_element_type | solution.py:279
  83.3 6.0 %fusion.9 = f32[96,4096]{1,0:T(8,128)} fusion(bf16[1024,4096]{1,0:T(8,128)(2,1)} %param.13, bf16[12,8,8,128]{3,2,1,0:T(8,128)(2,1)S(1)} %bitcast.44), kind=kOutput, calls=%fused_computation.19 | convolution fusion | flops 805306368 | bytes 10158080 | tf_op jit(solution)/shard_map/dot_general | solution.py:280
  89.3 35.8 %reduce-scatter.2.cloned.1.call-done = f32[96,1024]{1,0:T(8,128)} async-done(((f32[96,4096]{1,0:T(8,128)}), f32[96,1024]{1,0:T(8,128)}) %reduce-scatter.2.cloned.1.call-update) | async-done | bytes 393232 | tf_op jit(solution)/shard_map/reduce_scatter | solution.py:281
  125.1 1.7 %convert_element_type.49 = bf16[96,1024]{1,0:T(8,128)(2,1)} convert(f32[96,1024]{1,0:T(8,128)} %reduce-scatter.2.cloned.1.call-done) | non-fusion elementwise | flops 98304 | bytes 589824 | tf_op jit(solution)/shard_map/convert_element_type | solution.py:281
  (37 shorter events, 3.5 us)
Async XLA Ops:
  6.5 1.1 copy-start
  7.7 5.0 %copy-start.1 = (s32[144]{0:T(256)S(1)}, s32[144]{0:T(256)}, u32[]{:S(2)}) copy-start(s32[144]{0:T(256)} %param.17) | copy-start | bytes 1732
  7.7 6.3 %copy-start.4 = (s32[96]{0:T(128)S(1)}, s32[96]{0:T(128)}, u32[]{:S(2)}) copy-start(s32[96]{0:T(128)} %param.21) | copy-start | bytes 1156
  7.7 6.9 %copy-start.3 = (s32[96]{0:T(128)S(1)}, s32[96]{0:T(128)}, u32[]{:S(2)}) copy-start(s32[96]{0:T(128)} %param.18) | copy-start | bytes 1156
  7.7 13.1 %copy-start.2 = (s32[18,64]{1,0:T(8,128)S(1)}, s32[18,64]{1,0:T(8,128)}, u32[]{:S(2)}) copy-start(s32[18,64]{1,0:T(8,128)} %param.16) | copy-start | bytes 13828
  15.7 11.3 %all-to-all-start = ((bf16[8,18,1024]{2,1,0:T(8,128)(2,1)}), bf16[8,18,1024]{2,1,0:T(8,128)(2,1)S(1)}, u32[]{:S(2)}, u32[]{:S(2)}) async-start(bf16[8,18,1024]{2,1,0:T(8,128)(2,1)} %reshape.197), calls=%async_computation | async-start | bytes 786432 | tf_op jit(solution)/shard_map/all_to_all | solution.py:240
  61.1 19.2 %all-to-all-start.1 = ((f32[8,18,9,128]{3,1,2,0:T(8,128)}), f32[8,18,9,128]{3,1,2,0:T(8,128)S(1)}, u32[]{:S(2)}, u32[]{:S(2)}) async-start(f32[8,18,9,128]{3,1,2,0:T(8,128)} %copy.31), calls=%async_computation.1 | async-start | bytes 1769472 | tf_op jit(solution)/shard_map/all_to_all | solution.py:258
  68.2 56.9 %reduce-scatter.2.cloned.1.call-start = ((), (), s32[]{:S(2)}) async-start(), calls=%async_computation.3 | async-start | bytes 1966080 | tf_op jit(solution)/shard_map/reduce_scatter | solution.py:281
Sparse Core Ops, SparseCore 0:
  89.4 35.6 reduce-scatter.1

commit v4 on v1

--- a/solution.py
+++ b/solution.py
@@ -264,10 +264,16 @@
     near_acc = pick_lanes(near_wide, kv_heads).reshape(requests, q_heads, HD)
     attn = combine(far_peak, far_total, far_acc, near_peak, near_total, near_acc)
     attn = attn.reshape(requests, q_heads * HD).astype(jnp.bfloat16)
-    partial_out = jnp.dot(attn, out_weight, preferred_element_type=jnp.float32)
-    return lax.psum_scatter(partial_out, "tensor", scatter_dimension=1, tiled=True).astype(
-        jnp.bfloat16
-    )
+    half = requests // 2
+    outs = []
+    for rows in (slice(0, half), slice(half, requests)):
+        partial_out = jnp.dot(attn[rows], out_weight, preferred_element_type=jnp.float32)
+        outs.append(
+            lax.psum_scatter(partial_out, "tensor", scatter_dimension=1, tiled=True).astype(
+                jnp.bfloat16
+            )
+        )
+    return jnp.concatenate(outs, axis=0)
 
 
 def solution(mesh):

time: 127 us -> 140 us (1.10)
  waiting for transfers between devices: 44.5 us -> 50.4 us
  matrix products: 19.5 us -> 25.3 us
    reduce_scatter x1 -> x2, waiting for transfers between devices: 34.8 us -> 40.8 us  [body(): lax.psum_scatter(partial_out, 'tensor', scatter_dimension=1, tiled=True)]
    dot_general x1 -> x2, matrix products: 6.07 us -> 11.8 us  [body(): jnp.dot(attn[rows], out_weight, preferred_element_type=jnp.float32)]
  transfers between devices with their start and end apart: 3 -> 4, of which waited for: 3 -> 4; matrix products, arithmetic and copies ran while one was open for 10% -> 14% of each run, Pallas kernels for 0% -> 0%
where the time goes in v4:
time: 140 us; the launch traced here: 138 us
  waiting for transfers between devices  50.4 us (36%)
  matrix products  25.3 us (18%)
  Pallas kernels  20.3 us (14%)
  between operations  13.7 us (10%)
  local copies, waits for them, and re-layouts  12.4 us (9%)
  starting transfers between devices  8.98 us (6%)
  other arithmetic  7.01 us (5%)
    reduce_scatter x2, waiting for transfers between devices, body(): lax.psum_scatter(partial_out, 'tensor', scatter_dimension=1, tiled=True)  40.8 us
    pallas_call x1, Pallas kernels, far_attention(): pl.pallas_call(kernel, grid_spec=grid_spec, out_shape=[jax.ShapeDtypeStru...  20.3 us
    dot_general x2, matrix products, body(): jnp.dot(attn[rows], out_weight, preferred_element_type=jnp.float32)  11.8 us
    all_to_all x1, waiting for transfers between devices, body(): lax.all_to_all(packed, 'group', split_axis=0, concat_axis=0, tiled=True)  8.35 us
    all_to_all x1, starting transfers between devices, body(): lax.all_to_all(outgoing.reshape(groups, local_groups, q_heads * HD), 'gro...  5.17 us
    dot_general x1, matrix products, body(): jnp.dot(hidden, query_weight, preferred_element_type=jnp.float32)  4.88 us
    dot_general x1, matrix products, body(): jnp.einsum('rqc,rtc->rqt', near_queries, suffix_keys, preferred_element_t...  4.59 us
    dot_general x1, matrix products, body(): jnp.einsum('rqt,rtc->rqc', near_weights, suffix_values, preferred_element...  3.77 us
  transfers between devices with their start and end apart: 4, of which 4 were waited for; matrix products, arithmetic and copies ran while one was open for 14% of the time, Pallas kernels for 0%

profile of v4, /device:TPU:0, one launch (start us, length us, event | category | flops | bytes accessed | tf_op | source)
XLA Modules:
  0.0 138.1 jit_solution(4304896275493579054)
XLA Ops:
  6.5 0.7 fusion.26
  7.7 4.9 %convolution_bitcast_fusion = f32[12,8,8,128]{3,1,2,0:T(8,128)S(1)} fusion(bf16[96,4096]{1,0:T(8,128)(2,1)S(1)} %copy-done, bf16[4096,1024]{1,0:T(8,128)(2,1)} %param.12), kind=kOutput, calls=%fused_computation.5 | convolution fusion | flops 805306368 | bytes 9568256 | tf_op jit(solution)/shard_map/dot_general | solution.py:204
  12.7 1.3 gather_fusion
  14.8 0.8 reshape.202
  15.6 5.2 %all-to-all-start = ((bf16[8,18,1024]{2,1,0:T(8,128)(2,1)}), bf16[8,18,1024]{2,1,0:T(8,128)(2,1)S(1)}, u32[]{:S(2)}, u32[]{:S(2)}) async-start(bf16[8,18,1024]{2,1,0:T(8,128)(2,1)} %reshape.202), calls=%async_computation | async-start | bytes 786432 | tf_op jit(solution)/shard_map/all_to_all | solution.py:215
  21.7 0.7 reshape.200.refs_0_
  23.3 4.6 %fusion.36 = (f32[96,8]{1,0:T(8,128)S(1)}, f32[96,8,128]{2,1,0:T(8,128)S(1)}) fusion(bf16[96,128,256]{2,1,0:T(8,128)(2,1)} %param.19, bf16[96,8,256]{2,1,0:T(8,128)(2,1)S(1)} %mul.157, bf16[8,256]{1,0:T(8,128)(2,1)S(1)} %bitcast.73, pred[96,128]{1,0:T(8,128)(4,1)S(1)} %iota_compare_fusion.2), kind=kOutput, calls=%fused_computation.68 | convolution fusion | flops 50822400 | bytes 7097344 | tf_op jit(solution)/shard_map/rqc,rtc->rqt/dot_general | solution.py:257
  27.9 1.2 all-to-all-done
  30.3 0.9 broadcast_multiply_fusion.refs_2_
  31.2 20.3 %shard_map.109 = (f32[18,64,128]{2,1,0:T(8,128)}, f32[18,64,128]{2,1,0:T(8,128)}) custom-call(s32[1152]{0:T(1024)} %reshape.200.refs_0_, s32[18]{0:T(128)} %dynamic_slice.3.refs_1_, bf16[18,64,256]{2,1,0:T(8,128)(2,1)} %broadcast_multiply_fusion.refs_2_, bf16[1152,16,256]{2,1,0:T(8,128)(2,1)} %refs_3_.1, bf16[1152,16,256]{2,1,0:T(8,128)(2,1)} %refs_4_.1), custom_call_target="tpu_custom_call" | custom-call | flops 1207959552 | bytes 20643840 | tf_op jit(solution)/shard_map/pallas_call | solution.py:169
  51.5 1.5 %fusion.34 = (f32[18,64,1]{2,1,0:T(8,128)S(1)}, f32[18,64,1]{2,1,0:T(8,128)S(1)}) fusion(f32[18,64,128]{2,1,0:T(8,128)} %get-tuple-element.8), kind=kLoop, calls=%fused_computation.66 | loop fusion | bytes 18432 | tf_op jit(solution)/shard_map/slice | solution.py:233
  54.3 1.4 %copy.71 = f32[18,8,8,128]{3,0,2,1:T(8,128)S(1)} copy(f32[18,8,8,128]{3,2,1,0:T(8,128)} %bitcast.66) | data formatting | bytes 1179648 | tf_op jit(solution)/shard_map/reshape | solution.py:232
  55.8 1.0 pad_maximum_fusion
  56.8 3.5 %all-to-all-start.1 = ((f32[8,18,9,128]{3,1,2,0:T(8,128)}), f32[8,18,9,128]{3,1,2,0:T(8,128)S(1)}, u32[]{:S(2)}, u32[]{:S(2)}) async-start(f32[8,18,9,128]{3,1,2,0:T(8,128)} %pad_maximum_fusion), calls=%async_computation.1 | async-start | bytes 1769472 | tf_op jit(solution)/shard_map/all_to_all | solution.py:245
  60.6 3.8 %fusion.7 = f32[96,8,256]{2,1,0:T(8,128)S(1)} fusion(bf16[96,128,256]{2,1,0:T(8,128)(2,1)} %param.20, f32[96,8,128]{2,1,0:T(8,128)S(1)} %get-tuple-element.27, f32[96,8]{1,0:T(8,128)S(1)} %get-tuple-element.26, pred[96,128]{1,0:T(8,128)(4,1)S(1)} %iota_compare_fusion.2), kind=kOutput, calls=%fused_computation.20 | convolution fusion | flops 50626560 | bytes 7486464 | tf_op jit(solution)/shard_map/rqt,rtc->rqc/dot_general | solution.py:261
  65.6 8.4 %all-to-all-done.1 = f32[8,18,9,128]{3,1,2,0:T(8,128)S(1)} async-done(((f32[8,18,9,128]{3,1,2,0:T(8,128)}), f32[8,18,9,128]{3,1,2,0:T(8,128)S(1)}, u32[]{:S(2)}, u32[]{:S(2)}) %all-to-all-start.1) | async-done | bytes 663584 | tf_op jit(solution)/shard_map/all_to_all | solution.py:245
  74.1 1.2 gather_fusion.1
  75.9 5.9 %fusion.18 = f32[48,4096]{1,0:T(8,128)} fusion(bf16[1024,4096]{1,0:T(8,128)(2,1)} %param.13, bf16[6,8,8,128]{3,2,1,0:T(8,128)(2,1)S(1)} %bitcast.65), kind=kOutput, calls=%fused_computation.33 | convolution fusion | flops 402653184 | bytes 9273344 | tf_op jit(solution)/shard_map/dot_general | solution.py:270
  81.9 5.9 %fusion.15 = f32[48,4096]{1,0:T(8,128)} fusion(bf16[1024,4096]{1,0:T(8,128)(2,1)} %param.13, bf16[6,8,8,128]{3,2,1,0:T(8,128)(2,1)S(1)} %bitcast.64), kind=kOutput, calls=%fused_computation.30 | convolution fusion | flops 402653184 | bytes 9273344 | tf_op jit(solution)/shard_map/dot_general | solution.py:270
  87.9 16.9 %reduce-scatter.3.cloned.1.call-done = f32[48,1024]{1,0:T(8,128)} async-done(((f32[48,4096]{1,0:T(8,128)}), f32[48,1024]{1,0:T(8,128)}) %reduce-scatter.3.cloned.1.call-update) | async-done | bytes 196624 | tf_op jit(solution)/shard_map/reduce_scatter | solution.py:272
  104.8 0.9 convert_element_type.49
  105.7 23.9 %reduce-scatter.5.cloned.1.call-done = f32[48,1024]{1,0:T(8,128)} async-done(((f32[48,4096]{1,0:T(8,128)}), f32[48,1024]{1,0:T(8,128)}) %reduce-scatter.5.cloned.1.call-update) | async-done | bytes 196624 | tf_op jit(solution)/shard_map/reduce_scatter | solution.py:272
  129.6 0.9 convert_element_type.50
  130.5 0.7 pad_maximum_fusion.4
  (55 shorter events, 7.9 us)
Async XLA Ops:
  6.5 1.1 copy-start
  7.7 5.0 %copy-start.2 = (s32[144]{0:T(256)S(1)}, s32[144]{0:T(256)}, u32[]{:S(2)}) copy-start(s32[144]{0:T(256)} %param.17) | copy-start | bytes 1732
  7.7 6.3 %copy-start.5 = (s32[96]{0:T(128)S(1)}, s32[96]{0:T(128)}, u32[]{:S(2)}) copy-start(s32[96]{0:T(128)} %param.21) | copy-start | bytes 1156
  7.7 6.9 %copy-start.4 = (s32[96]{0:T(128)S(1)}, s32[96]{0:T(128)}, u32[]{:S(2)}) copy-start(s32[96]{0:T(128)} %param.18) | copy-start | bytes 1156
  7.7 14.0 %copy-start.3 = (s32[18,64]{1,0:T(8,128)S(1)}, s32[18,64]{1,0:T(8,128)}, u32[]{:S(2)}) copy-start(s32[18,64]{1,0:T(8,128)} %param.16) | copy-start | bytes 13828
  15.6 13.5 %all-to-all-start = ((bf16[8,18,1024]{2,1,0:T(8,128)(2,1)}), bf16[8,18,1024]{2,1,0:T(8,128)(2,1)S(1)}, u32[]{:S(2)}, u32[]{:S(2)}) async-start(bf16[8,18,1024]{2,1,0:T(8,128)(2,1)} %reshape.202), calls=%async_computation | async-start | bytes 786432 | tf_op jit(solution)/shard_map/all_to_all | solution.py:215
  56.8 17.2 %all-to-all-start.1 = ((f32[8,18,9,128]{3,1,2,0:T(8,128)}), f32[8,18,9,128]{3,1,2,0:T(8,128)S(1)}, u32[]{:S(2)}, u32[]{:S(2)}) async-start(f32[8,18,9,128]{3,1,2,0:T(8,128)} %pad_maximum_fusion), calls=%async_computation.1 | async-start | bytes 1769472 | tf_op jit(solution)/shard_map/all_to_all | solution.py:245
  60.4 44.4 %reduce-scatter.3.cloned.1.call-start = ((), (), s32[]{:S(2)}) async-start(), calls=%async_computation.4 | async-start | bytes 983040 | tf_op jit(solution)/shard_map/reduce_scatter | solution.py:272
  81.8 47.8 %reduce-scatter.5.cloned.1.call-start = ((), (), s32[]{:S(2)}) async-start(), calls=%async_computation.5 | async-start | bytes 983040 | tf_op jit(solution)/shard_map/reduce_scatter | solution.py:272
  81.9 49.3 %copy-start.1 = (bf16[96,4096]{1,0:T(8,128)(2,1)S(1)}, bf16[96,4096]{1,0:T(8,128)(2,1)}, u32[]{:S(2)}) copy-start(bf16[96,4096]{1,0:T(8,128)(2,1)} %param.11) | copy-start | bytes 2359300
Sparse Core Ops, SparseCore 0:
  81.9 22.7 reduce-scatter.2
  107.1 22.4 reduce-scatter.4

commit v5 on v1

--- a/solution.py
+++ b/solution.py
@@ -264,10 +264,18 @@
     near_acc = pick_lanes(near_wide, kv_heads).reshape(requests, q_heads, HD)
     attn = combine(far_peak, far_total, far_acc, near_peak, near_total, near_acc)
     attn = attn.reshape(requests, q_heads * HD).astype(jnp.bfloat16)
-    partial_out = jnp.dot(attn, out_weight, preferred_element_type=jnp.float32)
-    return lax.psum_scatter(partial_out, "tensor", scatter_dimension=1, tiled=True).astype(
-        jnp.bfloat16
-    )
+    parts = lax.axis_size("tensor")
+    partial_out = lax.optimization_barrier(
+        jnp.dot(attn, out_weight, preferred_element_type=jnp.float32)
+    )
+    pieces = lax.all_to_all(
+        jnp.transpose(partial_out.reshape(requests, parts, -1), (1, 0, 2)),
+        "tensor",
+        split_axis=0,
+        concat_axis=0,
+        tiled=True,
+    )
+    return jnp.sum(pieces, axis=0).astype(jnp.bfloat16)
 
 
 def solution(mesh):

time: 127 us -> 116 us (0.913)
  the two profiles are of different devices: /device:TPU:0 before, /device:TPU:2 now
where the time goes in v5:
time: 116 us; the launch traced here: 114 us
  blocking collectives  41.9 us (36%)
  Pallas kernels  19.9 us (17%)
  matrix products  18.4 us (16%)
  local copies, waits for them, and re-layouts  12.5 us (11%)
  starting transfers between devices  8.56 us (7%)
  waiting for transfers between devices  7.14 us (6%)
  other arithmetic  5.28 us (5%)
    all_to_all x1, blocking collectives, body(): lax.all_to_all(jnp.transpose(partial_out.reshape(requests, parts, -1), (1...  41.9 us
    pallas_call x1, Pallas kernels, far_attention(): pl.pallas_call(kernel, grid_spec=grid_spec, out_shape=[jax.ShapeDtypeStru...  19.9 us
    all_to_all x1, waiting for transfers between devices, body(): lax.all_to_all(packed, 'group', split_axis=0, concat_axis=0, tiled=True)  7.14 us
    dot_general x1, matrix products, body(): jnp.dot(attn, out_weight, preferred_element_type=jnp.float32)  4.91 us
    dot_general x1, matrix products, body(): jnp.dot(hidden, query_weight, preferred_element_type=jnp.float32)  4.88 us
    dot_general x1, matrix products, body(): jnp.einsum('rqc,rtc->rqt', near_queries, suffix_keys, preferred_element_t...  4.59 us
    all_to_all x1, starting transfers between devices, body(): lax.all_to_all(packed, 'group', split_axis=0, concat_axis=0, tiled=True)  4.3 us
    all_to_all x1, starting transfers between devices, body(): lax.all_to_all(outgoing.reshape(groups, local_groups, q_heads * HD), 'gro...  4.25 us
  transfers between devices with their start and end apart: 2, of which 1 were waited for; matrix products, arithmetic and copies ran while one was open for 11% of the time, Pallas kernels for 0%

profile of v5, /device:TPU:2, one launch (start us, length us, event | category | flops | bytes accessed | tf_op | source)
XLA Modules:
  0.0 113.8 jit_solution(16974516160730604743)
XLA Ops:
  0.0 0.7 fusion.23
  1.2 4.9 %convolution_bitcast_fusion = f32[12,8,8,128]{3,1,2,0:T(8,128)S(1)} fusion(bf16[96,4096]{1,0:T(8,128)(2,1)S(1)} %copy-done, bf16[4096,1024]{1,0:T(8,128)(2,1)} %param.12), kind=kOutput, calls=%fused_computation.6 | convolution fusion | flops 805306368 | bytes 9568256 | tf_op jit(solution)/shard_map/dot_general | solution.py:204
  6.1 1.3 %gather_fusion = s32[96]{0:T(128)S(1)} fusion(s32[144]{0:T(256)S(1)} %copy-done.2, s32[1024]{0:T(1024)S(1)} %pad_clamp_fusion), kind=kCustom, calls=%fused_computation | custom fusion | bytes 1152 | tf_op jit(solution)/shard_map/gather | solution.py:207
  8.3 0.8 reshape.203
  9.1 4.3 %all-to-all-start = ((bf16[8,18,1024]{2,1,0:T(8,128)(2,1)}), bf16[8,18,1024]{2,1,0:T(8,128)(2,1)S(1)}, u32[]{:S(2)}, u32[]{:S(2)}) async-start(bf16[8,18,1024]{2,1,0:T(8,128)(2,1)} %reshape.203), calls=%async_computation | async-start | bytes 786432 | tf_op jit(solution)/shard_map/all_to_all | solution.py:215
  13.5 0.7 dynamic_slice.3.refs_1_
  14.2 0.7 reshape.201.refs_0_
  15.9 4.6 %fusion.32 = (f32[96,8]{1,0:T(8,128)S(1)}, f32[96,8,128]{2,1,0:T(8,128)S(1)}) fusion(bf16[96,128,256]{2,1,0:T(8,128)(2,1)} %param.19, bf16[96,8,256]{2,1,0:T(8,128)(2,1)S(1)} %mul.157, bf16[8,256]{1,0:T(8,128)(2,1)S(1)} %bitcast.76, pred[96,128]{1,0:T(8,128)(4,1)S(1)} %iota_compare_fusion.2), kind=kOutput, calls=%fused_computation.64 | convolution fusion | flops 50822400 | bytes 7097344 | tf_op jit(solution)/shard_map/rqc,rtc->rqt/dot_general | solution.py:257
  20.8 0.5 mul.150
  21.7 0.9 broadcast_multiply_fusion.refs_2_
  22.5 19.9 %shard_map.109 = (f32[18,64,128]{2,1,0:T(8,128)}, f32[18,64,128]{2,1,0:T(8,128)}) custom-call(s32[1152]{0:T(1024)} %reshape.201.refs_0_, s32[18]{0:T(128)} %dynamic_slice.3.refs_1_, bf16[18,64,256]{2,1,0:T(8,128)(2,1)} %broadcast_multiply_fusion.refs_2_, bf16[1152,16,256]{2,1,0:T(8,128)(2,1)} %refs_3_.1, bf16[1152,16,256]{2,1,0:T(8,128)(2,1)} %refs_4_.1), custom_call_target="tpu_custom_call" | custom-call | flops 1207959552 | bytes 20643840 | tf_op jit(solution)/shard_map/pallas_call | solution.py:169
  42.4 1.4 %copy.71 = f32[18,8,8,128]{3,0,2,1:T(8,128)S(1)} copy(f32[18,8,8,128]{3,2,1,0:T(8,128)} %bitcast.69) | data formatting | bytes 1179648 | tf_op jit(solution)/shard_map/reshape | solution.py:232
  43.9 1.5 %fusion.31 = (f32[18,64,1]{2,1,0:T(8,128)S(1)}, f32[18,64,1]{2,1,0:T(8,128)S(1)}) fusion(f32[18,64,128]{2,1,0:T(8,128)} %get-tuple-element.8), kind=kLoop, calls=%fused_computation.63 | loop fusion | bytes 18432 | tf_op jit(solution)/shard_map/slice | solution.py:233
  45.3 0.5 copy.41
  45.9 0.5 copy.42
  46.7 1.0 pad_maximum_fusion
  47.7 4.3 %all-to-all-start.1 = ((f32[8,18,9,128]{3,1,2,0:T(8,128)}), f32[8,18,9,128]{3,1,2,0:T(8,128)S(1)}, u32[]{:S(2)}, u32[]{:S(2)}) async-start(f32[8,18,9,128]{3,1,2,0:T(8,128)} %pad_maximum_fusion), calls=%async_computation.1 | async-start | bytes 1769472 | tf_op jit(solution)/shard_map/all_to_all | solution.py:245
  52.0 3.8 %fusion.7 = f32[96,8,256]{2,1,0:T(8,128)S(1)} fusion(bf16[96,128,256]{2,1,0:T(8,128)(2,1)} %param.20, f32[96,8,128]{2,1,0:T(8,128)S(1)} %get-tuple-element.25, f32[96,8]{1,0:T(8,128)S(1)} %get-tuple-element.24, pred[96,128]{1,0:T(8,128)(4,1)S(1)} %iota_compare_fusion.2), kind=kOutput, calls=%fused_computation.21 | convolution fusion | flops 50626560 | bytes 7486464 | tf_op jit(solution)/shard_map/rqt,rtc->rqc/dot_general | solution.py:261
  55.8 0.4 reshape.206
  57.0 7.1 %all-to-all-done.1 = f32[8,18,9,128]{3,1,2,0:T(8,128)S(1)} async-done(((f32[8,18,9,128]{3,1,2,0:T(8,128)}), f32[8,18,9,128]{3,1,2,0:T(8,128)S(1)}, u32[]{:S(2)}, u32[]{:S(2)}) %all-to-all-start.1) | async-done | bytes 663584 | tf_op jit(solution)/shard_map/all_to_all | solution.py:245
  64.4 1.2 %gather_fusion.1 = f32[96,9,128]{2,1,0:T(8,128)S(1)} fusion(f32[8,18,9,128]{3,2,1,0:T(8,128)S(1)} %copy.45, s32[96]{0:T(128)S(1)} %get-tuple-element.22), kind=kCustom, calls=%fused_computation.1 | custom fusion | bytes 885504 | tf_op jit(solution)/shard_map/gather | solution.py:248
  66.1 4.9 %fusion.9 = f32[96,4096]{1,0:T(8,128)S(1)} fusion(bf16[1024,4096]{1,0:T(8,128)(2,1)} %param.13, bf16[12,8,8,128]{3,2,1,0:T(8,128)(2,1)S(1)} %bitcast.64), kind=kOutput, calls=%fused_computation.22 | convolution fusion | flops 805306368 | bytes 10158080 | tf_op jit(solution)/shard_map/dot_general | solution.py:269
  71.2 41.9 %all_to_all.15 = f32[4,96,1024]{2,1,0:T(8,128)S(1)} all-to-all(f32[4,96,1024]{2,1,0:T(8,128)S(1)} %bitcast.58), channel_id=1, replica_groups=mesh['group'=8,'tensor'=4] {'tensor'}, dimensions={0} | all-to-all | bytes 3145728 | tf_op jit(solution)/shard_map/all_to_all | solution.py:271
  113.0 0.8 reduce_sum.19
  (47 shorter events, 5.1 us)
Async XLA Ops:
  0.0 1.1 %copy-start = (bf16[96,4096]{1,0:T(8,128)(2,1)S(1)}, bf16[96,4096]{1,0:T(8,128)(2,1)}, u32[]{:S(2)}) copy-start(bf16[96,4096]{1,0:T(8,128)(2,1)} %param.11) | copy-start | bytes 2359300
  1.2 5.0 %copy-start.2 = (s32[144]{0:T(256)S(1)}, s32[144]{0:T(256)}, u32[]{:S(2)}) copy-start(s32[144]{0:T(256)} %param.17) | copy-start | bytes 1732
  1.2 6.3 %copy-start.5 = (s32[96]{0:T(128)S(1)}, s32[96]{0:T(128)}, u32[]{:S(2)}) copy-start(s32[96]{0:T(128)} %param.21) | copy-start | bytes 1156
  1.2 6.9 %copy-start.4 = (s32[96]{0:T(128)S(1)}, s32[96]{0:T(128)}, u32[]{:S(2)}) copy-start(s32[96]{0:T(128)} %param.18) | copy-start | bytes 1156
  1.2 13.1 %copy-start.3 = (s32[18,64]{1,0:T(8,128)S(1)}, s32[18,64]{1,0:T(8,128)}, u32[]{:S(2)}) copy-start(s32[18,64]{1,0:T(8,128)} %param.16) | copy-start | bytes 13828
  9.1 11.4 %all-to-all-start = ((bf16[8,18,1024]{2,1,0:T(8,128)(2,1)}), bf16[8,18,1024]{2,1,0:T(8,128)(2,1)S(1)}, u32[]{:S(2)}, u32[]{:S(2)}) async-start(bf16[8,18,1024]{2,1,0:T(8,128)(2,1)} %reshape.203), calls=%async_computation | async-start | bytes 786432 | tf_op jit(solution)/shard_map/all_to_all | solution.py:215
  47.7 16.5 %all-to-all-start.1 = ((f32[8,18,9,128]{3,1,2,0:T(8,128)}), f32[8,18,9,128]{3,1,2,0:T(8,128)S(1)}, u32[]{:S(2)}, u32[]{:S(2)}) async-start(f32[8,18,9,128]{3,1,2,0:T(8,128)} %pad_maximum_fusion), calls=%async_computation.1 | async-start | bytes 1769472 | tf_op jit(solution)/shard_map/all_to_all | solution.py:245
  66.1 47.7 %copy-start.1 = (bf16[96,4096]{1,0:T(8,128)(2,1)S(1)}, bf16[96,4096]{1,0:T(8,128)(2,1)}, u32[]{:S(2)}) copy-start(bf16[96,4096]{1,0:T(8,128)(2,1)} %param.11) | copy-start | bytes 2359300

commit v6 on v1

--- a/solution.py
+++ b/solution.py
@@ -264,10 +264,26 @@
     near_acc = pick_lanes(near_wide, kv_heads).reshape(requests, q_heads, HD)
     attn = combine(far_peak, far_total, far_acc, near_peak, near_total, near_acc)
     attn = attn.reshape(requests, q_heads * HD).astype(jnp.bfloat16)
-    partial_out = jnp.dot(attn, out_weight, preferred_element_type=jnp.float32)
-    return lax.psum_scatter(partial_out, "tensor", scatter_dimension=1, tiled=True).astype(
-        jnp.bfloat16
-    )
+    parts = lax.axis_size("tensor")
+    partial_out = lax.optimization_barrier(
+        jnp.dot(attn, out_weight, preferred_element_type=jnp.float32)
+    )
+    blocks = partial_out.reshape(requests, parts, -1)
+    me = lax.axis_index("tensor")
+
+    def block(c):
+        return lax.dynamic_index_in_dim(blocks, jnp.clip(c, 0, parts - 1), axis=1, keepdims=False)
+
+    rightward = [(i, i + 1) for i in range(parts - 1)]
+    leftward = [(i + 1, i) for i in range(parts - 1)]
+    from_left = jnp.zeros_like(block(me))
+    from_right = jnp.zeros_like(block(me))
+    for step in range(1, parts):
+        send_right = block(me + parts - step) + from_left
+        send_left = block(me - parts + step) + from_right
+        from_left = lax.ppermute(send_right, "tensor", rightward)
+        from_right = lax.ppermute(send_left, "tensor", leftward)
+    return (block(me) + from_left + from_right).astype(jnp.bfloat16)
 
 
 def solution(mesh):

time: 127 us -> 121 us (0.953)
  the two profiles are of different devices: /device:TPU:0 before, /device:TPU:2 now
where the time goes in v6:
time: 121 us; the launch traced here: 119 us
  waiting for transfers between devices  30.3 us (25%)
  starting transfers between devices  25.2 us (21%)
  Pallas kernels  20.5 us (17%)
  matrix products  19.5 us (16%)
  local copies, waits for them, and re-layouts  17.7 us (15%)
  other arithmetic  5.62 us (5%)
    pallas_call x1, Pallas kernels, far_attention(): pl.pallas_call(kernel, grid_spec=grid_spec, out_shape=[jax.ShapeDtypeStru...  20.5 us
    ppermute x3, waiting for transfers between devices, body(): from_left = lax.ppermute(send_right, 'tensor', rightward)  18.9 us
    ppermute x3, starting transfers between devices, body(): from_left = lax.ppermute(send_right, 'tensor', rightward)  12.3 us
    all_to_all x1, waiting for transfers between devices, body(): lax.all_to_all(packed, 'group', split_axis=0, concat_axis=0, tiled=True)  7.14 us
    dot_general x1, matrix products, body(): jnp.dot(attn, out_weight, preferred_element_type=jnp.float32)  6.01 us
    dot_general x1, matrix products, body(): jnp.dot(hidden, query_weight, preferred_element_type=jnp.float32)  4.88 us
    all_to_all x1, starting transfers between devices, body(): lax.all_to_all(packed, 'group', split_axis=0, concat_axis=0, tiled=True)  4.7 us
    dot_general x1, matrix products, body(): jnp.einsum('rqc,rtc->rqt', near_queries, suffix_keys, preferred_element_t...  4.59 us
  transfers between devices with their start and end apart: 8, of which 5 were waited for; matrix products, arithmetic and copies ran while one was open for 10% of the time, Pallas kernels for 0%

profile of v6, /device:TPU:2, one launch (start us, length us, event | category | flops | bytes accessed | tf_op | source)
XLA Modules:
  0.0 119.1 jit_solution(1070728138283431588)
XLA Ops:
  1.2 4.9 %convolution_bitcast_fusion = f32[12,8,8,128]{3,1,2,0:T(8,128)S(1)} fusion(bf16[96,4096]{1,0:T(8,128)(2,1)S(1)} %copy-done, bf16[4096,1024]{1,0:T(8,128)(2,1)} %param.12), kind=kOutput, calls=%fused_computation.5 | convolution fusion | flops 805306368 | bytes 9568256 | tf_op jit(solution)/shard_map/dot_general | solution.py:204
  6.1 1.3 %gather_fusion = s32[96]{0:T(128)S(1)} fusion(s32[144]{0:T(256)S(1)} %copy-done.2, s32[1024]{0:T(1024)S(1)} %pad_clamp_fusion), kind=kCustom, calls=%fused_computation | custom fusion | bytes 1152 | tf_op jit(solution)/shard_map/gather | solution.py:207
  9.1 4.3 %all-to-all-start = ((bf16[8,18,1024]{2,1,0:T(8,128)(2,1)}), bf16[8,18,1024]{2,1,0:T(8,128)(2,1)S(1)}, u32[]{:S(2)}, u32[]{:S(2)}) async-start(bf16[8,18,1024]{2,1,0:T(8,128)(2,1)} %reshape.203), calls=%async_computation | async-start | bytes 786432 | tf_op jit(solution)/shard_map/all_to_all | solution.py:215
  15.9 4.6 %fusion.34 = (f32[96,8]{1,0:T(8,128)S(1)}, f32[96,8,128]{2,1,0:T(8,128)S(1)}) fusion(bf16[96,128,256]{2,1,0:T(8,128)(2,1)} %param.19, bf16[96,8,256]{2,1,0:T(8,128)(2,1)S(1)} %mul.157, bf16[8,256]{1,0:T(8,128)(2,1)S(1)} %bitcast.89, pred[96,128]{1,0:T(8,128)(4,1)S(1)} %iota_compare_fusion.2), kind=kOutput, calls=%fused_computation.79 | convolution fusion | flops 50822400 | bytes 7097344 | tf_op jit(solution)/shard_map/rqc,rtc->rqt/dot_general | solution.py:257
  22.5 20.5 %shard_map.109 = (f32[18,64,128]{2,1,0:T(8,128)}, f32[18,64,128]{2,1,0:T(8,128)}) custom-call(s32[1152]{0:T(1024)} %reshape.201.refs_0_, s32[18]{0:T(128)} %dynamic_slice.25.refs_1_, bf16[18,64,256]{2,1,0:T(8,128)(2,1)} %broadcast_multiply_fusion.refs_2_, bf16[1152,16,256]{2,1,0:T(8,128)(2,1)} %refs_3_.1, bf16[1152,16,256]{2,1,0:T(8,128)(2,1)} %refs_4_.1), custom_call_target="tpu_custom_call" | custom-call | flops 1207959552 | bytes 20643840 | tf_op jit(solution)/shard_map/pallas_call | solution.py:169
  43.0 1.4 %copy.80 = f32[18,8,8,128]{3,0,2,1:T(8,128)S(1)} copy(f32[18,8,8,128]{3,2,1,0:T(8,128)} %bitcast.80) | data formatting | bytes 1179648 | tf_op jit(solution)/shard_map/reshape | solution.py:232
  44.4 1.5 %fusion.33 = (f32[18,64,1]{2,1,0:T(8,128)S(1)}, f32[18,64,1]{2,1,0:T(8,128)S(1)}) fusion(f32[18,64,128]{2,1,0:T(8,128)} %get-tuple-element.8), kind=kLoop, calls=%fused_computation.78 | loop fusion | bytes 18432 | tf_op jit(solution)/shard_map/slice | solution.py:233
  48.3 4.7 %all-to-all-start.1 = ((f32[8,18,9,128]{3,1,2,0:T(8,128)}), f32[8,18,9,128]{3,1,2,0:T(8,128)S(1)}, u32[]{:S(2)}, u32[]{:S(2)}) async-start(f32[8,18,9,128]{3,1,2,0:T(8,128)} %pad_maximum_fusion), calls=%async_computation.1 | async-start | bytes 1769472 | tf_op jit(solution)/shard_map/all_to_all | solution.py:245
  53.0 3.8 %fusion.9 = f32[96,8,256]{2,1,0:T(8,128)S(1)} fusion(bf16[96,128,256]{2,1,0:T(8,128)(2,1)} %param.20, f32[96,8,128]{2,1,0:T(8,128)S(1)} %get-tuple-element.32, f32[96,8]{1,0:T(8,128)S(1)} %get-tuple-element.31, pred[96,128]{1,0:T(8,128)(4,1)S(1)} %iota_compare_fusion.2), kind=kOutput, calls=%fused_computation.29 | convolution fusion | flops 50626560 | bytes 7486464 | tf_op jit(solution)/shard_map/rqt,rtc->rqc/dot_general | solution.py:261
  58.0 7.1 %all-to-all-done.1 = f32[8,18,9,128]{3,1,2,0:T(8,128)S(1)} async-done(((f32[8,18,9,128]{3,1,2,0:T(8,128)}), f32[8,18,9,128]{3,1,2,0:T(8,128)S(1)}, u32[]{:S(2)}, u32[]{:S(2)}) %all-to-all-start.1) | async-done | bytes 663584 | tf_op jit(solution)/shard_map/all_to_all | solution.py:245
  65.3 1.2 gather_fusion.1
  67.1 6.0 %fusion.11 = f32[96,4096]{1,0:T(8,128)} fusion(bf16[1024,4096]{1,0:T(8,128)(2,1)} %param.13, bf16[12,8,8,128]{3,2,1,0:T(8,128)(2,1)S(1)} %bitcast.75), kind=kOutput, calls=%fused_computation.30 | convolution fusion | flops 805306368 | bytes 10158080 | tf_op jit(solution)/shard_map/dot_general | solution.py:269
  73.1 2.4 %reshape.208 = f32[96,4,1024]{2,1,0:T(4,128)S(1)} reshape(f32[96,4096]{1,0:T(8,128)} %fusion.11) | data formatting | bytes 3145728 | tf_op jit(solution)/shard_map/reshape | solution.py:271
  75.5 2.8 %constant_dynamic-slice_fusion.6 = (f32[96,1,1024]{2,1,0:T(1,128)S(1)}, f32[96,1,1024]{2,1,0:T(1,128)S(1)}, f32[96,1,1024]{2,1,0:T(1,128)S(1)}, f32[96,1,1024]{2...) fusion(f32[96,4,1024]{2,1,0:T(4,128)S(1)} %reshape.208, ...), kind=kLoop, calls=%fused_computation.67 | loop fusion | bytes 5505052 | tf_op jit(solution)/shard_map/jit(dynamic_index_in_dim)/dynamic_slice | solution.py:275
  78.5 3.5 %collective-permute-start = (f32[96,1024]{1,0:T(8,128)S(1)}, f32[96,1024]{1,0:T(8,128)S(1)}, u32[]{:S(2)}, u32[]{:S(2)}) collective-permute-start(f32[96,1024]{1,0:T(8,128)S(1)} %bitcast.82), channel_id=1, source_target_pairs={{0,1},{1,2},{2,3},{4,5},{5,6},{6,7},{8,9},{9,10},{10,11},{12,13},{... | collective-permute-start | bytes 1179656 | tf_op jit(solution)/shard_map/ppermute | solution.py:284
  82.0 1.3 %collective-permute-start.3 = (f32[96,1024]{1,0:T(8,128)S(1)}, f32[96,1024]{1,0:T(8,128)S(1)}, u32[]{:S(2)}, u32[]{:S(2)}) collective-permute-start(f32[96,1024]{1,0:T(8,128)S(1)} %bitcast.81), channel_id=1, source_target_pairs={{1,0},{2,1},{3,2},{5,4},{6,5},{7,6},{9,8},{10,9},{11,10},{13,12},{... | collective-permute-start | bytes 1179656 | tf_op jit(solution)/shard_map/ppermute | solution.py:285
  83.3 7.2 %collective-permute-done = f32[96,1024]{1,0:T(8,128)S(1)} collective-permute-done((f32[96,1024]{1,0:T(8,128)S(1)}, f32[96,1024]{1,0:T(8,128)S(1)}, u32[]{:S(2)}, u32[]{:S(2)}) %collective-permute-start) | collective-permute-done | bytes 393248 | tf_op jit(solution)/shard_map/ppermute | solution.py:284
  90.6 4.4 %collective-permute-start.1 = (f32[96,1024]{1,0:T(8,128)S(1)}, f32[96,1024]{1,0:T(8,128)S(1)}, u32[]{:S(2)}, u32[]{:S(2)}) collective-permute-start(f32[96,1024]{1,0:T(8,128)S(1)} %bitcast_add_fusion.2), channel_id=1, source_target_pairs={{0,1},{1,2},{2,3},{4,5},{5,6},{6,7},{8,9},{9,10},{10,11},{12,13},{... | collective-permute-start | bytes 1179656 | tf_op jit(solution)/shard_map/ppermute | solution.py:284
  95.2 1.3 %collective-permute-start.4 = (f32[96,1024]{1,0:T(8,128)S(1)}, f32[96,1024]{1,0:T(8,128)S(1)}, u32[]{:S(2)}, u32[]{:S(2)}) collective-permute-start(f32[96,1024]{1,0:T(8,128)S(1)} %bitcast_add_fusion), channel_id=1, source_target_pairs={{1,0},{2,1},{3,2},{5,4},{6,5},{7,6},{9,8},{10,9},{11,10},{13,12},{... | collective-permute-start | bytes 1179656 | tf_op jit(solution)/shard_map/ppermute | solution.py:285
  96.5 6.3 %collective-permute-done.1 = f32[96,1024]{1,0:T(8,128)S(1)} collective-permute-done((f32[96,1024]{1,0:T(8,128)S(1)}, f32[96,1024]{1,0:T(8,128)S(1)}, u32[]{:S(2)}, u32[]{:S(2)}) %collective-permute-start.1) | collective-permute-done | bytes 393248 | tf_op jit(solution)/shard_map/ppermute | solution.py:284
  102.9 4.4 %collective-permute-start.2 = (f32[96,1024]{1,0:T(8,128)S(1)}, f32[96,1024]{1,0:T(8,128)S(1)}, u32[]{:S(2)}, u32[]{:S(2)}) collective-permute-start(f32[96,1024]{1,0:T(8,128)S(1)} %bitcast_add_fusion.3), channel_id=1, source_target_pairs={{0,1},{1,2},{2,3},{4,5},{5,6},{6,7},{8,9},{9,10},{10,11},{12,13},{... | collective-permute-start | bytes 1179656 | tf_op jit(solution)/shard_map/ppermute | solution.py:284
  107.4 1.3 %collective-permute-start.5 = (f32[96,1024]{1,0:T(8,128)S(1)}, f32[96,1024]{1,0:T(8,128)S(1)}, u32[]{:S(2)}, u32[]{:S(2)}) collective-permute-start(f32[96,1024]{1,0:T(8,128)S(1)} %bitcast_add_fusion.1), channel_id=1, source_target_pairs={{1,0},{2,1},{3,2},{5,4},{6,5},{7,6},{9,8},{10,9},{11,10},{13,12},{... | collective-permute-start | bytes 1179656 | tf_op jit(solution)/shard_map/ppermute | solution.py:285
  108.7 5.4 %collective-permute-done.2 = f32[96,1024]{1,0:T(8,128)S(1)} collective-permute-done((f32[96,1024]{1,0:T(8,128)S(1)}, f32[96,1024]{1,0:T(8,128)S(1)}, u32[]{:S(2)}, u32[]{:S(2)}) %collective-permute-start.2) | collective-permute-done | bytes 393248 | tf_op jit(solution)/shard_map/ppermute | solution.py:284
  114.1 4.2 %collective-permute-done.5 = f32[96,1024]{1,0:T(8,128)S(1)} collective-permute-done((f32[96,1024]{1,0:T(8,128)S(1)}, f32[96,1024]{1,0:T(8,128)S(1)}, u32[]{:S(2)}, u32[]{:S(2)}) %collective-permute-start.5) | collective-permute-done | bytes 393248 | tf_op jit(solution)/shard_map/ppermute | solution.py:285
  (65 shorter events, 13.0 us)
Async XLA Ops:
  0.0 1.1 copy-start
  1.2 5.0 %copy-start.2 = (s32[144]{0:T(256)S(1)}, s32[144]{0:T(256)}, u32[]{:S(2)}) copy-start(s32[144]{0:T(256)} %param.17) | copy-start | bytes 1732
  1.2 6.3 %copy-start.5 = (s32[96]{0:T(128)S(1)}, s32[96]{0:T(128)}, u32[]{:S(2)}) copy-start(s32[96]{0:T(128)} %param.21) | copy-start | bytes 1156
  1.2 6.9 %copy-start.4 = (s32[96]{0:T(128)S(1)}, s32[96]{0:T(128)}, u32[]{:S(2)}) copy-start(s32[96]{0:T(128)} %param.18) | copy-start | bytes 1156
  1.2 13.0 %copy-start.3 = (s32[18,64]{1,0:T(8,128)S(1)}, s32[18,64]{1,0:T(8,128)}, u32[]{:S(2)}) copy-start(s32[18,64]{1,0:T(8,128)} %param.16) | copy-start | bytes 13828
  9.1 11.3 %all-to-all-start = ((bf16[8,18,1024]{2,1,0:T(8,128)(2,1)}), bf16[8,18,1024]{2,1,0:T(8,128)(2,1)S(1)}, u32[]{:S(2)}, u32[]{:S(2)}) async-start(bf16[8,18,1024]{2,1,0:T(8,128)(2,1)} %reshape.203), calls=%async_computation | async-start | bytes 786432 | tf_op jit(solution)/shard_map/all_to_all | solution.py:215
  48.3 16.9 %all-to-all-start.1 = ((f32[8,18,9,128]{3,1,2,0:T(8,128)}), f32[8,18,9,128]{3,1,2,0:T(8,128)S(1)}, u32[]{:S(2)}, u32[]{:S(2)}) async-start(f32[8,18,9,128]{3,1,2,0:T(8,128)} %pad_maximum_fusion), calls=%async_computation.1 | async-start | bytes 1769472 | tf_op jit(solution)/shard_map/all_to_all | solution.py:245
  73.1 46.0 %copy-start.1 = (bf16[96,4096]{1,0:T(8,128)(2,1)S(1)}, bf16[96,4096]{1,0:T(8,128)(2,1)}, u32[]{:S(2)}) copy-start(bf16[96,4096]{1,0:T(8,128)(2,1)} %param.11) | copy-start | bytes 2359300
  78.5 12.1 %collective-permute-start = (f32[96,1024]{1,0:T(8,128)S(1)}, f32[96,1024]{1,0:T(8,128)S(1)}, u32[]{:S(2)}, u32[]{:S(2)}) collective-permute-start(f32[96,1024]{1,0:T(8,128)S(1)} %bitcast.82), channel_id=1, source_target_pairs={{0,1},{1,2},{2,3},{4,5},{5,6},{6,7},{8,9},{9,10},{10,11},{12,13},{... | collective-permute-start | bytes 1179656 | tf_op jit(solution)/shard_map/ppermute | solution.py:284
  82.0 13.0 %collective-permute-start.3 = (f32[96,1024]{1,0:T(8,128)S(1)}, f32[96,1024]{1,0:T(8,128)S(1)}, u32[]{:S(2)}, u32[]{:S(2)}) collective-permute-start(f32[96,1024]{1,0:T(8,128)S(1)} %bitcast.81), channel_id=1, source_target_pairs={{1,0},{2,1},{3,2},{5,4},{6,5},{7,6},{9,8},{10,9},{11,10},{13,12},{... | collective-permute-start | bytes 1179656 | tf_op jit(solution)/shard_map/ppermute | solution.py:285
  90.6 12.1 %collective-permute-start.1 = (f32[96,1024]{1,0:T(8,128)S(1)}, f32[96,1024]{1,0:T(8,128)S(1)}, u32[]{:S(2)}, u32[]{:S(2)}) collective-permute-start(f32[96,1024]{1,0:T(8,128)S(1)} %bitcast_add_fusion.2), channel_id=1, source_target_pairs={{0,1},{1,2},{2,3},{4,5},{5,6},{6,7},{8,9},{9,10},{10,11},{12,13},{... | collective-permute-start | bytes 1179656 | tf_op jit(solution)/shard_map/ppermute | solution.py:284
  95.2 12.1 %collective-permute-start.4 = (f32[96,1024]{1,0:T(8,128)S(1)}, f32[96,1024]{1,0:T(8,128)S(1)}, u32[]{:S(2)}, u32[]{:S(2)}) collective-permute-start(f32[96,1024]{1,0:T(8,128)S(1)} %bitcast_add_fusion), channel_id=1, source_target_pairs={{1,0},{2,1},{3,2},{5,4},{6,5},{7,6},{9,8},{10,9},{11,10},{13,12},{... | collective-permute-start | bytes 1179656 | tf_op jit(solution)/shard_map/ppermute | solution.py:285
  102.9 11.2 %collective-permute-start.2 = (f32[96,1024]{1,0:T(8,128)S(1)}, f32[96,1024]{1,0:T(8,128)S(1)}, u32[]{:S(2)}, u32[]{:S(2)}) collective-permute-start(f32[96,1024]{1,0:T(8,128)S(1)} %bitcast_add_fusion.3), channel_id=1, source_target_pairs={{0,1},{1,2},{2,3},{4,5},{5,6},{6,7},{8,9},{9,10},{10,11},{12,13},{... | collective-permute-start | bytes 1179656 | tf_op jit(solution)/shard_map/ppermute | solution.py:284
  107.4 10.9 %collective-permute-start.5 = (f32[96,1024]{1,0:T(8,128)S(1)}, f32[96,1024]{1,0:T(8,128)S(1)}, u32[]{:S(2)}, u32[]{:S(2)}) collective-permute-start(f32[96,1024]{1,0:T(8,128)S(1)} %bitcast_add_fusion.1), channel_id=1, source_target_pairs={{1,0},{2,1},{3,2},{5,4},{6,5},{7,6},{9,8},{10,9},{11,10},{13,12},{... | collective-permute-start | bytes 1179656 | tf_op jit(solution)/shard_map/ppermute | solution.py:285

commit v7 on v5

--- a/solution.py
+++ b/solution.py
@@ -204,7 +204,11 @@
     projected = jnp.dot(hidden, query_weight, preferred_element_type=jnp.float32).reshape(
         requests, q_heads, HD
     )
-    position = prompt_len[prompt_group] + suffix_len - 1
+    everyone = jnp.arange(prompt_len.shape[0], dtype=jnp.int32)
+    own_prompt = jnp.sum(
+        jnp.where(prompt_group[:, None] == everyone[None, :], prompt_len[None, :], 0), axis=1
+    )
+    position = own_prompt + suffix_len - 1
     rotated = rotate(projected, position).astype(jnp.bfloat16)
 
     slots = jnp.arange(groups * local_groups, dtype=jnp.int32)
@@ -243,9 +247,13 @@
     stats = jnp.transpose(stats, (1, 0, 2))[:, :, None, :]
     packed = jnp.concatenate([held_acc, stats], axis=2)
     back = lax.all_to_all(packed, "group", split_axis=0, concat_axis=0, tiled=True)
-    holder = prompt_group // local_groups
-    slot_index = prompt_group % local_groups
-    mine = back[holder, slot_index]
+    returned = jnp.dot(
+        picks.T.astype(jnp.float32),
+        back.reshape(groups * local_groups, -1),
+        precision=lax.Precision.HIGHEST,
+        preferred_element_type=jnp.float32,
+    )
+    mine = returned.reshape(requests, q_heads + 1, HD)
     far_acc = mine[:, :q_heads, :]
     far_peak = mine[:, q_heads, :q_heads]
     far_total = mine[:, q_heads, q_heads : 2 * q_heads]

time: 116 us -> 119 us (1.026)
  waiting for transfers between devices: 7.14 us -> 11.7 us
  local copies, waits for them, and re-layouts: 12.5 us -> 10.9 us
    all_to_all x1, waiting for transfers between devices: 7.14 us -> 11.7 us  [body(): lax.all_to_all(packed, 'group', split_axis=0, concat_axis=0, tiled=True)]
    gather x2 -> x0, local copies, waits for them, and re-layouts: 2.42 us -> none  [the longest x1 1.27 us: body(): position = prompt_len[prompt_group] + suffix_len - 1]
  transfers between devices with their start and end apart: 2 -> 2, of which waited for: 1 -> 1; matrix products, arithmetic and copies ran while one was open for 11% -> 10% of each run, Pallas kernels for 0% -> 0%
where the time goes in v7:
time: 119 us; the launch traced here: 117 us
  blocking collectives  41.9 us (35%)
  Pallas kernels  20.7 us (17%)
  matrix products  19 us (16%)
  waiting for transfers between devices  11.7 us (10%)
  local copies, waits for them, and re-layouts  10.9 us (9%)
  starting transfers between devices  7.94 us (7%)
  other arithmetic  4.57 us (4%)
    all_to_all x1, blocking collectives, body(): lax.all_to_all(jnp.transpose(partial_out.reshape(requests, parts, -1), (1...  41.9 us
    pallas_call x1, Pallas kernels, far_attention(): pl.pallas_call(kernel, grid_spec=grid_spec, out_shape=[jax.ShapeDtypeStru...  20.7 us
    all_to_all x1, waiting for transfers between devices, body(): lax.all_to_all(packed, 'group', split_axis=0, concat_axis=0, tiled=True)  11.7 us
    dot_general x1, matrix products, body(): jnp.dot(attn, out_weight, preferred_element_type=jnp.float32)  4.96 us
    dot_general x1, matrix products, body(): jnp.dot(hidden, query_weight, preferred_element_type=jnp.float32)  4.88 us
    dot_general x1, matrix products, body(): jnp.einsum('rqc,rtc->rqt', near_queries, suffix_keys, preferred_element_t...  4.59 us
    all_to_all x1, starting transfers between devices, body(): lax.all_to_all(outgoing.reshape(groups, local_groups, q_heads * HD), 'gro...  4.25 us
    dot_general x1, matrix products, body(): jnp.einsum('rqt,rtc->rqc', near_weights, suffix_values, preferred_element...  3.78 us
  transfers between devices with their start and end apart: 2, of which 1 were waited for; matrix products, arithmetic and copies ran while one was open for 10% of the time, Pallas kernels for 0%

profile of v7, /device:TPU:2, one launch (start us, length us, event | category | flops | bytes accessed | tf_op | source)
XLA Modules:
  0.0 117.0 jit_solution(11249697382376956647)
XLA Ops:
  0.0 1.1 copy-done
  1.1 4.9 %convolution_bitcast_fusion = f32[12,8,8,128]{3,1,2,0:T(8,128)S(1)} fusion(bf16[96,4096]{1,0:T(8,128)(2,1)S(1)} %copy-done, bf16[4096,1024]{1,0:T(8,128)(2,1)} %param.12), kind=kOutput, calls=%fused_computation.4 | convolution fusion | flops 805306368 | bytes 9568256 | tf_op jit(solution)/shard_map/dot_general | solution.py:204
  7.1 0.8 reshape.210
  7.9 4.3 %all-to-all-start = ((bf16[8,18,1024]{2,1,0:T(8,128)(2,1)}), bf16[8,18,1024]{2,1,0:T(8,128)(2,1)S(1)}, u32[]{:S(2)}, u32[]{:S(2)}) async-start(bf16[8,18,1024]{2,1,0:T(8,128)(2,1)} %reshape.210), calls=%async_computation | async-start | bytes 786432 | tf_op jit(solution)/shard_map/all_to_all | solution.py:219
  12.3 0.7 dynamic_slice.3.refs_1_
  13.0 0.7 reshape.208.refs_0_
  14.6 4.6 %fusion.34 = (f32[96,8]{1,0:T(8,128)S(1)}, f32[96,8,128]{2,1,0:T(8,128)S(1)}) fusion(bf16[96,128,256]{2,1,0:T(8,128)(2,1)} %param.19, bf16[96,8,256]{2,1,0:T(8,128)(2,1)S(1)} %mul.157, bf16[8,256]{1,0:T(8,128)(2,1)S(1)} %bitcast.101, pred[96,128]{1,0:T(8,128)(4,1)S(1)} %iota_compare_fusion.3), kind=kOutput, calls=%fused_computation.63 | convolution fusion | flops 50822400 | bytes 7097344 | tf_op jit(solution)/shard_map/rqc,rtc->rqt/dot_general | solution.py:265
  19.6 3.8 %fusion.10 = f32[96,8,256]{2,1,0:T(8,128)S(1)} fusion(bf16[96,128,256]{2,1,0:T(8,128)(2,1)} %param.20, f32[96,8,128]{2,1,0:T(8,128)S(1)} %get-tuple-element.23, f32[96,8]{1,0:T(8,128)S(1)} %get-tuple-element.22, pred[96,128]{1,0:T(8,128)(4,1)S(1)} %iota_compare_fusion.3), kind=kOutput, calls=%fused_computation.24 | convolution fusion | flops 50626560 | bytes 7486464 | tf_op jit(solution)/shard_map/rqt,rtc->rqc/dot_general | solution.py:269
  23.4 0.4 reshape.214
  24.2 0.5 mul.150
  25.1 0.9 broadcast_multiply_fusion.refs_2_
  26.0 20.7 %shard_map.109 = (f32[18,64,128]{2,1,0:T(8,128)}, f32[18,64,128]{2,1,0:T(8,128)}) custom-call(s32[1152]{0:T(1024)} %reshape.208.refs_0_, s32[18]{0:T(128)} %dynamic_slice.3.refs_1_, bf16[18,64,256]{2,1,0:T(8,128)(2,1)} %broadcast_multiply_fusion.refs_2_, bf16[1152,16,256]{2,1,0:T(8,128)(2,1)} %refs_3_.1, bf16[1152,16,256]{2,1,0:T(8,128)(2,1)} %refs_4_.1), custom_call_target="tpu_custom_call" | custom-call | flops 1207959552 | bytes 20643840 | tf_op jit(solution)/shard_map/pallas_call | solution.py:169
  46.7 1.4 %copy.151 = f32[18,8,8,128]{3,0,2,1:T(8,128)S(1)} copy(f32[18,8,8,128]{3,2,1,0:T(8,128)} %bitcast.96) | data formatting | bytes 1179648 | tf_op jit(solution)/shard_map/reshape | solution.py:236
  48.1 1.5 %fusion.32 = (f32[18,64,1]{2,1,0:T(8,128)S(1)}, f32[18,64,1]{2,1,0:T(8,128)S(1)}) fusion(f32[18,64,128]{2,1,0:T(8,128)} %get-tuple-element.8), kind=kLoop, calls=%fused_computation.61 | loop fusion | bytes 18432 | tf_op jit(solution)/shard_map/slice | solution.py:237
  49.6 0.5 copy.101
  50.1 0.5 copy.102
  51.0 1.0 pad_maximum_fusion
  52.0 3.7 %all-to-all-start.1 = ((f32[8,18,9,128]{3,1,2,0:T(8,128)}), f32[8,18,9,128]{3,1,2,0:T(8,128)S(1)}, u32[]{:S(2)}, u32[]{:S(2)}) async-start(f32[8,18,9,128]{3,1,2,0:T(8,128)} %pad_maximum_fusion), calls=%async_computation.1 | async-start | bytes 1769472 | tf_op jit(solution)/shard_map/all_to_all | solution.py:249
  56.1 11.7 %all-to-all-done.1 = f32[8,18,9,128]{3,1,2,0:T(8,128)S(1)} async-done(((f32[8,18,9,128]{3,1,2,0:T(8,128)}), f32[8,18,9,128]{3,1,2,0:T(8,128)S(1)}, u32[]{:S(2)}, u32[]{:S(2)}) %all-to-all-start.1) | async-done | bytes 663584 | tf_op jit(solution)/shard_map/all_to_all | solution.py:249
  68.0 0.6 fusion.1
  68.8 0.4 fusion.7
  69.3 5.0 %fusion.14 = f32[96,4096]{1,0:T(8,128)S(1)} fusion(bf16[1024,4096]{1,0:T(8,128)(2,1)} %param.13, bf16[96,8,128]{2,0,1:T(8,128)(2,1)S(1)} %fusion.7), kind=kOutput, calls=%fused_computation.27 | convolution fusion | flops 805306368 | bytes 10158080 | tf_op jit(solution)/shard_map/dot_general | solution.py:277
  74.3 41.9 %all_to_all.15 = f32[4,96,1024]{2,1,0:T(8,128)S(1)} all-to-all(f32[4,96,1024]{2,1,0:T(8,128)S(1)} %bitcast.88), channel_id=1, replica_groups=mesh['group'=8,'tensor'=4] {'tensor'}, dimensions={0} | all-to-all | bytes 3145728 | tf_op jit(solution)/shard_map/all_to_all | solution.py:279
  116.2 0.8 reduce_sum.29
  (50 shorter events, 4.5 us)
Async XLA Ops:
  0.0 1.1 copy-start
  1.1 5.0 %copy-start.3 = (s32[96]{0:T(128)S(1)}, s32[96]{0:T(128)}, u32[]{:S(2)}) copy-start(s32[96]{0:T(128)} %param.18) | copy-start | bytes 1156
  1.1 5.0 %copy-start.4 = (s32[144]{0:T(256)S(1)}, s32[144]{0:T(256)}, u32[]{:S(2)}) copy-start(s32[144]{0:T(256)} %param.17) | copy-start | bytes 1732
  1.1 5.1 %copy-start.5 = (s32[96]{0:T(128)S(1)}, s32[96]{0:T(128)}, u32[]{:S(2)}) copy-start(s32[96]{0:T(128)} %param.21) | copy-start | bytes 1156
  1.1 11.9 %copy-start.2 = (s32[18,64]{1,0:T(8,128)S(1)}, s32[18,64]{1,0:T(8,128)}, u32[]{:S(2)}) copy-start(s32[18,64]{1,0:T(8,128)} %param.16) | copy-start | bytes 13828
  7.9 16.0 %all-to-all-start = ((bf16[8,18,1024]{2,1,0:T(8,128)(2,1)}), bf16[8,18,1024]{2,1,0:T(8,128)(2,1)S(1)}, u32[]{:S(2)}, u32[]{:S(2)}) async-start(bf16[8,18,1024]{2,1,0:T(8,128)(2,1)} %reshape.210), calls=%async_computation | async-start | bytes 786432 | tf_op jit(solution)/shard_map/all_to_all | solution.py:219
  52.0 15.8 %all-to-all-start.1 = ((f32[8,18,9,128]{3,1,2,0:T(8,128)}), f32[8,18,9,128]{3,1,2,0:T(8,128)S(1)}, u32[]{:S(2)}, u32[]{:S(2)}) async-start(f32[8,18,9,128]{3,1,2,0:T(8,128)} %pad_maximum_fusion), calls=%async_computation.1 | async-start | bytes 1769472 | tf_op jit(solution)/shard_map/all_to_all | solution.py:249
  69.3 47.8 %copy-start.1 = (bf16[96,4096]{1,0:T(8,128)(2,1)S(1)}, bf16[96,4096]{1,0:T(8,128)(2,1)}, u32[]{:S(2)}) copy-start(bf16[96,4096]{1,0:T(8,128)(2,1)} %param.11) | copy-start | bytes 2359300

commit v8 on v7

--- a/solution.py
+++ b/solution.py
@@ -246,6 +246,16 @@
     )
     stats = jnp.transpose(stats, (1, 0, 2))[:, :, None, :]
     packed = jnp.concatenate([held_acc, stats], axis=2)
+
+    near_queries = spread_lanes(rotated.reshape(requests, kv_heads, share, HD), kv_heads)
+    own_count = suffix_keys.shape[1]
+    near_valid = jnp.arange(own_count, dtype=jnp.int32)[None, None, :] < suffix_len[:, None, None]
+    near_scores = (
+        jnp.einsum("rqc,rtc->rqt", near_queries, suffix_keys, preferred_element_type=jnp.float32)
+        * score_scale
+    )
+    near_peak, near_total, near_weights = softmax_parts(near_scores, near_valid)
+    packed, near_weights = lax.optimization_barrier((packed, near_weights))
     back = lax.all_to_all(packed, "group", split_axis=0, concat_axis=0, tiled=True)
     returned = jnp.dot(
         picks.T.astype(jnp.float32),
@@ -257,15 +267,6 @@
     far_acc = mine[:, :q_heads, :]
     far_peak = mine[:, q_heads, :q_heads]
     far_total = mine[:, q_heads, q_heads : 2 * q_heads]
-
-    near_queries = spread_lanes(rotated.reshape(requests, kv_heads, share, HD), kv_heads)
-    own_count = suffix_keys.shape[1]
-    near_valid = jnp.arange(own_count, dtype=jnp.int32)[None, None, :] < suffix_len[:, None, None]
-    near_scores = (
-        jnp.einsum("rqc,rtc->rqt", near_queries, suffix_keys, preferred_element_type=jnp.float32)
-        * score_scale
-    )
-    near_peak, near_total, near_weights = softmax_parts(near_scores, near_valid)
     near_wide = jnp.einsum(
         "rqt,rtc->rqc", near_weights, suffix_values, preferred_element_type=jnp.float32
     )

time: 119 us -> 115 us (0.966)
  waiting for transfers between devices: 11.7 us -> 7.38 us
    all_to_all x1, waiting for transfers between devices: 11.7 us -> 7.38 us  [body(): lax.all_to_all(packed, 'group', split_axis=0, concat_axis=0, tiled=True)]
  transfers between devices with their start and end apart: 2 -> 2, of which waited for: 1 -> 1; matrix products, arithmetic and copies ran while one was open for 10% -> 11% of each run, Pallas kernels for 0% -> 0%
where the time goes in v8:
time: 115 us; the launch traced here: 112 us
  blocking collectives  41.9 us (36%)
  Pallas kernels  20.6 us (18%)
  matrix products  18.9 us (16%)
  local copies, waits for them, and re-layouts  10.8 us (9%)
  starting transfers between devices  7.93 us (7%)
  waiting for transfers between devices  7.38 us (6%)
  other arithmetic  4.58 us (4%)
    all_to_all x1, blocking collectives, body(): lax.all_to_all(jnp.transpose(partial_out.reshape(requests, parts, -1), (1...  41.9 us
    pallas_call x1, Pallas kernels, far_attention(): pl.pallas_call(kernel, grid_spec=grid_spec, out_shape=[jax.ShapeDtypeStru...  20.6 us
    all_to_all x1, waiting for transfers between devices, body(): lax.all_to_all(packed, 'group', split_axis=0, concat_axis=0, tiled=True)  7.38 us
    dot_general x1, matrix products, body(): jnp.dot(attn, out_weight, preferred_element_type=jnp.float32)  4.95 us
    dot_general x1, matrix products, body(): jnp.dot(hidden, query_weight, preferred_element_type=jnp.float32)  4.87 us
    dot_general x1, matrix products, body(): jnp.einsum('rqc,rtc->rqt', near_queries, suffix_keys, preferred_element_t...  4.59 us
    all_to_all x1, starting transfers between devices, body(): lax.all_to_all(outgoing.reshape(groups, local_groups, q_heads * HD), 'gro...  4.25 us
    dot_general x1, matrix products, body(): jnp.einsum('rqt,rtc->rqc', near_weights, suffix_values, preferred_element...  3.7 us
  transfers between devices with their start and end apart: 2, of which 1 were waited for; matrix products, arithmetic and copies ran while one was open for 11% of the time, Pallas kernels for 0%

profile of v8, /device:TPU:2, one launch (start us, length us, event | category | flops | bytes accessed | tf_op | source)
XLA Modules:
  0.0 112.4 jit_solution(14748496371911693769)
XLA Ops:
  0.0 1.1 copy-done
  1.1 4.9 %convolution_bitcast_fusion = f32[12,8,8,128]{3,1,2,0:T(8,128)S(1)} fusion(bf16[96,4096]{1,0:T(8,128)(2,1)S(1)} %copy-done, bf16[4096,1024]{1,0:T(8,128)(2,1)} %param.12), kind=kOutput, calls=%fused_computation.4 | convolution fusion | flops 805306368 | bytes 9568256 | tf_op jit(solution)/shard_map/dot_general | solution.py:204
  7.1 0.8 reshape.210
  7.9 4.3 %all-to-all-start = ((bf16[8,18,1024]{2,1,0:T(8,128)(2,1)}), bf16[8,18,1024]{2,1,0:T(8,128)(2,1)S(1)}, u32[]{:S(2)}, u32[]{:S(2)}) async-start(bf16[8,18,1024]{2,1,0:T(8,128)(2,1)} %reshape.210), calls=%async_computation | async-start | bytes 786432 | tf_op jit(solution)/shard_map/all_to_all | solution.py:219
  13.2 4.6 %fusion.28 = (f32[96,8]{1,0:T(8,128)S(1)}, f32[96,8,128]{2,1,0:T(8,128)S(1)}) fusion(bf16[96,128,256]{2,1,0:T(8,128)(2,1)} %param.19, bf16[96,8,256]{2,1,0:T(8,128)(2,1)S(1)} %mul.157, bf16[8,256]{1,0:T(8,128)(2,1)S(1)} %bitcast.102, pred[96,128]{1,0:T(8,128)(4,1)S(1)} %iota_compare_fusion.3), kind=kOutput, calls=%fused_computation.58 | convolution fusion | flops 50822400 | bytes 7097344 | tf_op jit(solution)/shard_map/rqc,rtc->rqt/dot_general | solution.py:254
  17.7 0.6 dynamic_slice.3.refs_1_
  18.3 0.7 reshape.208.refs_0_
  19.9 0.5 mul.150
  20.8 0.9 broadcast_multiply_fusion.refs_2_
  21.7 20.6 %shard_map.109 = (f32[18,64,128]{2,1,0:T(8,128)}, f32[18,64,128]{2,1,0:T(8,128)}) custom-call(s32[1152]{0:T(1024)} %reshape.208.refs_0_, s32[18]{0:T(128)} %dynamic_slice.3.refs_1_, bf16[18,64,256]{2,1,0:T(8,128)(2,1)} %broadcast_multiply_fusion.refs_2_, bf16[1152,16,256]{2,1,0:T(8,128)(2,1)} %refs_3_.1, bf16[1152,16,256]{2,1,0:T(8,128)(2,1)} %refs_4_.1), custom_call_target="tpu_custom_call" | custom-call | flops 1207959552 | bytes 20643840 | tf_op jit(solution)/shard_map/pallas_call | solution.py:169
  42.3 1.4 %copy.151 = f32[18,8,8,128]{3,0,2,1:T(8,128)S(1)} copy(f32[18,8,8,128]{3,2,1,0:T(8,128)} %bitcast.97) | data formatting | bytes 1179648 | tf_op jit(solution)/shard_map/reshape | solution.py:236
  43.7 1.5 %fusion.26 = (f32[18,64,1]{2,1,0:T(8,128)S(1)}, f32[18,64,1]{2,1,0:T(8,128)S(1)}) fusion(f32[18,64,128]{2,1,0:T(8,128)} %get-tuple-element.10), kind=kLoop, calls=%fused_computation.56 | loop fusion | bytes 18432 | tf_op jit(solution)/shard_map/slice | solution.py:237
  45.2 0.5 copy.101
  45.7 0.5 copy.102
  46.6 1.0 pad_maximum_fusion
  47.6 3.7 %all-to-all-start.1 = ((f32[8,18,9,128]{3,1,2,0:T(8,128)}), f32[8,18,9,128]{3,1,2,0:T(8,128)S(1)}, u32[]{:S(2)}, u32[]{:S(2)}) async-start(f32[8,18,9,128]{3,1,2,0:T(8,128)} %pad_maximum_fusion), calls=%async_computation.1 | async-start | bytes 1769472 | tf_op jit(solution)/shard_map/all_to_all | solution.py:259
  51.3 3.7 %fusion.29 = f32[96,8,256]{2,1,0:T(8,128)S(1)} fusion(bf16[96,8,128]{2,1,0:T(8,128)(2,1)S(1)} %get-tuple-element.12, bf16[96,128,256]{2,1,0:T(8,128)(2,1)} %param.20), kind=kOutput, calls=%fused_computation.59 | convolution fusion | flops 50331648 | bytes 7274496 | tf_op jit(solution)/shard_map/rqt,rtc->rqc/dot_general | solution.py:270
  55.0 0.4 reshape.214
  55.9 7.4 %all-to-all-done.1 = f32[8,18,9,128]{3,1,2,0:T(8,128)S(1)} async-done(((f32[8,18,9,128]{3,1,2,0:T(8,128)}), f32[8,18,9,128]{3,1,2,0:T(8,128)S(1)}, u32[]{:S(2)}, u32[]{:S(2)}) %all-to-all-start.1) | async-done | bytes 663584 | tf_op jit(solution)/shard_map/all_to_all | solution.py:259
  63.4 0.6 fusion.1
  64.2 0.4 fusion.7
  64.6 5.0 %fusion.12 = f32[96,4096]{1,0:T(8,128)S(1)} fusion(bf16[1024,4096]{1,0:T(8,128)(2,1)} %param.13, bf16[96,8,128]{2,0,1:T(8,128)(2,1)S(1)} %fusion.7), kind=kOutput, calls=%fused_computation.26 | convolution fusion | flops 805306368 | bytes 10158080 | tf_op jit(solution)/shard_map/dot_general | solution.py:278
  69.7 41.9 %all_to_all.15 = f32[4,96,1024]{2,1,0:T(8,128)S(1)} all-to-all(f32[4,96,1024]{2,1,0:T(8,128)S(1)} %bitcast.89), channel_id=1, replica_groups=mesh['group'=8,'tensor'=4] {'tensor'}, dimensions={0} | all-to-all | bytes 3145728 | tf_op jit(solution)/shard_map/all_to_all | solution.py:280
  111.6 0.8 reduce_sum.29
  (50 shorter events, 4.5 us)
Async XLA Ops:
  0.0 1.1 %copy-start = (bf16[96,4096]{1,0:T(8,128)(2,1)S(1)}, bf16[96,4096]{1,0:T(8,128)(2,1)}, u32[]{:S(2)}) copy-start(bf16[96,4096]{1,0:T(8,128)(2,1)} %param.11) | copy-start | bytes 2359300
  1.1 5.0 %copy-start.3 = (s32[96]{0:T(128)S(1)}, s32[96]{0:T(128)}, u32[]{:S(2)}) copy-start(s32[96]{0:T(128)} %param.18) | copy-start | bytes 1156
  1.1 5.0 %copy-start.4 = (s32[144]{0:T(256)S(1)}, s32[144]{0:T(256)}, u32[]{:S(2)}) copy-start(s32[144]{0:T(256)} %param.17) | copy-start | bytes 1732
  1.1 5.1 %copy-start.5 = (s32[96]{0:T(128)S(1)}, s32[96]{0:T(128)}, u32[]{:S(2)}) copy-start(s32[96]{0:T(128)} %param.21) | copy-start | bytes 1156
  6.5 11.8 %copy-start.2 = (s32[18,64]{1,0:T(8,128)S(1)}, s32[18,64]{1,0:T(8,128)}, u32[]{:S(2)}) copy-start(s32[18,64]{1,0:T(8,128)} %param.16) | copy-start | bytes 13828
  7.9 11.7 %all-to-all-start = ((bf16[8,18,1024]{2,1,0:T(8,128)(2,1)}), bf16[8,18,1024]{2,1,0:T(8,128)(2,1)S(1)}, u32[]{:S(2)}, u32[]{:S(2)}) async-start(bf16[8,18,1024]{2,1,0:T(8,128)(2,1)} %reshape.210), calls=%async_computation | async-start | bytes 786432 | tf_op jit(solution)/shard_map/all_to_all | solution.py:219
  47.6 15.6 %all-to-all-start.1 = ((f32[8,18,9,128]{3,1,2,0:T(8,128)}), f32[8,18,9,128]{3,1,2,0:T(8,128)S(1)}, u32[]{:S(2)}, u32[]{:S(2)}) async-start(f32[8,18,9,128]{3,1,2,0:T(8,128)} %pad_maximum_fusion), calls=%async_computation.1 | async-start | bytes 1769472 | tf_op jit(solution)/shard_map/all_to_all | solution.py:259
  64.6 47.8 %copy-start.1 = (bf16[96,4096]{1,0:T(8,128)(2,1)S(1)}, bf16[96,4096]{1,0:T(8,128)(2,1)}, u32[]{:S(2)}) copy-start(bf16[96,4096]{1,0:T(8,128)(2,1)} %param.11) | copy-start | bytes 2359300

commit v9 on v8

--- a/solution.py
+++ b/solution.py
@@ -60,7 +60,7 @@
 
 
 def far_kernel(
-    table_ref, len_ref, q_ref, k_hbm, v_hbm, acc_ref, stat_ref, kbuf, vbuf, sems, *, share, scale
+    table_ref, len_ref, q_ref, k_hbm, v_hbm, out_ref, kbuf, vbuf, sems, *, share, scale
 ):
     j = pl.program_id(0)
     steps = pl.num_programs(0)
@@ -131,15 +131,23 @@
     acc = jnp.zeros((rows, HD), jnp.float32)
     for k in range(kv_heads):
         acc = jnp.where(row_head == k, wide[:, k * HD : (k + 1) * HD], acc)
-    acc_ref[0] = acc
-    lane = lax.broadcasted_iota(jnp.int32, (rows, HD), 1)
-    stat_ref[0] = jnp.where(lane < HD // 2, peak, total)
-
-
-def far_attention(table, lengths, queries, prefix_keys, prefix_values, share, scale):
+    sources = out_ref.shape[0]
+    q_heads = out_ref.shape[1] - 1
+    out_ref[:, :q_heads, pl.ds(j, 1), :] = acc.reshape(sources, q_heads, 1, HD)
+    lane = lax.broadcasted_iota(jnp.int32, (sources, q_heads, HD), 2)
+    head = lax.broadcasted_iota(jnp.int32, (sources, q_heads, HD), 1)
+    peak3 = jnp.broadcast_to(peak, (rows, HD)).reshape(sources, q_heads, HD)
+    total3 = jnp.broadcast_to(total, (rows, HD)).reshape(sources, q_heads, HD)
+    stat = jnp.where(lane == head, peak3, 0.0) + jnp.where(lane == head + q_heads, total3, 0.0)
+    out_ref[:, q_heads:, pl.ds(j, 1), :] = jnp.sum(stat, axis=1).reshape(sources, 1, 1, HD)
+
+
+def far_attention(table, lengths, queries, prefix_keys, prefix_values, share, scale, sources):
     local_groups, pblk = table.shape
     assert pblk % 8 == 0
     _, rows, width = queries.shape
+    q_heads = rows // sources
+    assert 2 * q_heads <= HD
     block = prefix_keys.shape[1]
     tokens = pblk * block
     kernel = lambda *refs: far_kernel(*refs, share=share, scale=scale)
@@ -151,10 +159,9 @@
             pl.BlockSpec(memory_space=pl.ANY),
             pl.BlockSpec(memory_space=pl.ANY),
         ],
-        out_specs=[
-            pl.BlockSpec((1, rows, HD), lambda j, *_: (j, 0, 0)),
-            pl.BlockSpec((1, rows, HD), lambda j, *_: (j, 0, 0)),
-        ],
+        out_specs=pl.BlockSpec(
+            (sources, q_heads + 1, local_groups, HD), lambda j, *_: (0, 0, 0, 0)
+        ),
         scratch_shapes=[
             pltpu.VMEM((2, pblk, block, width), prefix_keys.dtype),
             pltpu.VMEM((2, pblk, block, width), prefix_values.dtype),
@@ -169,10 +176,7 @@
     return pl.pallas_call(
         kernel,
         grid_spec=grid_spec,
-        out_shape=[
-            jax.ShapeDtypeStruct((local_groups, rows, HD), jnp.float32),
-            jax.ShapeDtypeStruct((local_groups, rows, HD), jnp.float32),
-        ],
+        out_shape=jax.ShapeDtypeStruct((sources, q_heads + 1, local_groups, HD), jnp.float32),
         compiler_params=pltpu.CompilerParams(dimension_semantics=("arbitrary",)),
         cost_estimate=cost,
     )(table.reshape(-1), lengths, queries, prefix_keys, prefix_values)
@@ -230,22 +234,11 @@
         local_groups, groups * q_heads, width
     )
     my_lengths = lax.dynamic_slice_in_dim(prompt_len, first_group, local_groups)
-    held_acc, held_stat = far_attention(
-        block_table, my_lengths, far_queries, prefix_keys, prefix_values, share, score_scale
-    )
-    held_acc = jnp.transpose(held_acc.reshape(local_groups, groups, q_heads, HD), (1, 0, 2, 3))
-    held_peak = held_stat[:, :, 0]
-    held_total = held_stat[:, :, HD // 2]
-    stats = jnp.concatenate(
-        [
-            held_peak.reshape(local_groups, groups, q_heads),
-            held_total.reshape(local_groups, groups, q_heads),
-            jnp.zeros((local_groups, groups, HD - 2 * q_heads), jnp.float32),
-        ],
-        axis=-1,
-    )
-    stats = jnp.transpose(stats, (1, 0, 2))[:, :, None, :]
-    packed = jnp.concatenate([held_acc, stats], axis=2)
+    packed = far_attention(
+        block_table, my_lengths, far_queries, prefix_keys, prefix_values, share, score_scale,
+        groups,
+    )
+    packed = jnp.transpose(packed, (0, 2, 1, 3))
 
     near_queries = spread_lanes(rotated.reshape(requests, kv_heads, share, HD), kv_heads)
     own_count = suffix_keys.shape[1]

time: 115 us -> 110 us (0.957)
  local copies, waits for them, and re-layouts: 10.8 us -> 6.64 us
    slice x3 -> x0, local copies, waits for them, and re-layouts: 2.53 us -> none  [the longest x2 2.01 us: body(): held_peak = held_stat[:, :, 0]]
    reshape x1 -> x0, local copies, waits for them, and re-layouts: 1.42 us -> none  [body(): held_acc.reshape(local_groups, groups, q_heads, HD)]
where the time goes in v9:
time: 110 us; the launch traced here: 108 us
  blocking collectives  41.8 us (38%)
  Pallas kernels  20.7 us (19%)
  matrix products  18.9 us (17%)
  starting transfers between devices  8.75 us (8%)
  waiting for transfers between devices  7.61 us (7%)
  local copies, waits for them, and re-layouts  6.64 us (6%)
  other arithmetic  3.5 us (3%)
    all_to_all x1, blocking collectives, body(): lax.all_to_all(jnp.transpose(partial_out.reshape(requests, parts, -1), (1...  41.8 us
    pallas_call x1, Pallas kernels, far_attention(): pl.pallas_call(kernel, grid_spec=grid_spec, out_shape=jax.ShapeDtypeStruc...  20.7 us
    all_to_all x1, waiting for transfers between devices, body(): lax.all_to_all(packed, 'group', split_axis=0, concat_axis=0, tiled=True)  7.61 us
    dot_general x1, matrix products, body(): jnp.dot(attn, out_weight, preferred_element_type=jnp.float32)  4.97 us
    dot_general x1, matrix products, body(): jnp.dot(hidden, query_weight, preferred_element_type=jnp.float32)  4.87 us
    dot_general x1, matrix products, body(): jnp.einsum('rqc,rtc->rqt', near_queries, suffix_keys, preferred_element_t...  4.59 us
    all_to_all x1, starting transfers between devices, body(): lax.all_to_all(packed, 'group', split_axis=0, concat_axis=0, tiled=True)  4.5 us
    all_to_all x1, starting transfers between devices, body(): lax.all_to_all(outgoing.reshape(groups, local_groups, q_heads * HD), 'gro...  4.25 us
  transfers between devices with their start and end apart: 2, of which 1 were waited for; matrix products, arithmetic and copies ran while one was open for 11% of the time, Pallas kernels for 0%

profile of v9, /device:TPU:2, one launch (start us, length us, event | category | flops | bytes accessed | tf_op | source)
XLA Modules:
  0.0 108.3 jit_solution(17157420967458265048)
XLA Ops:
  0.0 1.1 %copy-done = bf16[96,4096]{1,0:T(8,128)(2,1)S(1)} copy-done((bf16[96,4096]{1,0:T(8,128)(2,1)S(1)}, bf16[96,4096]{1,0:T(8,128)(2,1)}, u32[]{:S(2)}) %copy-start) | copy-done | bytes 786456
  1.1 4.9 %convolution_bitcast_fusion = f32[12,8,8,128]{3,1,2,0:T(8,128)S(1)} fusion(bf16[96,4096]{1,0:T(8,128)(2,1)S(1)} %copy-done, bf16[4096,1024]{1,0:T(8,128)(2,1)} %param.12), kind=kOutput, calls=%fused_computation.4 | convolution fusion | flops 805306368 | bytes 9568256 | tf_op jit(solution)/shard_map/dot_general | solution.py:208
  7.1 0.8 reshape.207
  7.9 4.3 %all-to-all-start = ((bf16[8,18,1024]{2,1,0:T(8,128)(2,1)}), bf16[8,18,1024]{2,1,0:T(8,128)(2,1)S(1)}, u32[]{:S(2)}, u32[]{:S(2)}) async-start(bf16[8,18,1024]{2,1,0:T(8,128)(2,1)} %reshape.207), calls=%async_computation | async-start | bytes 786432 | tf_op jit(solution)/shard_map/all_to_all | solution.py:223
  12.4 0.3 pad_maximum_fusion.2
  12.6 0.3 mul.156
  13.2 4.6 %fusion.27 = (f32[96,8]{1,0:T(8,128)S(1)}, f32[96,8,128]{2,1,0:T(8,128)S(1)}) fusion(bf16[96,128,256]{2,1,0:T(8,128)(2,1)} %param.19, bf16[96,8,256]{2,1,0:T(8,128)(2,1)S(1)} %mul.157, bf16[8,256]{1,0:T(8,128)(2,1)S(1)} %bitcast.90, pred[96,128]{1,0:T(8,128)(4,1)S(1)} %iota_compare_fusion.3), kind=kOutput, calls=%fused_computation.54 | convolution fusion | flops 50822400 | bytes 7097344 | tf_op jit(solution)/shard_map/rqc,rtc->rqt/dot_general | solution.py:247
  17.8 0.7 dynamic_slice.3.refs_1_
  18.4 0.7 reshape.205.refs_0_
  19.3 0.3 fusion.8
  20.0 0.5 mul.150
  20.5 0.4 mul.151
  20.8 0.9 broadcast_multiply_fusion.refs_2_
  21.7 20.7 %shard_map.109 = f32[8,9,18,128]{3,2,1,0:T(8,128)} custom-call(s32[1152]{0:T(1024)} %reshape.205.refs_0_, s32[18]{0:T(128)} %dynamic_slice.3.refs_1_, bf16[18,64,256]{2,1,0:T(8,128)(2,1)} %broadcast_multiply_fusion.refs_2_, bf16[1152,16,256]{2,1,0:T(8,128)(2,1)} %refs_3_.1, bf16[1152,16,256]{2,1,0:T(8,128)(2,1)} %refs_4_.1), custom_call_target="tpu_custom_call" | custom-call | flops 1207959552 | bytes 20643840 | tf_op jit(solution)/shard_map/pallas_call | solution.py:176
  42.4 4.5 %all-to-all-start.1 = ((f32[8,18,9,128]{3,1,2,0:T(8,128)}), f32[8,18,9,128]{3,1,2,0:T(8,128)S(1)}, u32[]{:S(2)}, u32[]{:S(2)}) async-start(f32[8,18,9,128]{3,1,2,0:T(8,128)} %bitcast.82), calls=%async_computation.1 | async-start | bytes 1769472 | tf_op jit(solution)/shard_map/all_to_all | solution.py:252
  46.9 3.7 %fusion.28 = f32[96,8,256]{2,1,0:T(8,128)S(1)} fusion(bf16[96,8,128]{2,1,0:T(8,128)(2,1)S(1)} %get-tuple-element.8, bf16[96,128,256]{2,1,0:T(8,128)(2,1)} %param.20), kind=kOutput, calls=%fused_computation.55 | convolution fusion | flops 50331648 | bytes 7274496 | tf_op jit(solution)/shard_map/rqt,rtc->rqc/dot_general | solution.py:263
  50.6 0.4 reshape.210
  51.1 0.3 fusion.25
  51.5 7.6 %all-to-all-done.1 = f32[8,18,9,128]{3,1,2,0:T(8,128)S(1)} async-done(((f32[8,18,9,128]{3,1,2,0:T(8,128)}), f32[8,18,9,128]{3,1,2,0:T(8,128)S(1)}, u32[]{:S(2)}, u32[]{:S(2)}) %all-to-all-start.1) | async-done | bytes 663584 | tf_op jit(solution)/shard_map/all_to_all | solution.py:252
  59.3 0.6 fusion.1
  60.1 0.4 fusion.7
  60.5 5.0 %fusion.12 = f32[96,4096]{1,0:T(8,128)S(1)} fusion(bf16[1024,4096]{1,0:T(8,128)(2,1)} %param.13, bf16[96,8,128]{2,0,1:T(8,128)(2,1)S(1)} %fusion.7), kind=kOutput, calls=%fused_computation.24 | convolution fusion | flops 805306368 | bytes 10158080 | tf_op jit(solution)/shard_map/dot_general | solution.py:271
  65.6 41.8 %all_to_all.15 = f32[4,96,1024]{2,1,0:T(8,128)S(1)} all-to-all(f32[4,96,1024]{2,1,0:T(8,128)S(1)} %bitcast.80), channel_id=1, replica_groups=mesh['group'=8,'tensor'=4] {'tensor'}, dimensions={0} | all-to-all | bytes 3145728 | tf_op jit(solution)/shard_map/all_to_all | solution.py:273
  107.4 0.8 reduce_sum.29
  (39 shorter events, 2.5 us)
Async XLA Ops:
  0.0 1.1 %copy-start = (bf16[96,4096]{1,0:T(8,128)(2,1)S(1)}, bf16[96,4096]{1,0:T(8,128)(2,1)}, u32[]{:S(2)}) copy-start(bf16[96,4096]{1,0:T(8,128)(2,1)} %param.11) | copy-start | bytes 2359300
  1.1 5.0 %copy-start.3 = (s32[96]{0:T(128)S(1)}, s32[96]{0:T(128)}, u32[]{:S(2)}) copy-start(s32[96]{0:T(128)} %param.18) | copy-start | bytes 1156
  1.1 5.0 %copy-start.4 = (s32[144]{0:T(256)S(1)}, s32[144]{0:T(256)}, u32[]{:S(2)}) copy-start(s32[144]{0:T(256)} %param.17) | copy-start | bytes 1732
  1.1 5.1 %copy-start.5 = (s32[96]{0:T(128)S(1)}, s32[96]{0:T(128)}, u32[]{:S(2)}) copy-start(s32[96]{0:T(128)} %param.21) | copy-start | bytes 1156
  6.5 11.9 %copy-start.2 = (s32[18,64]{1,0:T(8,128)S(1)}, s32[18,64]{1,0:T(8,128)}, u32[]{:S(2)}) copy-start(s32[18,64]{1,0:T(8,128)} %param.16) | copy-start | bytes 13828
  7.9 11.7 %all-to-all-start = ((bf16[8,18,1024]{2,1,0:T(8,128)(2,1)}), bf16[8,18,1024]{2,1,0:T(8,128)(2,1)S(1)}, u32[]{:S(2)}, u32[]{:S(2)}) async-start(bf16[8,18,1024]{2,1,0:T(8,128)(2,1)} %reshape.207), calls=%async_computation | async-start | bytes 786432 | tf_op jit(solution)/shard_map/all_to_all | solution.py:223
  42.4 16.6 %all-to-all-start.1 = ((f32[8,18,9,128]{3,1,2,0:T(8,128)}), f32[8,18,9,128]{3,1,2,0:T(8,128)S(1)}, u32[]{:S(2)}, u32[]{:S(2)}) async-start(f32[8,18,9,128]{3,1,2,0:T(8,128)} %bitcast.82), calls=%async_computation.1 | async-start | bytes 1769472 | tf_op jit(solution)/shard_map/all_to_all | solution.py:252
  60.5 47.8 %copy-start.1 = (bf16[96,4096]{1,0:T(8,128)(2,1)S(1)}, bf16[96,4096]{1,0:T(8,128)(2,1)}, u32[]{:S(2)}) copy-start(bf16[96,4096]{1,0:T(8,128)(2,1)} %param.11) | copy-start | bytes 2359300

commit v10 on v9

--- a/solution.py
+++ b/solution.py
@@ -116,16 +116,26 @@
     queries = q_ref[0]
     scores = (
         lax.dot_general(
-            queries, keys, (((1,), (1,)), ((), ())), preferred_element_type=jnp.float32
+            keys, queries, (((1,), (1,)), ((), ())), preferred_element_type=jnp.float32
         )
         * scale
     )
-    valid = lax.broadcasted_iota(jnp.int32, scores.shape, 1) < len_ref[j]
+    valid = lax.broadcasted_iota(jnp.int32, scores.shape, 0) < len_ref[j]
     masked = jnp.where(valid, scores, masked_score)
-    peak = jnp.max(masked, axis=1, keepdims=True)
-    weights = jnp.where(valid, jnp.exp(masked - peak), 0.0)
-    total = jnp.sum(weights, axis=1, keepdims=True)
-    wide = jnp.dot(weights.astype(jnp.bfloat16), values, preferred_element_type=jnp.float32)
+    peak_row = jnp.max(masked, axis=0, keepdims=True)
+    weights = jnp.where(valid, jnp.exp(masked - peak_row), 0.0)
+    total_row = jnp.sum(weights, axis=0, keepdims=True)
+    wide = lax.dot_general(
+        weights.astype(jnp.bfloat16), values, (((0,), (0,)), ((), ())),
+        preferred_element_type=jnp.float32,
+    )
+    count = scores.shape[1]
+    eye = (
+        lax.broadcasted_iota(jnp.int32, (count, count), 0)
+        == lax.broadcasted_iota(jnp.int32, (count, count), 1)
+    )
+    peak = jnp.sum(jnp.where(eye, peak_row, 0.0), axis=1, keepdims=True)
+    total = jnp.sum(jnp.where(eye, total_row, 0.0), axis=1, keepdims=True)
     rows = wide.shape[0]
     row_head = (lax.broadcasted_iota(jnp.int32, (rows, HD), 0) // share) % kv_heads
     acc = jnp.zeros((rows, HD), jnp.float32)

time: 110 us -> 110 us (level)
  Pallas kernels: 20.7 us -> 22.3 us
    pallas_call x1, Pallas kernels: 20.7 us -> 22.3 us  [far_attention(): pl.pallas_call(kernel, grid_spec=grid_spec, out_shape=jax.ShapeDtypeStruc...]
where the time goes in v10:
time: 110 us; the launch traced here: 109 us
  blocking collectives  41.8 us (38%)
  Pallas kernels  22.3 us (20%)
  matrix products  18.9 us (17%)
  starting transfers between devices  8.22 us (7%)
  waiting for transfers between devices  7.62 us (7%)
  local copies, waits for them, and re-layouts  6.64 us (6%)
  other arithmetic  3.5 us (3%)
    all_to_all x1, blocking collectives, body(): lax.all_to_all(jnp.transpose(partial_out.reshape(requests, parts, -1), (1...  41.8 us
    pallas_call x1, Pallas kernels, far_attention(): pl.pallas_call(kernel, grid_spec=grid_spec, out_shape=jax.ShapeDtypeStruc...  22.3 us
    all_to_all x1, waiting for transfers between devices, body(): lax.all_to_all(packed, 'group', split_axis=0, concat_axis=0, tiled=True)  7.62 us
    dot_general x1, matrix products, body(): jnp.dot(attn, out_weight, preferred_element_type=jnp.float32)  4.97 us
    dot_general x1, matrix products, body(): jnp.dot(hidden, query_weight, preferred_element_type=jnp.float32)  4.87 us
    dot_general x1, matrix products, body(): jnp.einsum('rqc,rtc->rqt', near_queries, suffix_keys, preferred_element_t...  4.59 us
    all_to_all x1, starting transfers between devices, body(): lax.all_to_all(outgoing.reshape(groups, local_groups, q_heads * HD), 'gro...  4.25 us
    all_to_all x1, starting transfers between devices, body(): lax.all_to_all(packed, 'group', split_axis=0, concat_axis=0, tiled=True)  3.96 us
  transfers between devices with their start and end apart: 2, of which 1 were waited for; matrix products, arithmetic and copies ran while one was open for 11% of the time, Pallas kernels for 0%

profile of v10, /device:TPU:2, one launch (start us, length us, event | category | flops | bytes accessed | tf_op | source)
XLA Modules:
  0.0 109.3 jit_solution(11066094408969134523)
XLA Ops:
  0.0 1.1 %copy-done = bf16[96,4096]{1,0:T(8,128)(2,1)S(1)} copy-done((bf16[96,4096]{1,0:T(8,128)(2,1)S(1)}, bf16[96,4096]{1,0:T(8,128)(2,1)}, u32[]{:S(2)}) %copy-start) | copy-done | bytes 786456
  1.1 4.9 %convolution_bitcast_fusion = f32[12,8,8,128]{3,1,2,0:T(8,128)S(1)} fusion(bf16[96,4096]{1,0:T(8,128)(2,1)S(1)} %copy-done, bf16[4096,1024]{1,0:T(8,128)(2,1)} %param.12), kind=kOutput, calls=%fused_computation.4 | convolution fusion | flops 805306368 | bytes 9568256 | tf_op jit(solution)/shard_map/dot_general | solution.py:218
  7.1 0.8 reshape.207
  7.9 4.3 %all-to-all-start = ((bf16[8,18,1024]{2,1,0:T(8,128)(2,1)}), bf16[8,18,1024]{2,1,0:T(8,128)(2,1)S(1)}, u32[]{:S(2)}, u32[]{:S(2)}) async-start(bf16[8,18,1024]{2,1,0:T(8,128)(2,1)} %reshape.207), calls=%async_computation | async-start | bytes 786432 | tf_op jit(solution)/shard_map/all_to_all | solution.py:233
  12.4 0.3 pad_maximum_fusion.2
  12.6 0.3 mul.156
  13.2 4.6 %fusion.27 = (f32[96,8]{1,0:T(8,128)S(1)}, f32[96,8,128]{2,1,0:T(8,128)S(1)}) fusion(bf16[96,128,256]{2,1,0:T(8,128)(2,1)} %param.19, bf16[96,8,256]{2,1,0:T(8,128)(2,1)S(1)} %mul.157, bf16[8,256]{1,0:T(8,128)(2,1)S(1)} %bitcast.90, pred[96,128]{1,0:T(8,128)(4,1)S(1)} %iota_compare_fusion.3), kind=kOutput, calls=%fused_computation.54 | convolution fusion | flops 50822400 | bytes 7097344 | tf_op jit(solution)/shard_map/rqc,rtc->rqt/dot_general | solution.py:257
  17.8 0.7 dynamic_slice.3.refs_1_
  18.4 0.7 reshape.205.refs_0_
  19.3 0.3 fusion.8
  20.0 0.5 mul.150
  20.5 0.4 mul.151
  20.8 0.9 broadcast_multiply_fusion.refs_2_
  21.7 22.3 %shard_map.109 = f32[8,9,18,128]{3,2,1,0:T(8,128)} custom-call(s32[1152]{0:T(1024)} %reshape.205.refs_0_, s32[18]{0:T(128)} %dynamic_slice.3.refs_1_, bf16[18,64,256]{2,1,0:T(8,128)(2,1)} %broadcast_multiply_fusion.refs_2_, bf16[1152,16,256]{2,1,0:T(8,128)(2,1)} %refs_3_.1, bf16[1152,16,256]{2,1,0:T(8,128)(2,1)} %refs_4_.1), custom_call_target="tpu_custom_call" | custom-call | flops 1207959552 | bytes 20643840 | tf_op jit(solution)/shard_map/pallas_call | solution.py:186
  44.1 4.0 %all-to-all-start.1 = ((f32[8,18,9,128]{3,1,2,0:T(8,128)}), f32[8,18,9,128]{3,1,2,0:T(8,128)S(1)}, u32[]{:S(2)}, u32[]{:S(2)}) async-start(f32[8,18,9,128]{3,1,2,0:T(8,128)} %bitcast.82), calls=%async_computation.1 | async-start | bytes 1769472 | tf_op jit(solution)/shard_map/all_to_all | solution.py:262
  48.0 3.7 %fusion.28 = f32[96,8,256]{2,1,0:T(8,128)S(1)} fusion(bf16[96,8,128]{2,1,0:T(8,128)(2,1)S(1)} %get-tuple-element.8, bf16[96,128,256]{2,1,0:T(8,128)(2,1)} %param.20), kind=kOutput, calls=%fused_computation.55 | convolution fusion | flops 50331648 | bytes 7274496 | tf_op jit(solution)/shard_map/rqt,rtc->rqc/dot_general | solution.py:273
  51.7 0.4 reshape.210
  52.1 0.3 fusion.25
  52.6 7.6 %all-to-all-done.1 = f32[8,18,9,128]{3,1,2,0:T(8,128)S(1)} async-done(((f32[8,18,9,128]{3,1,2,0:T(8,128)}), f32[8,18,9,128]{3,1,2,0:T(8,128)S(1)}, u32[]{:S(2)}, u32[]{:S(2)}) %all-to-all-start.1) | async-done | bytes 663584 | tf_op jit(solution)/shard_map/all_to_all | solution.py:262
  60.4 0.6 fusion.1
  61.2 0.4 fusion.7
  61.6 5.0 %fusion.12 = f32[96,4096]{1,0:T(8,128)S(1)} fusion(bf16[1024,4096]{1,0:T(8,128)(2,1)} %param.13, bf16[96,8,128]{2,0,1:T(8,128)(2,1)S(1)} %fusion.7), kind=kOutput, calls=%fused_computation.24 | convolution fusion | flops 805306368 | bytes 10158080 | tf_op jit(solution)/shard_map/dot_general | solution.py:281
  66.7 41.8 %all_to_all.15 = f32[4,96,1024]{2,1,0:T(8,128)S(1)} all-to-all(f32[4,96,1024]{2,1,0:T(8,128)S(1)} %bitcast.80), channel_id=1, replica_groups=mesh['group'=8,'tensor'=4] {'tensor'}, dimensions={0} | all-to-all | bytes 3145728 | tf_op jit(solution)/shard_map/all_to_all | solution.py:283
  108.5 0.8 reduce_sum.29
  (39 shorter events, 2.5 us)
Async XLA Ops:
  0.0 1.1 %copy-start = (bf16[96,4096]{1,0:T(8,128)(2,1)S(1)}, bf16[96,4096]{1,0:T(8,128)(2,1)}, u32[]{:S(2)}) copy-start(bf16[96,4096]{1,0:T(8,128)(2,1)} %param.11) | copy-start | bytes 2359300
  1.1 5.0 %copy-start.3 = (s32[96]{0:T(128)S(1)}, s32[96]{0:T(128)}, u32[]{:S(2)}) copy-start(s32[96]{0:T(128)} %param.18) | copy-start | bytes 1156
  1.1 5.0 %copy-start.4 = (s32[144]{0:T(256)S(1)}, s32[144]{0:T(256)}, u32[]{:S(2)}) copy-start(s32[144]{0:T(256)} %param.17) | copy-start | bytes 1732
  1.1 5.1 %copy-start.5 = (s32[96]{0:T(128)S(1)}, s32[96]{0:T(128)}, u32[]{:S(2)}) copy-start(s32[96]{0:T(128)} %param.21) | copy-start | bytes 1156
  6.5 11.9 %copy-start.2 = (s32[18,64]{1,0:T(8,128)S(1)}, s32[18,64]{1,0:T(8,128)}, u32[]{:S(2)}) copy-start(s32[18,64]{1,0:T(8,128)} %param.16) | copy-start | bytes 13828
  7.9 11.7 %all-to-all-start = ((bf16[8,18,1024]{2,1,0:T(8,128)(2,1)}), bf16[8,18,1024]{2,1,0:T(8,128)(2,1)S(1)}, u32[]{:S(2)}, u32[]{:S(2)}) async-start(bf16[8,18,1024]{2,1,0:T(8,128)(2,1)} %reshape.207), calls=%async_computation | async-start | bytes 786432 | tf_op jit(solution)/shard_map/all_to_all | solution.py:233
  44.1 16.1 %all-to-all-start.1 = ((f32[8,18,9,128]{3,1,2,0:T(8,128)}), f32[8,18,9,128]{3,1,2,0:T(8,128)S(1)}, u32[]{:S(2)}, u32[]{:S(2)}) async-start(f32[8,18,9,128]{3,1,2,0:T(8,128)} %bitcast.82), calls=%async_computation.1 | async-start | bytes 1769472 | tf_op jit(solution)/shard_map/all_to_all | solution.py:262
  61.6 47.8 %copy-start.1 = (bf16[96,4096]{1,0:T(8,128)(2,1)S(1)}, bf16[96,4096]{1,0:T(8,128)(2,1)}, u32[]{:S(2)}) copy-start(bf16[96,4096]{1,0:T(8,128)(2,1)} %param.11) | copy-start | bytes 2359300

commit v11 on v9

--- a/solution.py
+++ b/solution.py
@@ -62,19 +62,16 @@
 def far_kernel(
     table_ref, len_ref, q_ref, k_hbm, v_hbm, out_ref, kbuf, vbuf, sems, *, share, scale
 ):
-    j = pl.program_id(0)
-    steps = pl.num_programs(0)
+    steps = q_ref.shape[0]
     pblk = kbuf.shape[1]
+    block = kbuf.shape[2]
     width = kbuf.shape[3]
     kv_heads = width // HD
-
-    block = kbuf.shape[2]
-
-    @pl.when(j == 0)
-    def _():
-        vbuf[...] = jnp.zeros_like(vbuf)
-
     chunk = 8
+    sources = out_ref.shape[0]
+    q_heads = out_ref.shape[1] - 1
+
+    vbuf[...] = jnp.zeros_like(vbuf)
 
     def used_chunks(group):
         return (len_ref[group] + block * chunk - 1) // (block * chunk)
@@ -90,56 +87,56 @@
 
         lax.fori_loop(0, used_chunks(group), one, 0)
 
-    @pl.when(j == 0)
-    def _():
-        fetch(0, 0)
-
-    slot = j % 2
-
-    @pl.when(j + 1 < steps)
-    def _():
-        fetch(j + 1, 1 - slot)
-
-    def settle(c, carry):
-        part = pl.ds(pl.multiple_of(c * chunk, chunk), chunk)
-        pltpu.make_async_copy(
-            k_hbm.at[pl.ds(0, chunk)], kbuf.at[slot, part], sems.at[0, slot, c]
-        ).wait()
-        pltpu.make_async_copy(
-            v_hbm.at[pl.ds(0, chunk)], vbuf.at[slot, part], sems.at[1, slot, c]
-        ).wait()
+    fetch(0, 0)
+
+    def group_step(j, carry):
+        slot = j % 2
+
+        @pl.when(j + 1 < steps)
+        def _():
+            fetch(j + 1, 1 - slot)
+
+        def settle(c, carry):
+            part = pl.ds(pl.multiple_of(c * chunk, chunk), chunk)
+            pltpu.make_async_copy(
+                k_hbm.at[pl.ds(0, chunk)], kbuf.at[slot, part], sems.at[0, slot, c]
+            ).wait()
+            pltpu.make_async_copy(
+                v_hbm.at[pl.ds(0, chunk)], vbuf.at[slot, part], sems.at[1, slot, c]
+            ).wait()
+            return carry
+
+        lax.fori_loop(0, used_chunks(j), settle, 0)
+        keys = kbuf[slot].reshape(-1, width)
+        values = vbuf[slot].reshape(-1, width)
+        queries = q_ref[j]
+        scores = (
+            lax.dot_general(
+                queries, keys, (((1,), (1,)), ((), ())), preferred_element_type=jnp.float32
+            )
+            * scale
+        )
+        valid = lax.broadcasted_iota(jnp.int32, scores.shape, 1) < len_ref[j]
+        masked = jnp.where(valid, scores, masked_score)
+        peak = jnp.max(masked, axis=1, keepdims=True)
+        weights = jnp.where(valid, jnp.exp(masked - peak), 0.0)
+        total = jnp.sum(weights, axis=1, keepdims=True)
+        wide = jnp.dot(weights.astype(jnp.bfloat16), values, preferred_element_type=jnp.float32)
+        rows = wide.shape[0]
+        row_head = (lax.broadcasted_iota(jnp.int32, (rows, HD), 0) // share) % kv_heads
+        acc = jnp.zeros((rows, HD), jnp.float32)
+        for k in range(kv_heads):
+            acc = jnp.where(row_head == k, wide[:, k * HD : (k + 1) * HD], acc)
+        out_ref[:, :q_heads, pl.ds(j, 1), :] = acc.reshape(sources, q_heads, 1, HD)
+        lane = lax.broadcasted_iota(jnp.int32, (sources, q_heads, HD), 2)
+        head = lax.broadcasted_iota(jnp.int32, (sources, q_heads, HD), 1)
+        peak3 = jnp.broadcast_to(peak, (rows, HD)).reshape(sources, q_heads, HD)
+        total3 = jnp.broadcast_to(total, (rows, HD)).reshape(sources, q_heads, HD)
+        stat = jnp.where(lane == head, peak3, 0.0) + jnp.where(lane == head + q_heads, total3, 0.0)
+        out_ref[:, q_heads:, pl.ds(j, 1), :] = jnp.sum(stat, axis=1).reshape(sources, 1, 1, HD)
         return carry
 
-    lax.fori_loop(0, used_chunks(j), settle, 0)
-    keys = kbuf[slot].reshape(-1, width)
-    values = vbuf[slot].reshape(-1, width)
-    queries = q_ref[0]
-    scores = (
-        lax.dot_general(
-            queries, keys, (((1,), (1,)), ((), ())), preferred_element_type=jnp.float32
-        )
-        * scale
-    )
-    valid = lax.broadcasted_iota(jnp.int32, scores.shape, 1) < len_ref[j]
-    masked = jnp.where(valid, scores, masked_score)
-    peak = jnp.max(masked, axis=1, keepdims=True)
-    weights = jnp.where(valid, jnp.exp(masked - peak), 0.0)
-    total = jnp.sum(weights, axis=1, keepdims=True)
-    wide = jnp.dot(weights.astype(jnp.bfloat16), values, preferred_element_type=jnp.float32)
-    rows = wide.shape[0]
-    row_head = (lax.broadcasted_iota(jnp.int32, (rows, HD), 0) // share) % kv_heads
-    acc = jnp.zeros((rows, HD), jnp.float32)
-    for k in range(kv_heads):
-        acc = jnp.where(row_head == k, wide[:, k * HD : (k + 1) * HD], acc)
-    sources = out_ref.shape[0]
-    q_heads = out_ref.shape[1] - 1
-    out_ref[:, :q_heads, pl.ds(j, 1), :] = acc.reshape(sources, q_heads, 1, HD)
-    lane = lax.broadcasted_iota(jnp.int32, (sources, q_heads, HD), 2)
-    head = lax.broadcasted_iota(jnp.int32, (sources, q_heads, HD), 1)
-    peak3 = jnp.broadcast_to(peak, (rows, HD)).reshape(sources, q_heads, HD)
-    total3 = jnp.broadcast_to(total, (rows, HD)).reshape(sources, q_heads, HD)
-    stat = jnp.where(lane == head, peak3, 0.0) + jnp.where(lane == head + q_heads, total3, 0.0)
-    out_ref[:, q_heads:, pl.ds(j, 1), :] = jnp.sum(stat, axis=1).reshape(sources, 1, 1, HD)
+    lax.fori_loop(0, steps, group_step, 0)
 
 
 def far_attention(table, lengths, queries, prefix_keys, prefix_values, share, scale, sources):
@@ -153,9 +150,9 @@
     kernel = lambda *refs: far_kernel(*refs, share=share, scale=scale)
     grid_spec = pltpu.PrefetchScalarGridSpec(
         num_scalar_prefetch=2,
-        grid=(local_groups,),
+        grid=(1,),
         in_specs=[
-            pl.BlockSpec((1, rows, width), lambda j, *_: (j, 0, 0)),
+            pl.BlockSpec((local_groups, rows, width), lambda j, *_: (0, 0, 0)),
             pl.BlockSpec(memory_space=pl.ANY),
             pl.BlockSpec(memory_space=pl.ANY),
         ],

time: 110 us -> 109 us (level); the launches traced: 108 us -> 108 us
  no operation moved by 1% of the time
where the time goes in v11:
time: 109 us; the launch traced here: 108 us
  blocking collectives  41.9 us (38%)
  Pallas kernels  21 us (19%)
  matrix products  18.9 us (17%)
  starting transfers between devices  8.64 us (8%)
  waiting for transfers between devices  7.61 us (7%)
  local copies, waits for them, and re-layouts  6.64 us (6%)
  other arithmetic  3.5 us (3%)
    all_to_all x1, blocking collectives, body(): lax.all_to_all(jnp.transpose(partial_out.reshape(requests, parts, -1), (1...  41.9 us
    pallas_call x1, Pallas kernels, far_attention(): pl.pallas_call(kernel, grid_spec=grid_spec, out_shape=jax.ShapeDtypeStruc...  21 us
    all_to_all x1, waiting for transfers between devices, body(): lax.all_to_all(packed, 'group', split_axis=0, concat_axis=0, tiled=True)  7.61 us
    dot_general x1, matrix products, body(): jnp.dot(attn, out_weight, preferred_element_type=jnp.float32)  4.96 us
    dot_general x1, matrix products, body(): jnp.dot(hidden, query_weight, preferred_element_type=jnp.float32)  4.87 us
    dot_general x1, matrix products, body(): jnp.einsum('rqc,rtc->rqt', near_queries, suffix_keys, preferred_element_t...  4.59 us
    all_to_all x1, starting transfers between devices, body(): lax.all_to_all(packed, 'group', split_axis=0, concat_axis=0, tiled=True)  4.39 us
    all_to_all x1, starting transfers between devices, body(): lax.all_to_all(outgoing.reshape(groups, local_groups, q_heads * HD), 'gro...  4.25 us
  transfers between devices with their start and end apart: 2, of which 1 were waited for; matrix products, arithmetic and copies ran while one was open for 11% of the time, Pallas kernels for 0%

profile of v11, /device:TPU:2, one launch (start us, length us, event | category | flops | bytes accessed | tf_op | source)
XLA Modules:
  0.0 108.4 jit_solution(15385584121809466193)
XLA Ops:
  0.0 1.1 %copy-done = bf16[96,4096]{1,0:T(8,128)(2,1)S(1)} copy-done((bf16[96,4096]{1,0:T(8,128)(2,1)S(1)}, bf16[96,4096]{1,0:T(8,128)(2,1)}, u32[]{:S(2)}) %copy-start) | copy-done | bytes 786456
  1.1 4.9 %convolution_bitcast_fusion = f32[12,8,8,128]{3,1,2,0:T(8,128)S(1)} fusion(bf16[96,4096]{1,0:T(8,128)(2,1)S(1)} %copy-done, bf16[4096,1024]{1,0:T(8,128)(2,1)} %param.12), kind=kOutput, calls=%fused_computation.4 | convolution fusion | flops 805306368 | bytes 9568256 | tf_op jit(solution)/shard_map/dot_general | solution.py:205
  7.1 0.8 reshape.207
  7.9 4.3 %all-to-all-start = ((bf16[8,18,1024]{2,1,0:T(8,128)(2,1)}), bf16[8,18,1024]{2,1,0:T(8,128)(2,1)S(1)}, u32[]{:S(2)}, u32[]{:S(2)}) async-start(bf16[8,18,1024]{2,1,0:T(8,128)(2,1)} %reshape.207), calls=%async_computation | async-start | bytes 786432 | tf_op jit(solution)/shard_map/all_to_all | solution.py:220
  12.4 0.3 pad_maximum_fusion.2
  12.6 0.3 mul.156
  13.2 4.6 %fusion.27 = (f32[96,8]{1,0:T(8,128)S(1)}, f32[96,8,128]{2,1,0:T(8,128)S(1)}) fusion(bf16[96,128,256]{2,1,0:T(8,128)(2,1)} %param.19, bf16[96,8,256]{2,1,0:T(8,128)(2,1)S(1)} %mul.157, bf16[8,256]{1,0:T(8,128)(2,1)S(1)} %bitcast.90, pred[96,128]{1,0:T(8,128)(4,1)S(1)} %iota_compare_fusion.3), kind=kOutput, calls=%fused_computation.54 | convolution fusion | flops 50822400 | bytes 7097344 | tf_op jit(solution)/shard_map/rqc,rtc->rqt/dot_general | solution.py:244
  17.8 0.7 dynamic_slice.3.refs_1_
  18.4 0.7 reshape.205.refs_0_
  19.3 0.3 fusion.8
  20.0 0.5 mul.150
  20.5 0.4 mul.151
  20.8 0.9 broadcast_multiply_fusion.refs_2_
  21.7 21.0 %shard_map.109 = f32[8,9,18,128]{3,2,1,0:T(8,128)} custom-call(s32[1152]{0:T(1024)} %reshape.205.refs_0_, s32[18]{0:T(128)} %dynamic_slice.3.refs_1_, bf16[18,64,256]{2,1,0:T(8,128)(2,1)} %broadcast_multiply_fusion.refs_2_, bf16[1152,16,256]{2,1,0:T(8,128)(2,1)} %refs_3_.1, bf16[1152,16,256]{2,1,0:T(8,128)(2,1)} %refs_4_.1), custom_call_target="tpu_custom_call" | custom-call | flops 1207959552 | bytes 20643840 | tf_op jit(solution)/shard_map/pallas_call | solution.py:173
  42.7 4.4 %all-to-all-start.1 = ((f32[8,18,9,128]{3,1,2,0:T(8,128)}), f32[8,18,9,128]{3,1,2,0:T(8,128)S(1)}, u32[]{:S(2)}, u32[]{:S(2)}) async-start(f32[8,18,9,128]{3,1,2,0:T(8,128)} %bitcast.82), calls=%async_computation.1 | async-start | bytes 1769472 | tf_op jit(solution)/shard_map/all_to_all | solution.py:249
  47.1 3.7 %fusion.28 = f32[96,8,256]{2,1,0:T(8,128)S(1)} fusion(bf16[96,8,128]{2,1,0:T(8,128)(2,1)S(1)} %get-tuple-element.8, bf16[96,128,256]{2,1,0:T(8,128)(2,1)} %param.20), kind=kOutput, calls=%fused_computation.55 | convolution fusion | flops 50331648 | bytes 7274496 | tf_op jit(solution)/shard_map/rqt,rtc->rqc/dot_general | solution.py:260
  50.8 0.4 reshape.210
  51.2 0.3 fusion.25
  51.6 7.6 %all-to-all-done.1 = f32[8,18,9,128]{3,1,2,0:T(8,128)S(1)} async-done(((f32[8,18,9,128]{3,1,2,0:T(8,128)}), f32[8,18,9,128]{3,1,2,0:T(8,128)S(1)}, u32[]{:S(2)}, u32[]{:S(2)}) %all-to-all-start.1) | async-done | bytes 663584 | tf_op jit(solution)/shard_map/all_to_all | solution.py:249
  59.4 0.6 fusion.1
  60.2 0.4 fusion.7
  60.6 5.0 %fusion.12 = f32[96,4096]{1,0:T(8,128)S(1)} fusion(bf16[1024,4096]{1,0:T(8,128)(2,1)} %param.13, bf16[96,8,128]{2,0,1:T(8,128)(2,1)S(1)} %fusion.7), kind=kOutput, calls=%fused_computation.24 | convolution fusion | flops 805306368 | bytes 10158080 | tf_op jit(solution)/shard_map/dot_general | solution.py:268
  65.7 41.9 %all_to_all.15 = f32[4,96,1024]{2,1,0:T(8,128)S(1)} all-to-all(f32[4,96,1024]{2,1,0:T(8,128)S(1)} %bitcast.80), channel_id=1, replica_groups=mesh['group'=8,'tensor'=4] {'tensor'}, dimensions={0} | all-to-all | bytes 3145728 | tf_op jit(solution)/shard_map/all_to_all | solution.py:270
  107.6 0.8 reduce_sum.29
  (39 shorter events, 2.5 us)
Async XLA Ops:
  0.0 1.1 %copy-start = (bf16[96,4096]{1,0:T(8,128)(2,1)S(1)}, bf16[96,4096]{1,0:T(8,128)(2,1)}, u32[]{:S(2)}) copy-start(bf16[96,4096]{1,0:T(8,128)(2,1)} %param.11) | copy-start | bytes 2359300
  1.1 5.0 %copy-start.3 = (s32[96]{0:T(128)S(1)}, s32[96]{0:T(128)}, u32[]{:S(2)}) copy-start(s32[96]{0:T(128)} %param.18) | copy-start | bytes 1156
  1.1 5.0 %copy-start.4 = (s32[144]{0:T(256)S(1)}, s32[144]{0:T(256)}, u32[]{:S(2)}) copy-start(s32[144]{0:T(256)} %param.17) | copy-start | bytes 1732
  1.1 5.1 %copy-start.5 = (s32[96]{0:T(128)S(1)}, s32[96]{0:T(128)}, u32[]{:S(2)}) copy-start(s32[96]{0:T(128)} %param.21) | copy-start | bytes 1156
  6.5 11.9 %copy-start.2 = (s32[18,64]{1,0:T(8,128)S(1)}, s32[18,64]{1,0:T(8,128)}, u32[]{:S(2)}) copy-start(s32[18,64]{1,0:T(8,128)} %param.16) | copy-start | bytes 13828
  7.9 11.7 %all-to-all-start = ((bf16[8,18,1024]{2,1,0:T(8,128)(2,1)}), bf16[8,18,1024]{2,1,0:T(8,128)(2,1)S(1)}, u32[]{:S(2)}, u32[]{:S(2)}) async-start(bf16[8,18,1024]{2,1,0:T(8,128)(2,1)} %reshape.207), calls=%async_computation | async-start | bytes 786432 | tf_op jit(solution)/shard_map/all_to_all | solution.py:220
  42.7 16.5 %all-to-all-start.1 = ((f32[8,18,9,128]{3,1,2,0:T(8,128)}), f32[8,18,9,128]{3,1,2,0:T(8,128)S(1)}, u32[]{:S(2)}, u32[]{:S(2)}) async-start(f32[8,18,9,128]{3,1,2,0:T(8,128)} %bitcast.82), calls=%async_computation.1 | async-start | bytes 1769472 | tf_op jit(solution)/shard_map/all_to_all | solution.py:249
  60.6 47.8 %copy-start.1 = (bf16[96,4096]{1,0:T(8,128)(2,1)S(1)}, bf16[96,4096]{1,0:T(8,128)(2,1)}, u32[]{:S(2)}) copy-start(bf16[96,4096]{1,0:T(8,128)(2,1)} %param.11) | copy-start | bytes 2359300

commit v12 on v11

--- a/solution.py
+++ b/solution.py
@@ -109,7 +109,13 @@
         lax.fori_loop(0, used_chunks(j), settle, 0)
         keys = kbuf[slot].reshape(-1, width)
         values = vbuf[slot].reshape(-1, width)
-        queries = q_ref[j]
+        compact = q_ref[j]
+        rows = compact.shape[0]
+        row_head = (lax.broadcasted_iota(jnp.int32, (rows, HD), 0) // share) % kv_heads
+        queries = jnp.concatenate(
+            [jnp.where(row_head == k, compact, jnp.zeros_like(compact)) for k in range(kv_heads)],
+            axis=1,
+        )
         scores = (
             lax.dot_general(
                 queries, keys, (((1,), (1,)), ((), ())), preferred_element_type=jnp.float32
@@ -122,8 +128,6 @@
         weights = jnp.where(valid, jnp.exp(masked - peak), 0.0)
         total = jnp.sum(weights, axis=1, keepdims=True)
         wide = jnp.dot(weights.astype(jnp.bfloat16), values, preferred_element_type=jnp.float32)
-        rows = wide.shape[0]
-        row_head = (lax.broadcasted_iota(jnp.int32, (rows, HD), 0) // share) % kv_heads
         acc = jnp.zeros((rows, HD), jnp.float32)
         for k in range(kv_heads):
             acc = jnp.where(row_head == k, wide[:, k * HD : (k + 1) * HD], acc)
@@ -142,7 +146,8 @@
 def far_attention(table, lengths, queries, prefix_keys, prefix_values, share, scale, sources):
     local_groups, pblk = table.shape
     assert pblk % 8 == 0
-    _, rows, width = queries.shape
+    _, rows, _ = queries.shape
+    width = prefix_keys.shape[2]
     q_heads = rows // sources
     assert 2 * q_heads <= HD
     block = prefix_keys.shape[1]
@@ -152,7 +157,7 @@
         num_scalar_prefetch=2,
         grid=(1,),
         in_specs=[
-            pl.BlockSpec((local_groups, rows, width), lambda j, *_: (0, 0, 0)),
+            pl.BlockSpec((local_groups, rows, HD), lambda j, *_: (0, 0, 0)),
             pl.BlockSpec(memory_space=pl.ANY),
             pl.BlockSpec(memory_space=pl.ANY),
         ],
@@ -227,9 +232,7 @@
     far_queries = jnp.transpose(
         arrived.reshape(groups, local_groups, kv_heads, share, HD), (1, 0, 2, 3, 4)
     )
-    far_queries = spread_lanes(far_queries, kv_heads).reshape(
-        local_groups, groups * q_heads, width
-    )
+    far_queries = far_queries.reshape(local_groups, groups * q_heads, HD)
     my_lengths = lax.dynamic_slice_in_dim(prompt_len, first_group, local_groups)
     packed = far_attention(
         block_table, my_lengths, far_queries, prefix_keys, prefix_values, share, score_scale,

time: 109 us -> 108 us (level)
  starting transfers between devices: 8.64 us -> 9.85 us
    all_to_all x1, starting transfers between devices: 4.39 us -> 5.6 us  [body(): lax.all_to_all(packed, 'group', split_axis=0, concat_axis=0, tiled=True)]
where the time goes in v12:
time: 108 us; the launch traced here: 107 us
  blocking collectives  41.9 us (39%)
  Pallas kernels  20 us (19%)
  matrix products  18.8 us (17%)
  starting transfers between devices  9.85 us (9%)
  waiting for transfers between devices  7.62 us (7%)
  local copies, waits for them, and re-layouts  6.31 us (6%)
  other arithmetic  2.63 us (2%)
    all_to_all x1, blocking collectives, body(): lax.all_to_all(jnp.transpose(partial_out.reshape(requests, parts, -1), (1...  41.9 us
    pallas_call x1, Pallas kernels, far_attention(): pl.pallas_call(kernel, grid_spec=grid_spec, out_shape=jax.ShapeDtypeStruc...  20 us
    all_to_all x1, waiting for transfers between devices, body(): lax.all_to_all(packed, 'group', split_axis=0, concat_axis=0, tiled=True)  7.62 us
    all_to_all x1, starting transfers between devices, body(): lax.all_to_all(packed, 'group', split_axis=0, concat_axis=0, tiled=True)  5.6 us
    dot_general x1, matrix products, body(): jnp.dot(hidden, query_weight, preferred_element_type=jnp.float32)  4.87 us
    dot_general x1, matrix products, body(): jnp.dot(attn, out_weight, preferred_element_type=jnp.float32)  4.83 us
    dot_general x1, matrix products, body(): jnp.einsum('rqc,rtc->rqt', near_queries, suffix_keys, preferred_element_t...  4.59 us
    all_to_all x1, starting transfers between devices, body(): lax.all_to_all(outgoing.reshape(groups, local_groups, q_heads * HD), 'gro...  4.25 us
  transfers between devices with their start and end apart: 2, of which 1 were waited for; matrix products, arithmetic and copies ran while one was open for 11% of the time, Pallas kernels for 0%

profile of v12, /device:TPU:2, one launch (start us, length us, event | category | flops | bytes accessed | tf_op | source)
XLA Modules:
  0.0 107.2 jit_solution(18173741180193153704)
XLA Ops:
  0.0 1.1 %copy-done = bf16[96,4096]{1,0:T(8,128)(2,1)S(1)} copy-done((bf16[96,4096]{1,0:T(8,128)(2,1)S(1)}, bf16[96,4096]{1,0:T(8,128)(2,1)}, u32[]{:S(2)}) %copy-start) | copy-done | bytes 786456
  1.1 4.9 %convolution_bitcast_fusion = f32[12,8,8,128]{3,1,2,0:T(8,128)S(1)} fusion(bf16[96,4096]{1,0:T(8,128)(2,1)S(1)} %copy-done, bf16[4096,1024]{1,0:T(8,128)(2,1)} %param.12), kind=kOutput, calls=%fused_computation.4 | convolution fusion | flops 805306368 | bytes 9568256 | tf_op jit(solution)/shard_map/dot_general | solution.py:210
  6.2 0.2 multiply_cosine_fusion
  7.1 0.8 reshape.192
  7.9 4.3 %all-to-all-start = ((bf16[8,18,1024]{2,1,0:T(8,128)(2,1)}), bf16[8,18,1024]{2,1,0:T(8,128)(2,1)S(1)}, u32[]{:S(2)}, u32[]{:S(2)}) async-start(bf16[8,18,1024]{2,1,0:T(8,128)(2,1)} %reshape.192), calls=%async_computation | async-start | bytes 786432 | tf_op jit(solution)/shard_map/all_to_all | solution.py:225
  12.3 0.3 pad_maximum_fusion.2
  12.6 0.3 mul.130
  12.9 0.3 mul.131
  13.2 4.6 %fusion.27 = (f32[96,8]{1,0:T(8,128)S(1)}, f32[96,8,128]{2,1,0:T(8,128)S(1)}) fusion(bf16[96,128,256]{2,1,0:T(8,128)(2,1)} %param.19, bf16[96,8,256]{2,1,0:T(8,128)(2,1)S(1)} %mul.131, bf16[8,256]{1,0:T(8,128)(2,1)S(1)} %bitcast.85, pred[96,128]{1,0:T(8,128)(4,1)S(1)} %iota_compare_fusion.3), kind=kOutput, calls=%fused_computation.52 | convolution fusion | flops 50822400 | bytes 7097344 | tf_op jit(solution)/shard_map/rqc,rtc->rqt/dot_general | solution.py:247
  17.8 0.6 dynamic_slice.3.refs_1_
  18.3 0.7 reshape.190.refs_0_
  19.1 0.3 fusion.8
  19.6 0.9 copy.71
  20.5 20.0 %shard_map.109 = f32[8,9,18,128]{3,2,1,0:T(8,128)} custom-call(s32[1152]{0:T(1024)} %reshape.190.refs_0_, s32[18]{0:T(128)} %dynamic_slice.3.refs_1_, bf16[18,64,128]{2,1,0:T(8,128)(2,1)} %bitcast.83, bf16[1152,16,256]{2,1,0:T(8,128)(2,1)} %refs_3_.1, bf16[1152,16,256]{2,1,0:T(8,128)(2,1)} %refs_4_.1), custom_call_target="tpu_custom_call" | custom-call | flops 1207959552 | bytes 20643840 | tf_op jit(solution)/shard_map/pallas_call | solution.py:178
  40.4 5.6 %all-to-all-start.1 = ((f32[8,18,9,128]{3,1,2,0:T(8,128)}), f32[8,18,9,128]{3,1,2,0:T(8,128)S(1)}, u32[]{:S(2)}, u32[]{:S(2)}) async-start(f32[8,18,9,128]{3,1,2,0:T(8,128)} %bitcast.78), calls=%async_computation.1 | async-start | bytes 1769472 | tf_op jit(solution)/shard_map/all_to_all | solution.py:252
  46.0 3.7 %fusion.28 = f32[96,8,256]{2,1,0:T(8,128)S(1)} fusion(bf16[96,8,128]{2,1,0:T(8,128)(2,1)S(1)} %get-tuple-element.8, bf16[96,128,256]{2,1,0:T(8,128)(2,1)} %param.20), kind=kOutput, calls=%fused_computation.53 | convolution fusion | flops 50331648 | bytes 7274496 | tf_op jit(solution)/shard_map/rqt,rtc->rqc/dot_general | solution.py:263
  49.7 0.4 reshape.196
  50.2 0.3 fusion.25
  50.6 7.6 %all-to-all-done.1 = f32[8,18,9,128]{3,1,2,0:T(8,128)S(1)} async-done(((f32[8,18,9,128]{3,1,2,0:T(8,128)}), f32[8,18,9,128]{3,1,2,0:T(8,128)S(1)}, u32[]{:S(2)}, u32[]{:S(2)}) %all-to-all-start.1) | async-done | bytes 663584 | tf_op jit(solution)/shard_map/all_to_all | solution.py:252
  58.4 0.6 fusion.1
  59.2 0.4 fusion.7
  59.6 4.8 %fusion.12 = f32[96,4096]{1,0:T(8,128)S(1)} fusion(bf16[1024,4096]{1,0:T(8,128)(2,1)} %param.13, bf16[96,8,128]{2,0,1:T(8,128)(2,1)S(1)} %fusion.7), kind=kOutput, calls=%fused_computation.23 | convolution fusion | flops 805306368 | bytes 10158080 | tf_op jit(solution)/shard_map/dot_general | solution.py:271
  64.5 41.9 %all_to_all.15 = f32[4,96,1024]{2,1,0:T(8,128)S(1)} all-to-all(f32[4,96,1024]{2,1,0:T(8,128)S(1)} %bitcast.76), channel_id=1, replica_groups=mesh['group'=8,'tensor'=4] {'tensor'}, dimensions={0} | all-to-all | bytes 3145728 | tf_op jit(solution)/shard_map/all_to_all | solution.py:273
  106.4 0.8 reduce_sum.29
  (32 shorter events, 1.8 us)
Async XLA Ops:
  0.0 1.1 %copy-start = (bf16[96,4096]{1,0:T(8,128)(2,1)S(1)}, bf16[96,4096]{1,0:T(8,128)(2,1)}, u32[]{:S(2)}) copy-start(bf16[96,4096]{1,0:T(8,128)(2,1)} %param.11) | copy-start | bytes 2359300
  1.1 5.0 %copy-start.2 = (s32[96]{0:T(128)S(1)}, s32[96]{0:T(128)}, u32[]{:S(2)}) copy-start(s32[96]{0:T(128)} %param.18) | copy-start | bytes 1156
  1.1 5.0 %copy-start.3 = (s32[144]{0:T(256)S(1)}, s32[144]{0:T(256)}, u32[]{:S(2)}) copy-start(s32[144]{0:T(256)} %param.17) | copy-start | bytes 1732
  1.1 5.1 %copy-start.4 = (s32[96]{0:T(128)S(1)}, s32[96]{0:T(128)}, u32[]{:S(2)}) copy-start(s32[96]{0:T(128)} %param.21) | copy-start | bytes 1156
  6.5 11.9 %copy-start.1 = (s32[18,64]{1,0:T(8,128)S(1)}, s32[18,64]{1,0:T(8,128)}, u32[]{:S(2)}) copy-start(s32[18,64]{1,0:T(8,128)} %param.16) | copy-start | bytes 13828
  7.9 11.5 %all-to-all-start = ((bf16[8,18,1024]{2,1,0:T(8,128)(2,1)}), bf16[8,18,1024]{2,1,0:T(8,128)(2,1)S(1)}, u32[]{:S(2)}, u32[]{:S(2)}) async-start(bf16[8,18,1024]{2,1,0:T(8,128)(2,1)} %reshape.192), calls=%async_computation | async-start | bytes 786432 | tf_op jit(solution)/shard_map/all_to_all | solution.py:225
  40.4 17.8 %all-to-all-start.1 = ((f32[8,18,9,128]{3,1,2,0:T(8,128)}), f32[8,18,9,128]{3,1,2,0:T(8,128)S(1)}, u32[]{:S(2)}, u32[]{:S(2)}) async-start(f32[8,18,9,128]{3,1,2,0:T(8,128)} %bitcast.78), calls=%async_computation.1 | async-start | bytes 1769472 | tf_op jit(solution)/shard_map/all_to_all | solution.py:252

commit v13 on v12

--- a/solution.py
+++ b/solution.py
@@ -109,13 +109,15 @@
         lax.fori_loop(0, used_chunks(j), settle, 0)
         keys = kbuf[slot].reshape(-1, width)
         values = vbuf[slot].reshape(-1, width)
-        compact = q_ref[j]
+        arrived = q_ref[j].astype(jnp.float32)
+        compact = jnp.concatenate(
+            [arrived[:, h * HD : (h + 1) * HD] for h in range(q_heads)], axis=0
+        )
         rows = compact.shape[0]
-        row_head = (lax.broadcasted_iota(jnp.int32, (rows, HD), 0) // share) % kv_heads
+        row_head = (lax.broadcasted_iota(jnp.int32, (rows, HD), 0) // (sources * share)) % kv_heads
         queries = jnp.concatenate(
-            [jnp.where(row_head == k, compact, jnp.zeros_like(compact)) for k in range(kv_heads)],
-            axis=1,
-        )
+            [jnp.where(row_head == k, compact, 0.0) for k in range(kv_heads)], axis=1
+        ).astype(jnp.bfloat16)
         scores = (
             lax.dot_general(
                 queries, keys, (((1,), (1,)), ((), ())), preferred_element_type=jnp.float32
@@ -131,13 +133,16 @@
         acc = jnp.zeros((rows, HD), jnp.float32)
         for k in range(kv_heads):
             acc = jnp.where(row_head == k, wide[:, k * HD : (k + 1) * HD], acc)
-        out_ref[:, :q_heads, pl.ds(j, 1), :] = acc.reshape(sources, q_heads, 1, HD)
-        lane = lax.broadcasted_iota(jnp.int32, (sources, q_heads, HD), 2)
-        head = lax.broadcasted_iota(jnp.int32, (sources, q_heads, HD), 1)
-        peak3 = jnp.broadcast_to(peak, (rows, HD)).reshape(sources, q_heads, HD)
-        total3 = jnp.broadcast_to(total, (rows, HD)).reshape(sources, q_heads, HD)
+        for h in range(q_heads):
+            out_ref[:, h : h + 1, pl.ds(j, 1), :] = acc[h * sources : (h + 1) * sources].reshape(
+                sources, 1, 1, HD
+            )
+        lane = lax.broadcasted_iota(jnp.int32, (q_heads, sources, HD), 2)
+        head = lax.broadcasted_iota(jnp.int32, (q_heads, sources, HD), 0)
+        peak3 = jnp.broadcast_to(peak, (rows, HD)).reshape(q_heads, sources, HD)
+        total3 = jnp.broadcast_to(total, (rows, HD)).reshape(q_heads, sources, HD)
         stat = jnp.where(lane == head, peak3, 0.0) + jnp.where(lane == head + q_heads, total3, 0.0)
-        out_ref[:, q_heads:, pl.ds(j, 1), :] = jnp.sum(stat, axis=1).reshape(sources, 1, 1, HD)
+        out_ref[:, q_heads:, pl.ds(j, 1), :] = jnp.sum(stat, axis=0).reshape(sources, 1, 1, HD)
         return carry
 
     lax.fori_loop(0, steps, group_step, 0)
@@ -146,9 +151,10 @@
 def far_attention(table, lengths, queries, prefix_keys, prefix_values, share, scale, sources):
     local_groups, pblk = table.shape
     assert pblk % 8 == 0
-    _, rows, _ = queries.shape
+    _, _, wide_q = queries.shape
+    q_heads = wide_q // HD
+    rows = sources * q_heads
     width = prefix_keys.shape[2]
-    q_heads = rows // sources
     assert 2 * q_heads <= HD
     block = prefix_keys.shape[1]
     tokens = pblk * block
@@ -157,7 +163,7 @@
         num_scalar_prefetch=2,
         grid=(1,),
         in_specs=[
-            pl.BlockSpec((local_groups, rows, HD), lambda j, *_: (0, 0, 0)),
+            pl.BlockSpec((local_groups, sources, wide_q), lambda j, *_: (0, 0, 0)),
             pl.BlockSpec(memory_space=pl.ANY),
             pl.BlockSpec(memory_space=pl.ANY),
         ],
@@ -223,16 +229,13 @@
         picks, rotated.reshape(requests, q_heads * HD), preferred_element_type=jnp.float32
     ).astype(jnp.bfloat16)
     arrived = lax.all_to_all(
-        outgoing.reshape(groups, local_groups, q_heads * HD),
+        outgoing.reshape(groups, local_groups, 1, q_heads * HD),
         "group",
         split_axis=0,
-        concat_axis=0,
+        concat_axis=2,
         tiled=True,
     )
-    far_queries = jnp.transpose(
-        arrived.reshape(groups, local_groups, kv_heads, share, HD), (1, 0, 2, 3, 4)
-    )
-    far_queries = far_queries.reshape(local_groups, groups * q_heads, HD)
+    far_queries = arrived.reshape(local_groups, groups, q_heads * HD)
     my_lengths = lax.dynamic_slice_in_dim(prompt_len, first_group, local_groups)
     packed = far_attention(
         block_table, my_lengths, far_queries, prefix_keys, prefix_values, share, score_scale,

time: 108 us -> 108 us (level)
  no operation moved by 1% of the time
where the time goes in v13:
time: 108 us; the launch traced here: 107 us
  blocking collectives  41.9 us (39%)
  Pallas kernels  20.2 us (19%)
  matrix products  18.8 us (17%)
  starting transfers between devices  9.57 us (9%)
  waiting for transfers between devices  7.62 us (7%)
  local copies, waits for them, and re-layouts  6.18 us (6%)
  other arithmetic  2.63 us (2%)
    all_to_all x1, blocking collectives, body(): lax.all_to_all(jnp.transpose(partial_out.reshape(requests, parts, -1), (1...  41.9 us
    pallas_call x1, Pallas kernels, far_attention(): pl.pallas_call(kernel, grid_spec=grid_spec, out_shape=jax.ShapeDtypeStruc...  20.2 us
    all_to_all x1, waiting for transfers between devices, body(): lax.all_to_all(packed, 'group', split_axis=0, concat_axis=0, tiled=True)  7.62 us
    all_to_all x1, starting transfers between devices, body(): lax.all_to_all(packed, 'group', split_axis=0, concat_axis=0, tiled=True)  5.31 us
    dot_general x1, matrix products, body(): jnp.dot(hidden, query_weight, preferred_element_type=jnp.float32)  4.87 us
    dot_general x1, matrix products, body(): jnp.dot(attn, out_weight, preferred_element_type=jnp.float32)  4.83 us
    dot_general x1, matrix products, body(): jnp.einsum('rqc,rtc->rqt', near_queries, suffix_keys, preferred_element_t...  4.59 us
    all_to_all x1, starting transfers between devices, body(): lax.all_to_all(outgoing.reshape(groups, local_groups, 1, q_heads * HD), '...  4.25 us
  transfers between devices with their start and end apart: 2, of which 1 were waited for; matrix products, arithmetic and copies ran while one was open for 11% of the time, Pallas kernels for 0%

profile of v13, /device:TPU:2, one launch (start us, length us, event | category | flops | bytes accessed | tf_op | source)
XLA Modules:
  0.0 107.1 jit_solution(9720200391290952913)
XLA Ops:
  0.0 1.1 %copy-done = bf16[96,4096]{1,0:T(8,128)(2,1)S(1)} copy-done((bf16[96,4096]{1,0:T(8,128)(2,1)S(1)}, bf16[96,4096]{1,0:T(8,128)(2,1)}, u32[]{:S(2)}) %copy-start) | copy-done | bytes 786456
  1.1 4.9 %convolution_bitcast_fusion = f32[12,8,8,128]{3,1,2,0:T(8,128)S(1)} fusion(bf16[96,4096]{1,0:T(8,128)(2,1)S(1)} %copy-done, bf16[4096,1024]{1,0:T(8,128)(2,1)} %param.12), kind=kOutput, calls=%fused_computation.4 | convolution fusion | flops 805306368 | bytes 9568256 | tf_op jit(solution)/shard_map/dot_general | solution.py:216
  6.2 0.2 multiply_cosine_fusion
  7.1 0.8 reshape.190
  7.9 4.3 %all-to-all-start = ((bf16[8,18,1,1024]{3,1,2,0:T(8,128)(2,1)}), bf16[8,18,1,1024]{3,1,2,0:T(8,128)(2,1)S(1)}, u32[]{:S(2)}, u32[]{:S(2)}) async-start(bf16[8,18,1,1024]{3,1,2,0:T(8,128)(2,1)} %bitcast.1), calls=%async_computation | async-start | bytes 786432 | tf_op jit(solution)/shard_map/all_to_all | solution.py:231
  12.3 0.3 pad_maximum_fusion.2
  12.6 0.3 mul.130
  12.9 0.3 mul.131
  13.2 4.6 %fusion.27 = (f32[96,8]{1,0:T(8,128)S(1)}, f32[96,8,128]{2,1,0:T(8,128)S(1)}) fusion(bf16[96,128,256]{2,1,0:T(8,128)(2,1)} %param.19, bf16[96,8,256]{2,1,0:T(8,128)(2,1)S(1)} %mul.131, bf16[8,256]{1,0:T(8,128)(2,1)S(1)} %bitcast.88, pred[96,128]{1,0:T(8,128)(4,1)S(1)} %iota_compare_fusion.3), kind=kOutput, calls=%fused_computation.53 | convolution fusion | flops 50822400 | bytes 7097344 | tf_op jit(solution)/shard_map/rqc,rtc->rqt/dot_general | solution.py:250
  17.8 0.6 dynamic_slice.3.refs_1_
  18.3 0.7 reshape.188.refs_0_
  19.1 0.3 fusion.8
  19.4 0.9 copy.104
  20.3 20.2 %shard_map.109 = f32[8,9,18,128]{3,2,1,0:T(8,128)} custom-call(s32[1152]{0:T(1024)} %reshape.188.refs_0_, s32[18]{0:T(128)} %dynamic_slice.3.refs_1_, bf16[18,8,1024]{2,1,0:T(8,128)(2,1)} %bitcast.86, bf16[1152,16,256]{2,1,0:T(8,128)(2,1)} %refs_3_.1, bf16[1152,16,256]{2,1,0:T(8,128)(2,1)} %refs_4_.1), custom_call_target="tpu_custom_call" | custom-call | flops 1207959552 | bytes 20643840 | tf_op jit(solution)/shard_map/pallas_call | solution.py:184
  40.6 5.3 %all-to-all-start.1 = ((f32[8,18,9,128]{3,1,2,0:T(8,128)}), f32[8,18,9,128]{3,1,2,0:T(8,128)S(1)}, u32[]{:S(2)}, u32[]{:S(2)}) async-start(f32[8,18,9,128]{3,1,2,0:T(8,128)} %bitcast.82), calls=%async_computation.1 | async-start | bytes 1769472 | tf_op jit(solution)/shard_map/all_to_all | solution.py:255
  45.9 3.7 %fusion.28 = f32[96,8,256]{2,1,0:T(8,128)S(1)} fusion(bf16[96,8,128]{2,1,0:T(8,128)(2,1)S(1)} %get-tuple-element.8, bf16[96,128,256]{2,1,0:T(8,128)(2,1)} %param.20), kind=kOutput, calls=%fused_computation.54 | convolution fusion | flops 50331648 | bytes 7274496 | tf_op jit(solution)/shard_map/rqt,rtc->rqc/dot_general | solution.py:266
  49.6 0.4 reshape.193
  50.0 0.3 fusion.25
  50.4 7.6 %all-to-all-done.1 = f32[8,18,9,128]{3,1,2,0:T(8,128)S(1)} async-done(((f32[8,18,9,128]{3,1,2,0:T(8,128)}), f32[8,18,9,128]{3,1,2,0:T(8,128)S(1)}, u32[]{:S(2)}, u32[]{:S(2)}) %all-to-all-start.1) | async-done | bytes 663584 | tf_op jit(solution)/shard_map/all_to_all | solution.py:255
  58.2 0.6 fusion.1
  59.1 0.4 fusion.7
  59.5 4.8 %fusion.12 = f32[96,4096]{1,0:T(8,128)S(1)} fusion(bf16[1024,4096]{1,0:T(8,128)(2,1)} %param.13, bf16[96,8,128]{2,0,1:T(8,128)(2,1)S(1)} %fusion.7), kind=kOutput, calls=%fused_computation.24 | convolution fusion | flops 805306368 | bytes 10158080 | tf_op jit(solution)/shard_map/dot_general | solution.py:274
  64.4 41.9 %all_to_all.25 = f32[4,96,1024]{2,1,0:T(8,128)S(1)} all-to-all(f32[4,96,1024]{2,1,0:T(8,128)S(1)} %bitcast.80), channel_id=1, replica_groups=mesh['group'=8,'tensor'=4] {'tensor'}, dimensions={0} | all-to-all | bytes 3145728 | tf_op jit(solution)/shard_map/all_to_all | solution.py:276
  106.3 0.8 reduce_sum.29
  (31 shorter events, 1.6 us)
Async XLA Ops:
  0.0 1.1 %copy-start = (bf16[96,4096]{1,0:T(8,128)(2,1)S(1)}, bf16[96,4096]{1,0:T(8,128)(2,1)}, u32[]{:S(2)}) copy-start(bf16[96,4096]{1,0:T(8,128)(2,1)} %param.11) | copy-start | bytes 2359300
  1.1 5.0 %copy-start.2 = (s32[96]{0:T(128)S(1)}, s32[96]{0:T(128)}, u32[]{:S(2)}) copy-start(s32[96]{0:T(128)} %param.18) | copy-start | bytes 1156
  1.1 5.0 %copy-start.3 = (s32[144]{0:T(256)S(1)}, s32[144]{0:T(256)}, u32[]{:S(2)}) copy-start(s32[144]{0:T(256)} %param.17) | copy-start | bytes 1732
  1.1 5.1 %copy-start.4 = (s32[96]{0:T(128)S(1)}, s32[96]{0:T(128)}, u32[]{:S(2)}) copy-start(s32[96]{0:T(128)} %param.21) | copy-start | bytes 1156
  6.5 11.9 %copy-start.1 = (s32[18,64]{1,0:T(8,128)S(1)}, s32[18,64]{1,0:T(8,128)}, u32[]{:S(2)}) copy-start(s32[18,64]{1,0:T(8,128)} %param.16) | copy-start | bytes 13828
  7.9 11.5 %all-to-all-start = ((bf16[8,18,1,1024]{3,1,2,0:T(8,128)(2,1)}), bf16[8,18,1,1024]{3,1,2,0:T(8,128)(2,1)S(1)}, u32[]{:S(2)}, u32[]{:S(2)}) async-start(bf16[8,18,1,1024]{3,1,2,0:T(8,128)(2,1)} %bitcast.1), calls=%async_computation | async-start | bytes 786432 | tf_op jit(solution)/shard_map/all_to_all | solution.py:231
  40.6 17.5 %all-to-all-start.1 = ((f32[8,18,9,128]{3,1,2,0:T(8,128)}), f32[8,18,9,128]{3,1,2,0:T(8,128)S(1)}, u32[]{:S(2)}, u32[]{:S(2)}) async-start(f32[8,18,9,128]{3,1,2,0:T(8,128)} %bitcast.82), calls=%async_computation.1 | async-start | bytes 1769472 | tf_op jit(solution)/shard_map/all_to_all | solution.py:255

commit v14 on v13

--- a/solution.py
+++ b/solution.py
@@ -225,8 +225,11 @@
 
     slots = jnp.arange(groups * local_groups, dtype=jnp.int32)
     picks = (slots[:, None] == prompt_group[None, :]).astype(jnp.bfloat16)
-    outgoing = jnp.dot(
-        picks, rotated.reshape(requests, q_heads * HD), preferred_element_type=jnp.float32
+    outgoing = jnp.einsum(
+        "glr,rf->glf",
+        picks.reshape(groups, local_groups, requests),
+        rotated.reshape(requests, q_heads * HD),
+        preferred_element_type=jnp.float32,
     ).astype(jnp.bfloat16)
     arrived = lax.all_to_all(
         outgoing.reshape(groups, local_groups, 1, q_heads * HD),

time: 108 us -> 108 us (level)
  no operation moved by 1% of the time
where the time goes in v14:
time: 108 us; the launch traced here: 107 us
  blocking collectives  41.9 us (39%)
  Pallas kernels  19.7 us (18%)
  matrix products  19.6 us (18%)
  starting transfers between devices  9.78 us (9%)
  waiting for transfers between devices  7.62 us (7%)
  local copies, waits for them, and re-layouts  5.43 us (5%)
  other arithmetic  2.63 us (2%)
    all_to_all x1, blocking collectives, body(): lax.all_to_all(jnp.transpose(partial_out.reshape(requests, parts, -1), (1...  41.9 us
    pallas_call x1, Pallas kernels, far_attention(): pl.pallas_call(kernel, grid_spec=grid_spec, out_shape=jax.ShapeDtypeStruc...  19.7 us
    all_to_all x1, waiting for transfers between devices, body(): lax.all_to_all(packed, 'group', split_axis=0, concat_axis=0, tiled=True)  7.62 us
    all_to_all x1, starting transfers between devices, body(): lax.all_to_all(packed, 'group', split_axis=0, concat_axis=0, tiled=True)  5.53 us
    dot_general x1, matrix products, body(): jnp.dot(hidden, query_weight, preferred_element_type=jnp.float32)  4.87 us
    dot_general x1, matrix products, body(): jnp.dot(attn, out_weight, preferred_element_type=jnp.float32)  4.83 us
    dot_general x1, matrix products, body(): jnp.einsum('rqc,rtc->rqt', near_queries, suffix_keys, preferred_element_t...  4.59 us
    all_to_all x1, starting transfers between devices, body(): lax.all_to_all(outgoing.reshape(groups, local_groups, 1, q_heads * HD), '...  4.25 us
  transfers between devices with their start and end apart: 2, of which 1 were waited for; matrix products, arithmetic and copies ran while one was open for 11% of the time, Pallas kernels for 0%

profile of v14, /device:TPU:2, one launch (start us, length us, event | category | flops | bytes accessed | tf_op | source)
XLA Modules:
  0.0 106.9 jit_solution(16771652944033664258)
XLA Ops:
  0.0 1.1 %copy-done = bf16[96,4096]{1,0:T(8,128)(2,1)S(1)} copy-done((bf16[96,4096]{1,0:T(8,128)(2,1)S(1)}, bf16[96,4096]{1,0:T(8,128)(2,1)}, u32[]{:S(2)}) %copy-start) | copy-done | bytes 786456
  1.1 4.9 %convolution_bitcast_fusion = f32[12,8,8,128]{3,1,2,0:T(8,128)S(1)} fusion(bf16[96,4096]{1,0:T(8,128)(2,1)S(1)} %copy-done, bf16[4096,1024]{1,0:T(8,128)(2,1)} %param.12), kind=kOutput, calls=%fused_computation.5 | convolution fusion | flops 805306368 | bytes 9568256 | tf_op jit(solution)/shard_map/dot_general | solution.py:216
  6.2 0.2 multiply_cosine_fusion
  7.0 1.0 fusion
  8.0 4.3 %all-to-all-start = ((bf16[8,18,1,1024]{3,1,2,0:T(8,128)(2,1)}), bf16[8,18,1,1024]{3,1,2,0:T(8,128)(2,1)S(1)}, u32[]{:S(2)}, u32[]{:S(2)}) async-start(bf16[8,18,1,1024]{3,1,2,0:T(8,128)(2,1)} %fusion), calls=%async_computation | async-start | bytes 786432 | tf_op jit(solution)/shard_map/all_to_all | solution.py:234
  12.4 0.3 pad_maximum_fusion.2
  12.7 0.3 mul.130
  13.0 0.3 mul.131
  13.2 4.6 %fusion.28 = (f32[96,8]{1,0:T(8,128)S(1)}, f32[96,8,128]{2,1,0:T(8,128)S(1)}) fusion(bf16[96,128,256]{2,1,0:T(8,128)(2,1)} %param.19, bf16[96,8,256]{2,1,0:T(8,128)(2,1)S(1)} %mul.131, bf16[8,256]{1,0:T(8,128)(2,1)S(1)} %bitcast.87, pred[96,128]{1,0:T(8,128)(4,1)S(1)} %iota_compare_fusion.2), kind=kOutput, calls=%fused_computation.55 | convolution fusion | flops 50822400 | bytes 7097344 | tf_op jit(solution)/shard_map/rqc,rtc->rqt/dot_general | solution.py:253
  17.8 0.6 dynamic_slice.3.refs_1_
  18.4 0.7 reshape.207.refs_0_
  19.1 0.3 fusion.9
  19.5 0.9 copy.100
  20.4 19.7 %shard_map.109 = f32[8,9,18,128]{3,2,1,0:T(8,128)} custom-call(s32[1152]{0:T(1024)} %reshape.207.refs_0_, s32[18]{0:T(128)} %dynamic_slice.3.refs_1_, bf16[18,8,1024]{2,1,0:T(8,128)(2,1)} %bitcast.86, bf16[1152,16,256]{2,1,0:T(8,128)(2,1)} %refs_3_.1, bf16[1152,16,256]{2,1,0:T(8,128)(2,1)} %refs_4_.1), custom_call_target="tpu_custom_call" | custom-call | flops 1207959552 | bytes 20643840 | tf_op jit(solution)/shard_map/pallas_call | solution.py:184
  40.1 5.5 %all-to-all-start.1 = ((f32[8,18,9,128]{3,1,2,0:T(8,128)}), f32[8,18,9,128]{3,1,2,0:T(8,128)S(1)}, u32[]{:S(2)}, u32[]{:S(2)}) async-start(f32[8,18,9,128]{3,1,2,0:T(8,128)} %bitcast.82), calls=%async_computation.1 | async-start | bytes 1769472 | tf_op jit(solution)/shard_map/all_to_all | solution.py:258
  45.7 3.7 %fusion.29 = f32[96,8,256]{2,1,0:T(8,128)S(1)} fusion(bf16[96,8,128]{2,1,0:T(8,128)(2,1)S(1)} %get-tuple-element.8, bf16[96,128,256]{2,1,0:T(8,128)(2,1)} %param.20), kind=kOutput, calls=%fused_computation.56 | convolution fusion | flops 50331648 | bytes 7274496 | tf_op jit(solution)/shard_map/rqt,rtc->rqc/dot_general | solution.py:269
  49.4 0.4 reshape.212
  49.8 0.3 fusion.26
  50.2 7.6 %all-to-all-done.1 = f32[8,18,9,128]{3,1,2,0:T(8,128)S(1)} async-done(((f32[8,18,9,128]{3,1,2,0:T(8,128)}), f32[8,18,9,128]{3,1,2,0:T(8,128)S(1)}, u32[]{:S(2)}, u32[]{:S(2)}) %all-to-all-start.1) | async-done | bytes 663584 | tf_op jit(solution)/shard_map/all_to_all | solution.py:258
  58.0 0.6 fusion.2
  58.8 0.4 fusion.8
  59.2 4.8 %fusion.11 = f32[96,4096]{1,0:T(8,128)S(1)} fusion(bf16[1024,4096]{1,0:T(8,128)(2,1)} %param.13, bf16[96,8,128]{2,0,1:T(8,128)(2,1)S(1)} %fusion.8), kind=kOutput, calls=%fused_computation.23 | convolution fusion | flops 805306368 | bytes 10158080 | tf_op jit(solution)/shard_map/dot_general | solution.py:277
  64.2 41.9 %all_to_all.25 = f32[4,96,1024]{2,1,0:T(8,128)S(1)} all-to-all(f32[4,96,1024]{2,1,0:T(8,128)S(1)} %bitcast.80), channel_id=1, replica_groups=mesh['group'=8,'tensor'=4] {'tensor'}, dimensions={0} | all-to-all | bytes 3145728 | tf_op jit(solution)/shard_map/all_to_all | solution.py:279
  106.0 0.8 reduce_sum.29
  (32 shorter events, 1.5 us)
Async XLA Ops:
  0.0 1.1 %copy-start = (bf16[96,4096]{1,0:T(8,128)(2,1)S(1)}, bf16[96,4096]{1,0:T(8,128)(2,1)}, u32[]{:S(2)}) copy-start(bf16[96,4096]{1,0:T(8,128)(2,1)} %param.11) | copy-start | bytes 2359300
  1.1 5.0 %copy-start.2 = (s32[96]{0:T(128)S(1)}, s32[96]{0:T(128)}, u32[]{:S(2)}) copy-start(s32[96]{0:T(128)} %param.18) | copy-start | bytes 1156
  1.1 5.0 %copy-start.3 = (s32[144]{0:T(256)S(1)}, s32[144]{0:T(256)}, u32[]{:S(2)}) copy-start(s32[144]{0:T(256)} %param.17) | copy-start | bytes 1732
  1.1 5.1 %copy-start.4 = (s32[96]{0:T(128)S(1)}, s32[96]{0:T(128)}, u32[]{:S(2)}) copy-start(s32[96]{0:T(128)} %param.21) | copy-start | bytes 1156
  6.5 11.9 %copy-start.1 = (s32[18,64]{1,0:T(8,128)S(1)}, s32[18,64]{1,0:T(8,128)}, u32[]{:S(2)}) copy-start(s32[18,64]{1,0:T(8,128)} %param.16) | copy-start | bytes 13828
  8.0 11.5 %all-to-all-start = ((bf16[8,18,1,1024]{3,1,2,0:T(8,128)(2,1)}), bf16[8,18,1,1024]{3,1,2,0:T(8,128)(2,1)S(1)}, u32[]{:S(2)}, u32[]{:S(2)}) async-start(bf16[8,18,1,1024]{3,1,2,0:T(8,128)(2,1)} %fusion), calls=%async_computation | async-start | bytes 786432 | tf_op jit(solution)/shard_map/all_to_all | solution.py:234
  40.1 17.7 %all-to-all-start.1 = ((f32[8,18,9,128]{3,1,2,0:T(8,128)}), f32[8,18,9,128]{3,1,2,0:T(8,128)S(1)}, u32[]{:S(2)}, u32[]{:S(2)}) async-start(f32[8,18,9,128]{3,1,2,0:T(8,128)} %bitcast.82), calls=%async_computation.1 | async-start | bytes 1769472 | tf_op jit(solution)/shard_map/all_to_all | solution.py:258
